TPU v7x, 256 devices: a whole 4x4x8 slice. The times are simulated.
256 devices in a mesh: seq: 16 (over x_lo, y, core), tensor: 16 (over z, x_hi).
Axes of the slice: x: 4 (x_hi: 2, x_lo: 2; x = x_hi * 2 + x_lo), y: 4, z: 8, core: 2. Of those that a mesh axis runs over, the one named last changes fastest.
Arguments:
- tokens: bfloat16 [4096, 8192], P('tensor', 'seq'), may hold values from -6 to 6
- in_weight: bfloat16 [3, 8192, 8192], P(None, 'seq', 'tensor'), may hold values from -0.0625 to 0.0625
- filters: float32 [512, 128], P('tensor'), may hold values from -0.5 to 0.5
- skip_gain: float32 [8192], P('tensor'), may hold values from -4 to 4
- out_weight: bfloat16 [8192, 8192], P('tensor', 'seq'), may hold values from -0.0625 to 0.0625
Outputs:
- mixed: bfloat16 [4096, 8192], P('seq', 'tensor')
All inputs are finite; a program needn't handle non-finite values.
Results may differ from a plain program's by a relative error of at most 0.035.
Values may be sent and summed in bfloat16 or wider, within the bound.
No kernel may reach another device: no remote copies, remote signals or barrier semaphores. Data moves between devices by JAX's collectives and lax.ppermute only.
A program may use at most 128 MiB of HBM per device.

v0:
```python
import jax
import jax.numpy as jnp
from jax import lax
from jax.sharding import PartitionSpec as P


def from_behind(x, axis, by):
    peers = lax.axis_size(axis)
    pairs = [(i, i + by) for i in range(peers) if 0 <= i + by < peers]
    return lax.ppermute(x, axis, pairs)


def toeplitz_conv(ext, filters):
    groups, taps = filters.shape
    rows, channels = ext.shape
    tok = rows - (taps - 1)
    gw = channels // groups
    nblk = tok // taps
    extp = jnp.concatenate([ext, jnp.zeros((1, channels), ext.dtype)], axis=0)
    blocks = extp.reshape(nblk + 1, taps, groups, gw)
    win = jnp.concatenate([blocks[:-1], blocks[1:]], axis=1)
    w = jnp.pad(filters[:, ::-1], ((0, 0), (0, taps + 1)))
    toe = jnp.tile(w, (1, taps))[:, : taps * 2 * taps].reshape(groups, taps, 2 * taps)
    hi = toe.astype(jnp.bfloat16)
    lo = (toe - hi.astype(jnp.float32)).astype(jnp.bfloat16)
    out = jnp.einsum("gts,isgc->itgc", hi, win, preferred_element_type=jnp.float32)
    out = out + jnp.einsum("gts,isgc->itgc", lo, win, preferred_element_type=jnp.float32)
    return out.reshape(tok, channels)


def per_device(tokens, in_weight, filters, skip_gain, out_weight):
    gathered = lax.all_gather(tokens, "tensor", axis=0, tiled=True)
    tok_dev = gathered.shape[0] // lax.axis_size("seq")
    channels = in_weight.shape[2]
    taps_count = filters.shape[1]
    group_width = channels // filters.shape[0]
    summed = lax.psum_scatter(
        jnp.einsum("rf,sfc->rsc", gathered, in_weight, preferred_element_type=jnp.float32).astype(
            jnp.bfloat16
        ),
        "seq",
        scatter_dimension=0,
        tiled=True,
    ).astype(jnp.float32)
    query_rows = summed[:, 0].astype(jnp.bfloat16)
    key_rows = summed[:, 1].astype(jnp.bfloat16)
    value_rows = summed[:, 2].astype(jnp.bfloat16)
    product = (key_rows.astype(jnp.float32) * value_rows.astype(jnp.float32)).astype(jnp.bfloat16)
    previous = from_behind(product[tok_dev - (taps_count - 1) :], "seq", 1)
    product_f = product.astype(jnp.float32)
    extended = jnp.concatenate([previous, product], axis=0)
    conv = toeplitz_conv(extended, filters)
    conv = conv + skip_gain[None, :] * product_f
    gated = (query_rows.astype(jnp.float32) * conv).astype(jnp.bfloat16)
    partial_out = jnp.dot(
        gated,
        lax.all_gather(out_weight, "seq", axis=1, tiled=True),
        preferred_element_type=jnp.float32,
    )
    return lax.psum_scatter(
        partial_out.astype(jnp.bfloat16), "tensor", scatter_dimension=1, tiled=True
    )


def solution(mesh):
    placed = (
        P("tensor", "seq"),
        P(None, "seq", "tensor"),
        P("tensor", None),
        P("tensor"),
        P("tensor", "seq"),
    )
    return jax.shard_map(
        per_device, mesh=mesh, in_specs=placed, out_specs=P("seq", "tensor"), check_vma=False
    )
```

profile of v0, /device:TPU:1, one launch (start us, length us, event | category | flops | bytes accessed | tf_op | source)
XLA Modules:
  0.0 486.3 jit_solution(14399103536930337372)
XLA Ops:
  6.5 0.0 copy-start
  6.5 0.0 all-gather.3.cloned.1.call-start
  6.5 0.7 all-gather.3.cloned.1.call-update
  7.3 0.0 reduce-scatter.3.cloned.1.call-start
  7.3 103.2 %all-gather.3.cloned.1.call-done = bf16[4096,512]{1,0:T(8,128)(2,1)} async-done(((bf16[256,512]{1,0:T(8,128)(2,1)}), bf16[4096,512]{1,0:T(8,128)(2,1)}) %all-gather.3.cloned.1.call-update) | async-done | bytes 4194320 | tf_op jit(solution)/shard_map/all_gather | solution.py:32
  110.5 0.0 copy-done
  110.5 11.8 %convolution_convert_fusion.1 = bf16[4096,3,512]{2,0,1:T(8,128)(2,1)} fusion(bf16[3,512,512]{2,1,0:T(8,128)(2,1)S(1)} %copy-done, bf16[4096,512]{1,0:T(8,128)(2,1)} %all-gather.3.cloned.1.call-done), kind=kOutput, calls=%fused_computation.1 | convolution fusion | flops 6448742400 | bytes 18350080 | tf_op jit(solution)/shard_map/rf,sfc->rsc/dot_general | solution.py:38
  122.3 0.0 copy-start.2
  122.3 0.0 reduce-scatter.3.cloned.1.call-update
  122.4 0.0 all-gather.5.cloned.1.call-start
  122.4 0.7 all-gather.5.cloned.1.call-update
  123.1 0.0 reduce-scatter.5.cloned.1.call-start
  123.2 0.0 copy-done.2
  123.2 0.1 rev.3
  123.2 3.1 tile.4
  126.3 6.6 %tile.10 = f32[32,32896]{1,0:T(8,128)} reshape(f32[32,128,257]{2,1,0:T(8,128)} %tile.4) | data formatting | bytes 8421376 | tf_op jit(solution)/shard_map/tile | solution.py:23
  132.9 0.0 slice-start
  132.9 2.7 slice-done
  135.7 1.3 copy.17
  137.0 3.1 fusion
  140.0 64.0 %reduce-scatter.3.cloned.1.call-done = bf16[256,3,512]{2,0,1:T(8,128)(2,1)} async-done(((bf16[4096,3,512]{2,0,1:T(8,128)(2,1)}), bf16[256,3,512]{2,0,1:T(8,128)(2,1)}) %reduce-scatter.3.cloned.1.call-update) | async-done | bytes 786448 | tf_op jit(solution)/shard_map/reduce_scatter | solution.py:37
  204.1 1.1 multiply_convert_fusion
  205.2 2.1 collective-permute-start
  207.3 1.1 fusion.20
  208.4 2.8 collective-permute-done
  211.2 0.1 pad_slice_fusion
  211.3 0.1 copy.9
  211.4 0.1 slice.41
  211.5 0.1 copy.10
  211.7 0.1 slice.43
  211.7 0.0 copy-start.1
  211.7 0.1 copy_dynamic-update-slice_fusion.1
  211.8 0.1 copy_dynamic-update-slice_fusion
  211.9 2.5 fusion.2
  214.4 0.0 copy-start.3
  214.4 0.0 copy-done.1
  214.4 0.8 fusion.9
  215.2 0.3 copy.13
  215.6 0.2 copy.14
  215.8 47.4 %all-gather.5.cloned.1.call-done = bf16[512,8192]{1,0:T(8,128)(2,1)} async-done(((bf16[512,512]{1,0:T(8,128)(2,1)}), bf16[512,8192]{1,0:T(8,128)(2,1)}) %all-gather.5.cloned.1.call-update) | async-done | bytes 8388624 | tf_op jit(solution)/shard_map/all_gather | solution.py:57
  263.2 0.0 copy-done.3
  263.2 7.8 %convolution_convert_fusion = bf16[256,8192]{1,0:T(8,128)(2,1)} fusion(bf16[512,8192]{1,0:T(8,128)(2,1)} %all-gather.5.cloned.1.call-done, f32[256,512]{1,0:T(8,128)S(1)} %copy.14, bf16[256,3,512]{2,0,1:T(8,128)(2,1)} %reduce-scatter.3.cloned.1.call-done, f32[512]{0:T(512)S(1)} %copy-done.3, bf16[256,1,512]{2,0,1:T(8,128)(2,1)S(1)} %multiply_convert_fusion), kind=kOutput, calls=%fused_computation | convolution fusion | flops 2150367232 | bytes 13633536 | tf_op jit(solution)/shard_map/dot_general | solution.py:55
  271.0 0.0 reduce-scatter.5.cloned.1.call-update
  271.0 208.8 %reduce-scatter.5.cloned.1.call-done = bf16[256,512]{1,0:T(8,128)(2,1)} async-done(((bf16[256,8192]{1,0:T(8,128)(2,1)}), bf16[256,512]{1,0:T(8,128)(2,1)}) %reduce-scatter.5.cloned.1.call-update) | async-done | bytes 262160 | tf_op jit(solution)/shard_map/reduce_scatter | solution.py:60
  (3 shorter events, 0.1 us)
Async XLA Ops:
  6.5 104.0 %copy-start = (bf16[3,512,512]{2,1,0:T(8,128)(2,1)S(1)}, bf16[3,512,512]{2,1,0:T(8,128)(2,1)}, u32[]{:S(2)}) copy-start(bf16[3,512,512]{2,1,0:T(8,128)(2,1)} %param.6) | copy-start | bytes 4718596
  6.5 104.0 %all-gather.3.cloned.1.call-start = ((), (), s32[]{:S(2)}) async-start(), calls=%async_computation.2 | async-start | bytes 4456448 | tf_op jit(solution)/shard_map/all_gather | solution.py:32
  7.3 196.8 %reduce-scatter.3.cloned.1.call-start = ((), (), s32[]{:S(2)}) async-start(), calls=%async_computation.3 | async-start | bytes 13369344 | tf_op jit(solution)/shard_map/reduce_scatter | solution.py:37
  122.3 0.8 copy-start.2
  122.4 140.8 %all-gather.5.cloned.1.call-start = ((), (), s32[]{:S(2)}) async-start(), calls=%async_computation.4 | async-start | bytes 8912896 | tf_op jit(solution)/shard_map/all_gather | solution.py:57
  123.1 356.7 %reduce-scatter.5.cloned.1.call-start = ((), (), s32[]{:S(2)}) async-start(), calls=%async_computation.5 | async-start | bytes 4456448 | tf_op jit(solution)/shard_map/reduce_scatter | solution.py:60
  132.9 2.7 slice-start
  205.2 6.0 %collective-permute-start = (bf16[127,512]{1,0:T(8,128)(2,1)S(1)}, bf16[127,512]{1,0:T(8,128)(2,1)S(1)}, u32[]{:S(2)}, u32[]{:S(2)}) collective-permute-start(bf16[127,512]{1,0:T(8,128)(2,1)S(1)} %slice_bitcast_fusion.2), channel_id=1, source_target_pairs={{0,16},{16,32},{32,48},{48,64},{64,80},{80,96},{96,112},{112,128},... | collective-permute-start | bytes 390152 | tf_op jit(solution)/shard_map/ppermute | solution.py:10
  211.7 2.7 copy-start.1
  214.4 48.8 %copy-start.3 = (f32[512]{0:T(512)S(1)}, f32[512]{0:T(512)}, u32[]{:S(2)}) copy-start(f32[512]{0:T(512)} %param.8) | copy-start | bytes 6148
Sparse Core Ops, SparseCore 0:
  9.9 100.5 all-gather.2
  122.5 81.5 reduce-scatter.2
  205.9 57.2 all-gather.4
  271.1 208.6 reduce-scatter.4
where the time goes:
time: 490 us; the launch traced here: 486 us
  waiting for transfers between devices  428 us (87%)
  matrix products  22.9 us (5%)
  local copies, waits for them, and re-layouts  14.9 us (3%)
  between operations  13.3 us (3%)
  other arithmetic  5.34 us (1%)
    reduce_scatter x1, waiting for transfers between devices, per_device(): lax.psum_scatter(partial_out.astype(jnp.bfloat16), 'tensor', scatter_dime...  209 us
    all_gather x1, waiting for transfers between devices, per_device(): gathered = lax.all_gather(tokens, 'tensor', axis=0, tiled=True)  103 us
    reduce_scatter x1, waiting for transfers between devices, per_device(): lax.psum_scatter(jnp.einsum('rf,sfc->rsc', gathered, in_weight, preferred...  64 us
    all_gather x1, waiting for transfers between devices, per_device(): lax.all_gather(out_weight, 'seq', axis=1, tiled=True)  47.4 us
    dot_general x1, matrix products, per_device(): jnp.einsum('rf,sfc->rsc', gathered, in_weight, preferred_element_type=jnp...  11.8 us
  transfers between devices with their start and end apart: 5, of which 5 were waited for; matrix products, arithmetic and copies ran while one was open for 4% of the time, Pallas kernels for 0%

commit v1 on v0

--- a/solution.py
+++ b/solution.py
@@ -1,11 +1,22 @@
 import jax
 import jax.numpy as jnp
 from jax import lax
-from jax.sharding import PartitionSpec as P
+from jax.sharding import Mesh, PartitionSpec as P
+
+
+SEQ = ("xlo", "y", "core")
+TEN = ("z", "xhi")
+
+
+def axis_size(names):
+    size = 1
+    for name in names:
+        size *= lax.axis_size(name)
+    return size
 
 
 def from_behind(x, axis, by):
-    peers = lax.axis_size(axis)
+    peers = axis_size(axis)
     pairs = [(i, i + by) for i in range(peers) if 0 <= i + by < peers]
     return lax.ppermute(x, axis, pairs)
 
@@ -29,8 +40,8 @@
 
 
 def per_device(tokens, in_weight, filters, skip_gain, out_weight):
-    gathered = lax.all_gather(tokens, "tensor", axis=0, tiled=True)
-    tok_dev = gathered.shape[0] // lax.axis_size("seq")
+    gathered = lax.all_gather(lax.all_gather(tokens, "xhi", axis=0, tiled=True), "z", axis=0, tiled=True)
+    tok_dev = gathered.shape[0] // axis_size(SEQ)
     channels = in_weight.shape[2]
     taps_count = filters.shape[1]
     group_width = channels // filters.shape[0]
@@ -38,7 +49,7 @@
         jnp.einsum("rf,sfc->rsc", gathered, in_weight, preferred_element_type=jnp.float32).astype(
             jnp.bfloat16
         ),
-        "seq",
+        SEQ,
         scatter_dimension=0,
         tiled=True,
     ).astype(jnp.float32)
@@ -46,7 +57,7 @@
     key_rows = summed[:, 1].astype(jnp.bfloat16)
     value_rows = summed[:, 2].astype(jnp.bfloat16)
     product = (key_rows.astype(jnp.float32) * value_rows.astype(jnp.float32)).astype(jnp.bfloat16)
-    previous = from_behind(product[tok_dev - (taps_count - 1) :], "seq", 1)
+    previous = from_behind(product[tok_dev - (taps_count - 1) :], SEQ, 1)
     product_f = product.astype(jnp.float32)
     extended = jnp.concatenate([previous, product], axis=0)
     conv = toeplitz_conv(extended, filters)
@@ -54,22 +65,27 @@
     gated = (query_rows.astype(jnp.float32) * conv).astype(jnp.bfloat16)
     partial_out = jnp.dot(
         gated,
-        lax.all_gather(out_weight, "seq", axis=1, tiled=True),
+        lax.all_gather(out_weight, SEQ, axis=1, tiled=True),
         preferred_element_type=jnp.float32,
     )
-    return lax.psum_scatter(
-        partial_out.astype(jnp.bfloat16), "tensor", scatter_dimension=1, tiled=True
-    )
+    rows, cols = partial_out.shape
+    n_z, n_x = lax.axis_size("z"), lax.axis_size("xhi")
+    split = partial_out.astype(jnp.bfloat16).reshape(rows, n_z, n_x, cols // (n_z * n_x))
+    split = lax.psum_scatter(split, "z", scatter_dimension=1, tiled=True)
+    split = lax.psum_scatter(split, "xhi", scatter_dimension=2, tiled=True)
+    return split.reshape(rows, cols // (n_z * n_x))
 
 
 def solution(mesh):
+    n_seq, n_ten = mesh.devices.shape
+    fine = Mesh(mesh.devices.reshape(2, 4, 2, n_ten // 2, 2), SEQ + TEN)
     placed = (
-        P("tensor", "seq"),
-        P(None, "seq", "tensor"),
-        P("tensor", None),
-        P("tensor"),
-        P("tensor", "seq"),
+        P(TEN, SEQ),
+        P(None, SEQ, TEN),
+        P(TEN, None),
+        P(TEN),
+        P(TEN, SEQ),
     )
     return jax.shard_map(
-        per_device, mesh=mesh, in_specs=placed, out_specs=P("seq", "tensor"), check_vma=False
+        per_device, mesh=fine, in_specs=placed, out_specs=P(SEQ, TEN), check_vma=False
     )

time: 490 us -> 335 us (0.68)
  waiting for transfers between devices: 428 us -> 248 us
  local copies, waits for them, and re-layouts: 14.9 us -> 28.8 us
  blocking collectives: 0 us -> 11.7 us
    reduce_scatter x1 -> x2, waiting for transfers between devices: 209 us -> 78.1 us  [the longest x1 56 us: per_device(): split = lax.psum_scatter(split, 'z', scatter_dimension=1, tiled=True)]
    all_gather x2, waiting for transfers between devices: 151 us -> 104 us  [the longest x1 57.7 us: per_device(): lax.all_gather(lax.all_gather(tokens, 'xhi', axis=0, tiled=True), 'z', ax...]
    reshape x0 -> x2, local copies, waits for them, and re-layouts: none -> 14.4 us  [per_device(): partial_out.astype(jnp.bfloat16)]
    all_gather x0 -> x1, blocking collectives: none -> 11.7 us  [per_device(): lax.all_gather(tokens, 'xhi', axis=0, tiled=True)]
  transfers between devices with their start and end apart: 5 -> 6, of which waited for: 5 -> 6; matrix products, arithmetic and copies ran while one was open for 4% -> 7% of each run, Pallas kernels for 0% -> 0%
where the time goes in v1:
time: 335 us; the launch traced here: 334 us
  waiting for transfers between devices  248 us (74%)
  local copies, waits for them, and re-layouts  28.8 us (9%)
  matrix products  24.4 us (7%)
  between operations  13.3 us (4%)
  blocking collectives  11.7 us (3%)
  other arithmetic  5.34 us (2%)
    reduce_scatter x1, waiting for transfers between devices, per_device(): lax.psum_scatter(jnp.einsum('rf,sfc->rsc', gathered, in_weight, preferred...  63.4 us
    all_gather x1, waiting for transfers between devices, per_device(): lax.all_gather(lax.all_gather(tokens, 'xhi', axis=0, tiled=True), 'z', ax...  57.7 us
    reduce_scatter x1, waiting for transfers between devices, per_device(): split = lax.psum_scatter(split, 'z', scatter_dimension=1, tiled=True)  56 us
    all_gather x1, waiting for transfers between devices, per_device(): lax.all_gather(out_weight, SEQ, axis=1, tiled=True)  45.9 us
    reduce_scatter x1, waiting for transfers between devices, per_device(): split = lax.psum_scatter(split, 'xhi', scatter_dimension=2, tiled=True)  22.1 us
    reshape x2, local copies, waits for them, and re-layouts, per_device(): partial_out.astype(jnp.bfloat16)  14.4 us
    dot_general x1, matrix products, per_device(): jnp.einsum('rf,sfc->rsc', gathered, in_weight, preferred_element_type=jnp...  11.8 us
    all_gather x1, blocking collectives, per_device(): lax.all_gather(tokens, 'xhi', axis=0, tiled=True)  11.7 us
  transfers between devices with their start and end apart: 6, of which 6 were waited for; matrix products, arithmetic and copies ran while one was open for 7% of the time, Pallas kernels for 0%

profile of v1, /device:TPU:1, one launch (start us, length us, event | category | flops | bytes accessed | tf_op | source)
XLA Modules:
  0.0 334.4 jit_solution(3243714141979442488)
XLA Ops:
  6.5 0.0 copy-start
  6.5 0.0 all-gather.3.cloned.1.call-start
  6.5 11.7 %all_gather.9 = bf16[512,512]{1,0:T(8,128)(2,1)} all-gather(bf16[256,512]{1,0:T(8,128)(2,1)} %param.5), channel_id=1, replica_groups=mesh['xlo'=2,'y'=4,'core'=2,'z'=8,'xhi'=2] {'xhi'}, dimensions={0}, use_global_device_ids=true | all-gather | bytes 786432 | tf_op jit(solution)/shard_map/all_gather | solution.py:43
  18.2 0.0 all-gather.3.cloned.1.call-update
  18.2 0.0 reduce-scatter.4.cloned.1.call-start
  18.3 57.7 %all-gather.3.cloned.1.call-done = bf16[4096,512]{1,0:T(8,128)(2,1)} async-done(((bf16[512,512]{1,0:T(8,128)(2,1)}), bf16[4096,512]{1,0:T(8,128)(2,1)}) %all-gather.3.cloned.1.call-update) | async-done | bytes 4194320 | tf_op jit(solution)/shard_map/all_gather | solution.py:43
  76.0 0.0 copy-done
  76.0 11.8 %convolution_convert_fusion.1 = bf16[4096,3,512]{2,0,1:T(8,128)(2,1)} fusion(bf16[3,512,512]{2,1,0:T(8,128)(2,1)S(1)} %copy-done, bf16[4096,512]{1,0:T(8,128)(2,1)} %all-gather.3.cloned.1.call-done), kind=kOutput, calls=%fused_computation.1 | convolution fusion | flops 6448742400 | bytes 18350080 | tf_op jit(solution)/shard_map/rf,sfc->rsc/dot_general | solution.py:49
  87.8 0.0 copy-start.2
  87.8 0.0 reduce-scatter.4.cloned.1.call-update
  87.8 0.0 all-gather.5.cloned.1.call-start
  87.9 0.7 all-gather.5.cloned.1.call-update
  88.6 0.0 reduce-scatter.6.cloned.1.call-start
  88.6 0.0 copy-done.2
  88.6 0.1 rev.3
  88.7 3.1 tile.4
  91.8 6.6 %tile.10 = f32[32,32896]{1,0:T(8,128)} reshape(f32[32,128,257]{2,1,0:T(8,128)} %tile.4) | data formatting | bytes 8421376 | tf_op jit(solution)/shard_map/tile | solution.py:34
  98.4 0.0 slice-start
  98.4 2.2 slice-done
  100.6 1.3 copy.19
  101.9 3.1 fusion
  105.0 63.4 %reduce-scatter.4.cloned.1.call-done = bf16[256,3,512]{2,0,1:T(8,128)(2,1)} async-done(((bf16[4096,3,512]{2,0,1:T(8,128)(2,1)}), bf16[256,3,512]{2,0,1:T(8,128)(2,1)}) %reduce-scatter.4.cloned.1.call-update) | async-done | bytes 786448 | tf_op jit(solution)/shard_map/reduce_scatter | solution.py:48
  168.4 1.1 multiply_convert_fusion
  169.5 2.3 collective-permute-start
  171.8 1.1 fusion.20
  172.9 2.6 collective-permute-done
  175.5 0.1 pad_slice_fusion
  175.6 0.1 copy.10
  175.8 0.1 slice.41
  175.8 0.1 copy.11
  176.0 0.1 slice.43
  176.0 0.1 copy_dynamic-update-slice_fusion.1
  176.1 0.1 copy_dynamic-update-slice_fusion
  176.2 2.4 fusion.2
  178.6 0.0 copy-start.3
  178.6 2.4 fusion.9
  181.0 0.3 copy.14
  181.3 0.2 copy.15
  181.5 45.9 %all-gather.5.cloned.1.call-done = bf16[512,8192]{1,0:T(8,128)(2,1)} async-done(((bf16[512,512]{1,0:T(8,128)(2,1)}), bf16[512,8192]{1,0:T(8,128)(2,1)}) %all-gather.5.cloned.1.call-update) | async-done | bytes 8388624 | tf_op jit(solution)/shard_map/all_gather | solution.py:68
  227.4 0.0 copy-done.3
  227.4 7.8 %convolution_convert_fusion = bf16[256,8192]{1,0:T(8,128)(2,1)} fusion(bf16[512,8192]{1,0:T(8,128)(2,1)} %all-gather.5.cloned.1.call-done, f32[256,512]{1,0:T(8,128)S(1)} %copy.15, bf16[256,3,512]{2,0,1:T(8,128)(2,1)} %reduce-scatter.4.cloned.1.call-done, f32[512]{0:T(512)S(1)} %copy-done.3, bf16[256,1,512]{2,0,1:T(8,128)(2,1)S(1)} %multiply_convert_fusion), kind=kOutput, calls=%fused_computation | convolution fusion | flops 2150367232 | bytes 13633536 | tf_op jit(solution)/shard_map/dot_general | solution.py:66
  235.2 7.8 %reshape.32 = bf16[256,8,2,512]{3,2,1,0:T(2,128)(2,1)} reshape(bf16[256,8192]{1,0:T(8,128)(2,1)} %convolution_convert_fusion) | data formatting | bytes 8388608 | tf_op jit(solution)/shard_map/reshape | solution.py:73
  243.0 0.0 copy-start.1
  243.0 6.6 %copy.16 = bf16[256,8,2,512]{3,0,2,1:T(8,128)(2,1)} copy(bf16[256,8,2,512]{3,2,1,0:T(2,128)(2,1)} %reshape.32) | data formatting | bytes 8388608 | tf_op jit(solution)/shard_map/reshape | solution.py:73
  249.6 0.0 reduce-scatter.6.cloned.1.call-update
  249.7 0.0 reduce-scatter.8.cloned.1.call-start
  249.7 56.0 %reduce-scatter.6.cloned.1.call-done = bf16[256,1,2,512]{3,0,2,1:T(8,128)(2,1)} async-done(((bf16[256,8,2,512]{3,0,2,1:T(8,128)(2,1)}), bf16[256,1,2,512]{3,0,2,1:T(8,128)(2,1)}) %reduce-scatter.6.cloned.1.call-update) | async-done | bytes 524304 | tf_op jit(solution)/shard_map/reduce_scatter | solution.py:74
  305.7 0.0 reduce-scatter.8.cloned.1.call-update
  305.8 22.1 %reduce-scatter.8.cloned.1.call-done = bf16[256,1,1,512]{3,0,2,1:T(8,128)(2,1)} async-done(((bf16[256,1,2,512]{3,0,2,1:T(8,128)(2,1)}), bf16[256,1,1,512]{3,0,2,1:T(8,128)(2,1)}) %reduce-scatter.8.cloned.1.call-update) | async-done | bytes 262160 | tf_op jit(solution)/shard_map/reduce_scatter | solution.py:75
  327.9 0.0 copy-done.1
  (3 shorter events, 0.1 us)
Async XLA Ops:
  6.5 69.5 %copy-start = (bf16[3,512,512]{2,1,0:T(8,128)(2,1)S(1)}, bf16[3,512,512]{2,1,0:T(8,128)(2,1)}, u32[]{:S(2)}) copy-start(bf16[3,512,512]{2,1,0:T(8,128)(2,1)} %param.6) | copy-start | bytes 4718596
  6.5 69.5 %all-gather.3.cloned.1.call-start = ((), (), s32[]{:S(2)}) async-start(), calls=%async_computation.3 | async-start | bytes 4718592 | tf_op jit(solution)/shard_map/all_gather | solution.py:43
  18.2 150.2 %reduce-scatter.4.cloned.1.call-start = ((), (), s32[]{:S(2)}) async-start(), calls=%async_computation.4 | async-start | bytes 13369344 | tf_op jit(solution)/shard_map/reduce_scatter | solution.py:48
  87.8 0.8 copy-start.2
  87.8 139.6 %all-gather.5.cloned.1.call-start = ((), (), s32[]{:S(2)}) async-start(), calls=%async_computation.5 | async-start | bytes 8912896 | tf_op jit(solution)/shard_map/all_gather | solution.py:68
  88.6 217.2 %reduce-scatter.6.cloned.1.call-start = ((), (), s32[]{:S(2)}) async-start(), calls=%async_computation.6 | async-start | bytes 4718592 | tf_op jit(solution)/shard_map/reduce_scatter | solution.py:74
  98.4 2.2 slice-start
  169.5 6.0 %collective-permute-start = (bf16[127,512]{1,0:T(8,128)(2,1)S(1)}, bf16[127,512]{1,0:T(8,128)(2,1)S(1)}, u32[]{:S(2)}, u32[]{:S(2)}) collective-permute-start(bf16[127,512]{1,0:T(8,128)(2,1)S(1)} %slice_bitcast_fusion.2), channel_id=1, source_target_pairs={{0,16},{16,32},{32,48},{48,64},{64,80},{80,96},{96,112},{112,128},... | collective-permute-start | bytes 390152 | tf_op jit(solution)/shard_map/ppermute | solution.py:21
  178.6 48.8 %copy-start.3 = (f32[512]{0:T(512)S(1)}, f32[512]{0:T(512)}, u32[]{:S(2)}) copy-start(f32[512]{0:T(512)} %param.8) | copy-start | bytes 6148
  243.0 84.8 %copy-start.1 = (bf16[3,512,512]{2,1,0:T(8,128)(2,1)S(1)}, bf16[3,512,512]{2,1,0:T(8,128)(2,1)}, u32[]{:S(2)}) copy-start(bf16[3,512,512]{2,1,0:T(8,128)(2,1)} %param.6) | copy-start | bytes 4718596
  249.7 78.2 %reduce-scatter.8.cloned.1.call-start = ((), (), s32[]{:S(2)}) async-start(), calls=%async_computation.7 | async-start | bytes 786432 | tf_op jit(solution)/shard_map/reduce_scatter | solution.py:75
Sparse Core Ops, SparseCore 0:
  18.4 57.6 all-gather.2
  87.9 80.4 reduce-scatter.3
  170.2 57.1 all-gather.4
  249.8 55.9 reduce-scatter.5
  308.1 19.7 reduce-scatter.7

commit v2 on v1

--- a/solution.py
+++ b/solution.py
@@ -63,17 +63,17 @@
     conv = toeplitz_conv(extended, filters)
     conv = conv + skip_gain[None, :] * product_f
     gated = (query_rows.astype(jnp.float32) * conv).astype(jnp.bfloat16)
-    partial_out = jnp.dot(
-        gated,
-        lax.all_gather(out_weight, SEQ, axis=1, tiled=True),
-        preferred_element_type=jnp.float32,
-    )
-    rows, cols = partial_out.shape
-    n_z, n_x = lax.axis_size("z"), lax.axis_size("xhi")
-    split = partial_out.astype(jnp.bfloat16).reshape(rows, n_z, n_x, cols // (n_z * n_x))
-    split = lax.psum_scatter(split, "z", scatter_dimension=1, tiled=True)
-    split = lax.psum_scatter(split, "xhi", scatter_dimension=2, tiled=True)
-    return split.reshape(rows, cols // (n_z * n_x))
+    w_chips = lax.all_gather(out_weight, ("xlo", "y"), axis=0, tiled=False)
+    w_all = lax.all_gather(w_chips, "core", axis=0, tiled=False)
+    partial_out = jnp.einsum(
+        "tc,jkco->jkto", gated, jnp.swapaxes(w_all, 0, 1), preferred_element_type=jnp.float32
+    ).astype(jnp.bfloat16)
+    by_z = lax.psum_scatter(partial_out, "z", scatter_dimension=0, tiled=True)[0]
+    me = lax.axis_index("xhi")
+    keep = lax.dynamic_index_in_dim(by_z, me, 0, keepdims=False)
+    give = lax.dynamic_index_in_dim(by_z, 1 - me, 0, keepdims=False)
+    got = lax.ppermute(give, "xhi", [(0, 1), (1, 0)])
+    return (keep.astype(jnp.float32) + got.astype(jnp.float32)).astype(jnp.bfloat16)
 
 
 def solution(mesh):

time: 335 us -> 327 us (0.976)
  local copies, waits for them, and re-layouts: 28.8 us -> 15.4 us
    reduce_scatter x2 -> x1, waiting for transfers between devices: 78.1 us -> 56.1 us  [per_device(): lax.psum_scatter(partial_out, 'z', scatter_dimension=0, tiled=True)[0]]
    reshape x2 -> x0, local copies, waits for them, and re-layouts: 14.4 us -> none  [per_device(): partial_out.astype(jnp.bfloat16)]
    all_gather x1 -> x2, waiting for transfers between devices: 45.9 us -> 60.3 us  [the longest x1 43.7 us: per_device(): w_chips = lax.all_gather(out_weight, ('xlo', 'y'), axis=0, tiled=False)]
    ppermute x0 -> x1, waiting for transfers between devices: none -> 6.08 us  [per_device(): got = lax.ppermute(give, 'xhi', [(0, 1), (1, 0)])]
    reduce_scatter x1, waiting for transfers between devices: 63.4 us -> 66.8 us  [per_device(): lax.psum_scatter(jnp.einsum('rf,sfc->rsc', gathered, in_weight, preferred...]
  transfers between devices with their start and end apart: 6 -> 7, of which waited for: 6 -> 7; matrix products, arithmetic and copies ran while one was open for 7% -> 10% of each run, Pallas kernels for 0% -> 0%
where the time goes in v2:
time: 327 us
  waiting for transfers between devices  250 us (76%)
  matrix products  24.5 us (7%)
  local copies, waits for them, and re-layouts  15.4 us (5%)
  between operations  13.3 us (4%)
  blocking collectives  11.6 us (4%)
  other arithmetic  7.03 us (2%)
  starting transfers between devices  5.06 us (2%)
    reduce_scatter x1, waiting for transfers between devices, per_device(): lax.psum_scatter(jnp.einsum('rf,sfc->rsc', gathered, in_weight, preferred...  66.8 us
    all_gather x1, waiting for transfers between devices, per_device(): lax.all_gather(lax.all_gather(tokens, 'xhi', axis=0, tiled=True), 'z', ax...  57 us
    reduce_scatter x1, waiting for transfers between devices, per_device(): lax.psum_scatter(partial_out, 'z', scatter_dimension=0, tiled=True)[0]  56.1 us
    all_gather x1, waiting for transfers between devices, per_device(): w_chips = lax.all_gather(out_weight, ('xlo', 'y'), axis=0, tiled=False)  43.7 us
    all_gather x1, waiting for transfers between devices, per_device(): w_all = lax.all_gather(w_chips, 'core', axis=0, tiled=False)  16.6 us
    dot_general x1, matrix products, per_device(): jnp.einsum('rf,sfc->rsc', gathered, in_weight, preferred_element_type=jnp...  11.8 us
    all_gather x1, blocking collectives, per_device(): lax.all_gather(tokens, 'xhi', axis=0, tiled=True)  11.6 us
    another operation x2, local copies, waits for them, and re-layouts, toeplitz_conv(): jnp.tile(w, (1, taps))[:, :taps * 2 * taps].reshape(groups, taps, 2 * taps)  9.74 us
  transfers between devices with their start and end apart: 7, of which 7 were waited for; matrix products, arithmetic and copies ran while one was open for 10% of the time, Pallas kernels for 0%

profile of v2, /device:TPU:1, one launch (start us, length us, event | category | flops | bytes accessed | tf_op | source)
XLA Modules:
  0.0 326.6 jit_solution(2877533018983542358)
XLA Ops:
  6.5 0.0 copy-start
  6.5 0.0 all-gather.6.cloned.1.call-start
  6.5 11.6 %all_gather.18 = bf16[512,512]{1,0:T(8,128)(2,1)} all-gather(bf16[256,512]{1,0:T(8,128)(2,1)} %param.5), channel_id=1, replica_groups=mesh['xlo'=2,'y'=4,'core'=2,'z'=8,'xhi'=2] {'xhi'}, dimensions={0}, use_global_device_ids=true | all-gather | bytes 786432 | tf_op jit(solution)/shard_map/all_gather | solution.py:43
  18.2 0.0 all-gather.6.cloned.1.call-update
  18.2 0.0 all-gather.8.cloned.1.call-start
  18.3 0.7 all-gather.8.cloned.1.call-update
  19.0 0.0 reduce-scatter.3.cloned.1.call-start
  19.0 57.0 %all-gather.6.cloned.1.call-done = bf16[4096,512]{1,0:T(8,128)(2,1)} async-done(((bf16[512,512]{1,0:T(8,128)(2,1)}), bf16[4096,512]{1,0:T(8,128)(2,1)}) %all-gather.6.cloned.1.call-update) | async-done | bytes 4194320 | tf_op jit(solution)/shard_map/all_gather | solution.py:43
  76.0 0.0 copy-done
  76.0 11.8 %convolution_convert_fusion = bf16[4096,3,512]{2,0,1:T(8,128)(2,1)} fusion(bf16[3,512,512]{2,1,0:T(8,128)(2,1)S(1)} %copy-done, bf16[4096,512]{1,0:T(8,128)(2,1)} %all-gather.6.cloned.1.call-done), kind=kOutput, calls=%fused_computation | convolution fusion | flops 6448742400 | bytes 18350080 | tf_op jit(solution)/shard_map/rf,sfc->rsc/dot_general | solution.py:49
  87.8 0.0 reduce-scatter.3.cloned.1.call-update
  87.8 0.0 copy-start.2
  87.8 0.0 all-gather.10.cloned.1.call-start
  87.9 43.7 %all-gather.8.cloned.1.call-done = bf16[4096,512]{1,0:T(8,128)(2,1)} async-done(((bf16[512,512]{1,0:T(8,128)(2,1)}), bf16[4096,512]{1,0:T(8,128)(2,1)}) %all-gather.8.cloned.1.call-update) | async-done | bytes 4194320 | tf_op jit(solution)/shard_map/all_gather | solution.py:66
  131.6 0.0 all-gather.10.cloned.1.call-update
  131.6 0.0 reduce-scatter.5.cloned.1.call-start
  131.6 0.0 copy-done.2
  131.7 0.1 rev.3
  131.7 3.1 tile.4
  134.8 6.7 %tile.10 = f32[32,32896]{1,0:T(8,128)} reshape(f32[32,128,257]{2,1,0:T(8,128)} %tile.4) | data formatting | bytes 8421376 | tf_op jit(solution)/shard_map/tile | solution.py:34
  141.5 0.0 slice-start
  141.5 2.2 slice-done
  143.7 1.3 copy.26
  144.9 3.1 fusion.3
  148.0 66.8 %reduce-scatter.3.cloned.1.call-done = bf16[256,3,512]{2,0,1:T(8,128)(2,1)} async-done(((bf16[4096,3,512]{2,0,1:T(8,128)(2,1)}), bf16[256,3,512]{2,0,1:T(8,128)(2,1)}) %reduce-scatter.3.cloned.1.call-update) | async-done | bytes 786448 | tf_op jit(solution)/shard_map/reduce_scatter | solution.py:48
  214.8 1.1 multiply_convert_fusion
  215.9 2.1 collective-permute-start
  218.1 1.1 fusion.26
  219.2 2.8 collective-permute-done
  221.9 0.1 pad_slice_fusion
  222.0 0.1 copy.16
  222.1 0.1 slice.41
  222.2 0.1 copy.17
  222.4 0.1 slice.43
  222.4 0.1 copy_dynamic-update-slice_fusion.1
  222.5 0.1 copy_dynamic-update-slice_fusion
  222.6 2.4 fusion.7
  225.0 0.0 copy-start.3
  225.0 2.4 fusion.14
  227.4 0.3 copy.20
  227.7 0.2 copy.21
  227.9 16.6 %all-gather.10.cloned.1.call-done = bf16[16,512,512]{2,1,0:T(8,128)(2,1)} async-done(((bf16[8,512,512]{2,1,0:T(8,128)(2,1)}), bf16[16,512,512]{2,1,0:T(8,128)(2,1)}) %all-gather.10.cloned.1.call-update) | async-done | bytes 8388624 | tf_op jit(solution)/shard_map/all_gather | solution.py:67
  244.5 0.0 copy-done.3
  244.5 0.0 copy-start.1
  244.5 7.9 %convert_bitcast_fusion = bf16[8,2,256,512]{3,2,1,0:T(8,128)(2,1)} fusion(bf16[2,8,512,512]{3,2,1,0:T(8,128)(2,1)} %bitcast.77, f32[256,512]{1,0:T(8,128)S(1)} %copy.21, bf16[256,3,512]{2,0,1:T(8,128)(2,1)} %reduce-scatter.3.cloned.1.call-done, f32[512]{0:T(512)S(1)} %copy-done.3, bf16[256,1,512]{2,0,1:T(8,128)(2,1)S(1)} %multiply_convert_fusion), kind=kOutput, calls=%fused_computation.8 | convolution fusion | flops 2150367232 | bytes 13633536 | tf_op jit(solution)/shard_map/tc,jkco->jkto/dot_general | solution.py:68
  252.4 0.0 reduce-scatter.5.cloned.1.call-update
  252.4 56.1 %reduce-scatter.5.cloned.1.call-done = bf16[1,2,256,512]{3,2,1,0:T(8,128)(2,1)} async-done(((bf16[8,2,256,512]{3,2,1,0:T(8,128)(2,1)}), bf16[1,2,256,512]{3,2,1,0:T(8,128)(2,1)}) %reduce-scatter.5.cloned.1.call-update) | async-done | bytes 524304 | tf_op jit(solution)/shard_map/reduce_scatter | solution.py:71
  308.5 1.0 dynamic-slice_bitcast_fusion
  309.5 2.8 collective-permute-start.1
  312.3 6.1 %collective-permute-done.1 = bf16[256,512]{1,0:T(8,128)(2,1)S(1)} collective-permute-done((bf16[256,512]{1,0:T(8,128)(2,1)S(1)}, bf16[256,512]{1,0:T(8,128)(2,1)S(1)}, u32[]{:S(2)}, u32[]{:S(2)}) %collective-permute-start.1) | collective-permute-done | bytes 262176 | tf_op jit(solution)/shard_map/ppermute | solution.py:75
  318.3 1.7 fusion.17
  320.1 0.0 copy-done.1
  (3 shorter events, 0.1 us)
Async XLA Ops:
  6.5 69.5 %copy-start = (bf16[3,512,512]{2,1,0:T(8,128)(2,1)S(1)}, bf16[3,512,512]{2,1,0:T(8,128)(2,1)}, u32[]{:S(2)}) copy-start(bf16[3,512,512]{2,1,0:T(8,128)(2,1)} %param.6) | copy-start | bytes 4718596
  6.5 69.5 %all-gather.6.cloned.1.call-start = ((), (), s32[]{:S(2)}) async-start(), calls=%async_computation.2 | async-start | bytes 4718592 | tf_op jit(solution)/shard_map/all_gather | solution.py:43
  18.2 113.4 %all-gather.8.cloned.1.call-start = ((), (), s32[]{:S(2)}) async-start(), calls=%async_computation.5 | async-start | bytes 4718592 | tf_op jit(solution)/shard_map/all_gather | solution.py:66
  19.0 195.8 %reduce-scatter.3.cloned.1.call-start = ((), (), s32[]{:S(2)}) async-start(), calls=%async_computation.3 | async-start | bytes 13369344 | tf_op jit(solution)/shard_map/reduce_scatter | solution.py:48
  87.8 43.8 %copy-start.2 = (f32[32,128]{1,0:T(8,128)S(1)}, f32[32,128]{1,0:T(8,128)}, u32[]{:S(2)}) copy-start(f32[32,128]{1,0:T(8,128)} %param.7) | copy-start | bytes 49156
  87.8 156.7 %all-gather.10.cloned.1.call-start = ((), (), s32[]{:S(2)}) async-start(), calls=%async_computation.6 | async-start | bytes 12582912 | tf_op jit(solution)/shard_map/all_gather | solution.py:67
  131.6 176.9 %reduce-scatter.5.cloned.1.call-start = ((), (), s32[]{:S(2)}) async-start(), calls=%async_computation.4 | async-start | bytes 4718592 | tf_op jit(solution)/shard_map/reduce_scatter | solution.py:71
  141.5 2.2 slice-start
  215.9 6.0 %collective-permute-start = (bf16[127,512]{1,0:T(8,128)(2,1)S(1)}, bf16[127,512]{1,0:T(8,128)(2,1)S(1)}, u32[]{:S(2)}, u32[]{:S(2)}) collective-permute-start(bf16[127,512]{1,0:T(8,128)(2,1)S(1)} %slice_bitcast_fusion.2), channel_id=1, source_target_pairs={{0,16},{16,32},{32,48},{48,64},{64,80},{80,96},{96,112},{112,128},... | collective-permute-start | bytes 390152 | tf_op jit(solution)/shard_map/ppermute | solution.py:21
  225.0 19.5 %copy-start.3 = (f32[512]{0:T(512)S(1)}, f32[512]{0:T(512)}, u32[]{:S(2)}) copy-start(f32[512]{0:T(512)} %param.8) | copy-start | bytes 6148
  244.5 75.5 %copy-start.1 = (bf16[3,512,512]{2,1,0:T(8,128)(2,1)S(1)}, bf16[3,512,512]{2,1,0:T(8,128)(2,1)}, u32[]{:S(2)}) copy-start(bf16[3,512,512]{2,1,0:T(8,128)(2,1)} %param.6) | copy-start | bytes 4718596
  309.5 8.8 %collective-permute-start.1 = (bf16[256,512]{1,0:T(8,128)(2,1)S(1)}, bf16[256,512]{1,0:T(8,128)(2,1)S(1)}, u32[]{:S(2)}, u32[]{:S(2)}) collective-permute-start(bf16[256,512]{1,0:T(8,128)(2,1)S(1)} %dynamic-slice_bitcast_fusion), channel_id=1, source_target_pairs={{0,1},{1,0},{2,3},{3,2},{4,5},{5,4},{6,7},{7,6},{8,9},{9,8},{10,11... | collective-permute-start | bytes 786440 | tf_op jit(solution)/shard_map/ppermute | solution.py:75
Sparse Core Ops, SparseCore 0:
  18.3 57.6 all-gather.5
  77.8 53.7 all-gather.7
  134.1 80.5 reduce-scatter.2
  216.4 28.0 all-gather.9
  252.6 55.9 reduce-scatter.4

commit v3 on v2

--- a/solution.py
+++ b/solution.py
@@ -41,6 +41,10 @@
 
 def per_device(tokens, in_weight, filters, skip_gain, out_weight):
     gathered = lax.all_gather(lax.all_gather(tokens, "xhi", axis=0, tiled=True), "z", axis=0, tiled=True)
+    chips = axis_size(("xlo", "y"))
+    spread = jnp.broadcast_to(out_weight[None], (chips,) + out_weight.shape)
+    w_mine = lax.all_to_all(spread, ("xlo", "y"), 0, 0, tiled=True)
+    gathered, w_mine = lax.optimization_barrier((gathered, w_mine))
     tok_dev = gathered.shape[0] // axis_size(SEQ)
     channels = in_weight.shape[2]
     taps_count = filters.shape[1]
@@ -63,15 +67,14 @@
     conv = toeplitz_conv(extended, filters)
     conv = conv + skip_gain[None, :] * product_f
     gated = (query_rows.astype(jnp.float32) * conv).astype(jnp.bfloat16)
-    w_chips = lax.all_gather(out_weight, ("xlo", "y"), axis=0, tiled=False)
-    w_all = lax.all_gather(w_chips, "core", axis=0, tiled=False)
+    w_other = lax.ppermute(w_mine, "core", [(0, 1), (1, 0)])
     partial_out = jnp.einsum(
-        "tc,jkco->jkto", gated, jnp.swapaxes(w_all, 0, 1), preferred_element_type=jnp.float32
+        "tc,jmco->jmto", gated, jnp.stack([w_mine, w_other], axis=1), preferred_element_type=jnp.float32
     ).astype(jnp.bfloat16)
     by_z = lax.psum_scatter(partial_out, "z", scatter_dimension=0, tiled=True)[0]
-    me = lax.axis_index("xhi")
-    keep = lax.dynamic_index_in_dim(by_z, me, 0, keepdims=False)
-    give = lax.dynamic_index_in_dim(by_z, 1 - me, 0, keepdims=False)
+    keep_at = (lax.axis_index("xhi") != lax.axis_index("core")).astype(jnp.int32)
+    keep = lax.dynamic_index_in_dim(by_z, keep_at, 0, keepdims=False)
+    give = lax.dynamic_index_in_dim(by_z, 1 - keep_at, 0, keepdims=False)
     got = lax.ppermute(give, "xhi", [(0, 1), (1, 0)])
     return (keep.astype(jnp.float32) + got.astype(jnp.float32)).astype(jnp.bfloat16)
 

time: 327 us -> 267 us (0.82)
  waiting for transfers between devices: 250 us -> 135 us
  blocking collectives: 11.6 us -> 63.7 us
    all_gather x2 -> x0, waiting for transfers between devices: 60.3 us -> none  [the longest x1 43.7 us: per_device(): w_chips = lax.all_gather(out_weight, ('xlo', 'y'), axis=0, tiled=False)]
    all_gather x1, waiting for transfers between devices: 57 us -> 4.05 us  [per_device(): lax.all_gather(lax.all_gather(tokens, 'xhi', axis=0, tiled=True), 'z', ax...]
    all_to_all x0 -> x1, blocking collectives: none -> 52 us  [per_device(): w_mine = lax.all_to_all(spread, ('xlo', 'y'), 0, 0, tiled=True)]
    reduce_scatter x1, waiting for transfers between devices: 66.8 us -> 63.4 us  [per_device(): lax.psum_scatter(jnp.einsum('rf,sfc->rsc', gathered, in_weight, preferred...]
  transfers between devices with their start and end apart: 7 -> 6, of which waited for: 7 -> 5; matrix products, arithmetic and copies ran while one was open for 10% -> 9% of each run, Pallas kernels for 0% -> 0%
where the time goes in v3:
time: 267 us
  waiting for transfers between devices  135 us (51%)
  blocking collectives  63.7 us (24%)
  matrix products  24.5 us (9%)
  local copies, waits for them, and re-layouts  17.8 us (7%)
  between operations  13.3 us (5%)
  other arithmetic  6.34 us (2%)
  starting transfers between devices  5.91 us (2%)
    reduce_scatter x1, waiting for transfers between devices, per_device(): lax.psum_scatter(jnp.einsum('rf,sfc->rsc', gathered, in_weight, preferred...  63.4 us
    reduce_scatter x1, waiting for transfers between devices, per_device(): lax.psum_scatter(partial_out, 'z', scatter_dimension=0, tiled=True)[0]  59 us
    all_to_all x1, blocking collectives, per_device(): w_mine = lax.all_to_all(spread, ('xlo', 'y'), 0, 0, tiled=True)  52 us
    dot_general x1, matrix products, per_device(): jnp.einsum('rf,sfc->rsc', gathered, in_weight, preferred_element_type=jnp...  11.8 us
    all_gather x1, blocking collectives, per_device(): lax.all_gather(tokens, 'xhi', axis=0, tiled=True)  11.7 us
    another operation x2, local copies, waits for them, and re-layouts, toeplitz_conv(): jnp.tile(w, (1, taps))[:, :taps * 2 * taps].reshape(groups, taps, 2 * taps)  9.67 us
    dot_general x1, matrix products, per_device(): jnp.einsum('tc,jmco->jmto', gated, jnp.stack([w_mine, w_other], axis=1),...  7.93 us
    ppermute x1, waiting for transfers between devices, per_device(): got = lax.ppermute(give, 'xhi', [(0, 1), (1, 0)])  6.04 us
  transfers between devices with their start and end apart: 6, of which 5 were waited for; matrix products, arithmetic and copies ran while one was open for 9% of the time, Pallas kernels for 0%

profile of v3, /device:TPU:1, one launch (start us, length us, event | category | flops | bytes accessed | tf_op | source)
XLA Modules:
  0.0 266.7 jit_solution(395714901842107545)
XLA Ops:
  6.5 0.0 copy-start
  6.5 0.0 all-gather.2.cloned.1.call-start
  6.5 11.7 %all_gather.6 = bf16[512,512]{1,0:T(8,128)(2,1)} all-gather(bf16[256,512]{1,0:T(8,128)(2,1)} %param.5), channel_id=1, replica_groups=mesh['xlo'=2,'y'=4,'core'=2,'z'=8,'xhi'=2] {'xhi'}, dimensions={0}, use_global_device_ids=true | all-gather | bytes 786432 | tf_op jit(solution)/shard_map/all_gather | solution.py:43
  18.2 0.0 all-gather.2.cloned.1.call-update
  18.3 0.0 reduce-scatter.3.cloned.1.call-start
  18.3 1.3 copy.12
  19.6 0.4 broadcast_in_dim.2
  19.9 52.0 %all_to_all.5 = bf16[8,512,512]{1,2,0:T(8,128)(2,1)} all-to-all(bf16[8,512,512]{1,2,0:T(8,128)(2,1)S(1)} %broadcast_in_dim.2), channel_id=1, replica_groups=mesh['xlo'=2,'y'=4,'core'=2,'z'=8,'xhi'=2] {'xlo','y'}, dimensions={0} | all-to-all | bytes 8388608 | tf_op jit(solution)/shard_map/all_to_all | solution.py:46
  71.9 4.1 %all-gather.2.cloned.1.call-done = bf16[4096,512]{1,0:T(8,128)(2,1)} async-done(((bf16[512,512]{1,0:T(8,128)(2,1)}), bf16[4096,512]{1,0:T(8,128)(2,1)}) %all-gather.2.cloned.1.call-update) | async-done | bytes 4194320 | tf_op jit(solution)/shard_map/all_gather | solution.py:43
  76.0 0.0 copy-done
  76.0 11.8 %convolution_convert_fusion = bf16[4096,3,512]{2,0,1:T(8,128)(2,1)} fusion(bf16[3,512,512]{2,1,0:T(8,128)(2,1)S(1)} %copy-done, bf16[4096,512]{1,0:T(8,128)(2,1)} %all-gather.2.cloned.1.call-done), kind=kOutput, calls=%fused_computation | convolution fusion | flops 6448742400 | bytes 18350080 | tf_op jit(solution)/shard_map/rf,sfc->rsc/dot_general | solution.py:53
  87.8 0.0 copy-start.2
  87.8 0.0 reduce-scatter.3.cloned.1.call-update
  87.8 0.0 reduce-scatter.5.cloned.1.call-start
  87.9 0.8 collective-permute-start
  88.6 0.0 copy-done.2
  88.6 0.1 rev.3
  88.7 3.0 %tile.4 = f32[32,128,257]{2,1,0:T(8,128)} broadcast(f32[32,257]{1,0:T(8,128)S(1)} %pad.5), dimensions={0,2} | broadcast | bytes 4243584 | tf_op jit(solution)/shard_map/tile | solution.py:34
  91.7 6.7 %tile.10 = f32[32,32896]{1,0:T(8,128)} reshape(f32[32,128,257]{2,1,0:T(8,128)} %tile.4) | data formatting | bytes 8421376 | tf_op jit(solution)/shard_map/tile | solution.py:34
  98.4 0.0 slice-start
  98.4 2.2 slice-done
  100.6 1.3 copy.24
  101.9 3.1 %fusion.4 = (bf16[32,128,256]{2,1,0:T(8,128)(2,1)}, bf16[32,128,256]{2,1,0:T(8,128)(2,1)}) fusion(f32[4,8,128,256]{3,2,1,0:T(8,128)S(1)} %copy.24), kind=kLoop, calls=%fused_computation.7 | loop fusion | flops 4194304 | bytes 8388608 | tf_op jit(solution)/shard_map/convert_element_type | solution.py:36
  105.0 63.4 %reduce-scatter.3.cloned.1.call-done = bf16[256,3,512]{2,0,1:T(8,128)(2,1)} async-done(((bf16[4096,3,512]{2,0,1:T(8,128)(2,1)}), bf16[256,3,512]{2,0,1:T(8,128)(2,1)}) %reduce-scatter.3.cloned.1.call-update) | async-done | bytes 786448 | tf_op jit(solution)/shard_map/reduce_scatter | solution.py:52
  168.4 1.1 multiply_convert_fusion
  169.5 2.3 collective-permute-start.1
  171.8 1.1 fusion.28
  172.9 2.6 collective-permute-done.1
  175.5 0.1 pad_slice_fusion
  175.6 0.1 copy.14
  175.7 0.1 slice.41
  175.8 0.1 copy.15
  176.0 0.1 slice.43
  176.0 0.1 copy_dynamic-update-slice_fusion.1
  176.1 0.1 copy_dynamic-update-slice_fusion
  176.2 2.4 fusion.8
  178.6 0.0 copy-start.3
  178.6 2.4 fusion.15
  181.0 0.3 copy.18
  181.3 0.2 copy.19
  181.5 0.0 collective-permute-done
  181.6 0.0 copy-done.3
  181.6 0.0 copy-start.1
  181.6 7.9 %convert_bitcast_fusion = bf16[8,2,256,512]{2,3,1,0:T(8,128)(2,1)} fusion(bf16[8,1,512,512]{2,3,1,0:T(8,128)(2,1)} %bitcast.2, bf16[8,1,512,512]{2,3,1,0:T(8,128)(2,1)} %bitcast.71, f32[256,512]{1,0:T(8,128)S(1)} %copy.19, bf16[256,3,512]{2,0,1:T(8,128)(2,1)} %reduce-scatter.3.cloned.1.call-done, f32[512]{0:T(512)S(1)} %copy-done.3, ...), kind=kOutput, calls=%fused_computation.9 | convolution fusion | flops 2154561536 | bytes 13633536 | tf_op jit(solution)/shard_map/tc,jmco->jmto/dot_general | solution.py:71
  189.5 0.0 reduce-scatter.5.cloned.1.call-update
  189.5 59.0 %reduce-scatter.5.cloned.1.call-done = bf16[1,2,256,512]{2,3,1,0:T(8,128)(2,1)} async-done(((bf16[8,2,256,512]{2,3,1,0:T(8,128)(2,1)}), bf16[1,2,256,512]{2,3,1,0:T(8,128)(2,1)}) %reduce-scatter.5.cloned.1.call-update) | async-done | bytes 524304 | tf_op jit(solution)/shard_map/reduce_scatter | solution.py:74
  248.6 1.0 dynamic-slice_bitcast_fusion
  249.5 2.8 %collective-permute-start.2 = (bf16[256,512]{0,1:T(8,128)(2,1)S(1)}, bf16[256,512]{0,1:T(8,128)(2,1)S(1)}, u32[]{:S(2)}, u32[]{:S(2)}) collective-permute-start(bf16[256,512]{0,1:T(8,128)(2,1)S(1)} %dynamic-slice_bitcast_fusion), channel_id=1, source_target_pairs={{0,1},{1,0},{2,3},{3,2},{4,5},{5,4},{6,7},{7,6},{8,9},{9,8},{10,11... | collective-permute-start | bytes 786440 | tf_op jit(solution)/shard_map/ppermute | solution.py:78
  252.3 6.0 %collective-permute-done.2 = bf16[256,512]{0,1:T(8,128)(2,1)S(1)} collective-permute-done((bf16[256,512]{0,1:T(8,128)(2,1)S(1)}, bf16[256,512]{0,1:T(8,128)(2,1)S(1)}, u32[]{:S(2)}, u32[]{:S(2)}) %collective-permute-start.2) | collective-permute-done | bytes 262176 | tf_op jit(solution)/shard_map/ppermute | solution.py:78
  258.3 1.0 fusion.18
  259.4 0.8 copy.20
  260.2 0.0 copy-done.1
  (3 shorter events, 0.1 us)
Async XLA Ops:
  6.5 69.5 %copy-start = (bf16[3,512,512]{2,1,0:T(8,128)(2,1)S(1)}, bf16[3,512,512]{2,1,0:T(8,128)(2,1)}, u32[]{:S(2)}) copy-start(bf16[3,512,512]{2,1,0:T(8,128)(2,1)} %param.6) | copy-start | bytes 4718596
  6.5 69.5 %all-gather.2.cloned.1.call-start = ((), (), s32[]{:S(2)}) async-start(), calls=%async_computation.3 | async-start | bytes 4718592 | tf_op jit(solution)/shard_map/all_gather | solution.py:43
  18.3 150.1 %reduce-scatter.3.cloned.1.call-start = ((), (), s32[]{:S(2)}) async-start(), calls=%async_computation.4 | async-start | bytes 13369344 | tf_op jit(solution)/shard_map/reduce_scatter | solution.py:52
  87.8 0.8 copy-start.2
  87.8 160.7 %reduce-scatter.5.cloned.1.call-start = ((), (), s32[]{:S(2)}) async-start(), calls=%async_computation.5 | async-start | bytes 4718592 | tf_op jit(solution)/shard_map/reduce_scatter | solution.py:74
  87.9 93.7 %collective-permute-start = (bf16[8,512,512]{1,2,0:T(8,128)(2,1)}, bf16[8,512,512]{1,2,0:T(8,128)(2,1)}, u32[]{:S(2)}, u32[]{:S(2)}) collective-permute-start(bf16[8,512,512]{1,2,0:T(8,128)(2,1)} %all_to_all.5), channel_id=1, source_target_pairs={{0,16},{16,0},{1,17},{17,1},{2,18},{18,2},{3,19},{19,3},{4,20},{20... | collective-permute-start | bytes 12582920 | tf_op jit(solution)/shard_map/ppermute | solution.py:70
  98.4 2.2 slice-start
  169.5 6.0 %collective-permute-start.1 = (bf16[127,512]{1,0:T(8,128)(2,1)S(1)}, bf16[127,512]{1,0:T(8,128)(2,1)S(1)}, u32[]{:S(2)}, u32[]{:S(2)}) collective-permute-start(bf16[127,512]{1,0:T(8,128)(2,1)S(1)} %slice_bitcast_fusion.2), channel_id=1, source_target_pairs={{0,16},{16,32},{32,48},{48,64},{64,80},{80,96},{96,112},{112,128},... | collective-permute-start | bytes 390152 | tf_op jit(solution)/shard_map/ppermute | solution.py:21
  178.6 3.0 %copy-start.3 = (f32[512]{0:T(512)S(1)}, f32[512]{0:T(512)}, u32[]{:S(2)}) copy-start(f32[512]{0:T(512)} %param.8) | copy-start | bytes 6148
  181.6 78.6 %copy-start.1 = (bf16[3,512,512]{2,1,0:T(8,128)(2,1)S(1)}, bf16[3,512,512]{2,1,0:T(8,128)(2,1)}, u32[]{:S(2)}) copy-start(bf16[3,512,512]{2,1,0:T(8,128)(2,1)} %param.6) | copy-start | bytes 4718596
  249.5 8.8 %collective-permute-start.2 = (bf16[256,512]{0,1:T(8,128)(2,1)S(1)}, bf16[256,512]{0,1:T(8,128)(2,1)S(1)}, u32[]{:S(2)}, u32[]{:S(2)}) collective-permute-start(bf16[256,512]{0,1:T(8,128)(2,1)S(1)} %dynamic-slice_bitcast_fusion), channel_id=1, source_target_pairs={{0,1},{1,0},{2,3},{3,2},{4,5},{5,4},{6,7},{7,6},{8,9},{9,8},{10,11... | collective-permute-start | bytes 786440 | tf_op jit(solution)/shard_map/ppermute | solution.py:78
Sparse Core Ops, SparseCore 0:
  18.4 57.5 all-gather.1
  87.9 80.4 reduce-scatter.2
  189.7 58.8 reduce-scatter.4

commit v4 on v3

--- a/solution.py
+++ b/solution.py
@@ -49,17 +49,15 @@
     channels = in_weight.shape[2]
     taps_count = filters.shape[1]
     group_width = channels // filters.shape[0]
-    summed = lax.psum_scatter(
-        jnp.einsum("rf,sfc->rsc", gathered, in_weight, preferred_element_type=jnp.float32).astype(
-            jnp.bfloat16
-        ),
-        SEQ,
-        scatter_dimension=0,
-        tiled=True,
-    ).astype(jnp.float32)
-    query_rows = summed[:, 0].astype(jnp.bfloat16)
-    key_rows = summed[:, 1].astype(jnp.bfloat16)
-    value_rows = summed[:, 2].astype(jnp.bfloat16)
+    kv_part = jnp.einsum(
+        "rf,sfc->rsc", gathered, in_weight[1:], preferred_element_type=jnp.float32
+    ).astype(jnp.bfloat16)
+    kv = lax.psum_scatter(kv_part, SEQ, scatter_dimension=0, tiled=True)
+    q_part = jnp.dot(gathered, in_weight[0], preferred_element_type=jnp.float32).astype(jnp.bfloat16)
+    q_part, kv = lax.optimization_barrier((q_part, kv))
+    query_rows = lax.psum_scatter(q_part, SEQ, scatter_dimension=0, tiled=True)
+    key_rows = kv[:, 0]
+    value_rows = kv[:, 1]
     product = (key_rows.astype(jnp.float32) * value_rows.astype(jnp.float32)).astype(jnp.bfloat16)
     previous = from_behind(product[tok_dev - (taps_count - 1) :], SEQ, 1)
     product_f = product.astype(jnp.float32)
@@ -68,14 +66,15 @@
     conv = conv + skip_gain[None, :] * product_f
     gated = (query_rows.astype(jnp.float32) * conv).astype(jnp.bfloat16)
     w_other = lax.ppermute(w_mine, "core", [(0, 1), (1, 0)])
-    partial_out = jnp.einsum(
-        "tc,jmco->jmto", gated, jnp.stack([w_mine, w_other], axis=1), preferred_element_type=jnp.float32
-    ).astype(jnp.bfloat16)
-    by_z = lax.psum_scatter(partial_out, "z", scatter_dimension=0, tiled=True)[0]
     keep_at = (lax.axis_index("xhi") != lax.axis_index("core")).astype(jnp.int32)
-    keep = lax.dynamic_index_in_dim(by_z, keep_at, 0, keepdims=False)
-    give = lax.dynamic_index_in_dim(by_z, 1 - keep_at, 0, keepdims=False)
+    w_keep = jnp.where(keep_at == 0, w_mine, w_other)
+    w_give = jnp.where(keep_at == 0, w_other, w_mine)
+    give_part = jnp.einsum("tc,jco->jto", gated, w_give, preferred_element_type=jnp.float32)
+    give = lax.psum_scatter(give_part.astype(jnp.bfloat16), "z", scatter_dimension=0, tiled=True)[0]
+    keep_part = jnp.einsum("tc,jco->jto", gated, w_keep, preferred_element_type=jnp.float32)
+    keep_part, give = lax.optimization_barrier((keep_part.astype(jnp.bfloat16), give))
     got = lax.ppermute(give, "xhi", [(0, 1), (1, 0)])
+    keep = lax.psum_scatter(keep_part, "z", scatter_dimension=0, tiled=True)[0]
     return (keep.astype(jnp.float32) + got.astype(jnp.float32)).astype(jnp.bfloat16)
 
 

time: 267 us -> 330 us (1.24)
  waiting for transfers between devices: 135 us -> 186 us
  matrix products: 24.5 us -> 28.4 us
  starting transfers between devices: 5.91 us -> 9.57 us
    reduce_scatter x2 -> x4, waiting for transfers between devices: 122 us -> 176 us  [the longest x1 65.5 us: per_device(): kv = lax.psum_scatter(kv_part, SEQ, scatter_dimension=0, tiled=True)]
    dot_general x2 -> x4, matrix products: 19.7 us -> 25.1 us  [the longest x1 8.91 us: per_device(): jnp.einsum('rf,sfc->rsc', gathered, in_weight[1:], preferred_element_type...]
    ppermute x1, starting transfers between devices: 0.76 us -> 4.6 us  [per_device(): w_other = lax.ppermute(w_mine, 'core', [(0, 1), (1, 0)])]
  transfers between devices with their start and end apart: 6 -> 8, of which waited for: 5 -> 7; matrix products, arithmetic and copies ran while one was open for 9% -> 11% of each run, Pallas kernels for 0% -> 0%
where the time goes in v4:
time: 330 us; the launch traced here: 326 us
  waiting for transfers between devices  186 us (56%)
  blocking collectives  63.7 us (19%)
  matrix products  28.4 us (9%)
  local copies, waits for them, and re-layouts  18.8 us (6%)
  between operations  13.3 us (4%)
  starting transfers between devices  9.57 us (3%)
  other arithmetic  6.71 us (2%)
    reduce_scatter x1, waiting for transfers between devices, per_device(): kv = lax.psum_scatter(kv_part, SEQ, scatter_dimension=0, tiled=True)  65.5 us
    all_to_all x1, blocking collectives, per_device(): w_mine = lax.all_to_all(spread, ('xlo', 'y'), 0, 0, tiled=True)  52.2 us
    reduce_scatter x1, waiting for transfers between devices, per_device(): query_rows = lax.psum_scatter(q_part, SEQ, scatter_dimension=0, tiled=True)  38.1 us
    reduce_scatter x1, waiting for transfers between devices, per_device(): lax.psum_scatter(give_part.astype(jnp.bfloat16), 'z', scatter_dimension=0...  36.4 us
    reduce_scatter x1, waiting for transfers between devices, per_device(): keep = lax.psum_scatter(keep_part, 'z', scatter_dimension=0, tiled=True)[0]  36.2 us
    all_gather x1, blocking collectives, per_device(): lax.all_gather(tokens, 'xhi', axis=0, tiled=True)  11.5 us
    another operation x2, local copies, waits for them, and re-layouts, toeplitz_conv(): jnp.tile(w, (1, taps))[:, :taps * 2 * taps].reshape(groups, taps, 2 * taps)  9.68 us
    dot_general x1, matrix products, per_device(): jnp.einsum('rf,sfc->rsc', gathered, in_weight[1:], preferred_element_type...  8.91 us
  transfers between devices with their start and end apart: 8, of which 7 were waited for; matrix products, arithmetic and copies ran while one was open for 11% of the time, Pallas kernels for 0%

profile of v4, /device:TPU:1, one launch (start us, length us, event | category | flops | bytes accessed | tf_op | source)
XLA Modules:
  0.0 326.5 jit_solution(17706162137151438434)
XLA Ops:
  6.5 0.0 all-gather.2.cloned.1.call-start
  6.5 11.5 %all_gather.6 = bf16[512,512]{1,0:T(8,128)(2,1)} all-gather(bf16[256,512]{1,0:T(8,128)(2,1)} %param.5), channel_id=1, replica_groups=mesh['xlo'=2,'y'=4,'core'=2,'z'=8,'xhi'=2] {'xhi'}, dimensions={0}, use_global_device_ids=true | all-gather | bytes 786432 | tf_op jit(solution)/shard_map/all_gather | solution.py:43
  18.1 0.0 all-gather.2.cloned.1.call-update
  18.1 0.0 reduce-scatter.5.cloned.1.call-start
  18.2 1.3 copy.11
  19.4 0.4 broadcast_in_dim.2
  19.8 0.0 copy-start.3
  19.8 52.2 %all_to_all.5 = bf16[8,512,512]{1,2,0:T(8,128)(2,1)} all-to-all(bf16[8,512,512]{1,2,0:T(8,128)(2,1)S(1)} %broadcast_in_dim.2), channel_id=1, replica_groups=mesh['xlo'=2,'y'=4,'core'=2,'z'=8,'xhi'=2] {'xlo','y'}, dimensions={0} | all-to-all | bytes 8388608 | tf_op jit(solution)/shard_map/all_to_all | solution.py:46
  72.0 3.9 %all-gather.2.cloned.1.call-done = bf16[4096,512]{1,0:T(8,128)(2,1)} async-done(((bf16[512,512]{1,0:T(8,128)(2,1)}), bf16[4096,512]{1,0:T(8,128)(2,1)}) %all-gather.2.cloned.1.call-update) | async-done | bytes 4194320 | tf_op jit(solution)/shard_map/all_gather | solution.py:43
  75.9 0.0 copy-done.3
  75.9 8.9 %convolution_convert_fusion = bf16[4096,2,512]{2,0,1:T(8,128)(2,1)} fusion(bf16[4096,512]{1,0:T(8,128)(2,1)} %all-gather.2.cloned.1.call-done, bf16[3,512,512]{2,1,0:T(8,128)(2,1)S(1)} %copy-done.3), kind=kOutput, calls=%fused_computation | convolution fusion | flops 4299161600 | bytes 13631488 | tf_op jit(solution)/shard_map/rf,sfc->rsc/dot_general | solution.py:52
  84.8 0.0 reduce-scatter.5.cloned.1.call-update
  84.8 0.0 reduce-scatter.7.cloned.1.call-start
  84.9 6.6 %convolution_convert_fusion.1 = bf16[4096,512]{1,0:T(8,128)(2,1)} fusion(bf16[4096,512]{1,0:T(8,128)(2,1)} %all-gather.2.cloned.1.call-done, bf16[3,512,512]{2,1,0:T(8,128)(2,1)S(1)} %copy-done.3), kind=kOutput, calls=%fused_computation.1 | convolution fusion | flops 2149580800 | bytes 8912896 | tf_op jit(solution)/shard_map/dot_general | solution.py:56
  91.4 0.0 copy-start.1
  91.4 65.5 %reduce-scatter.5.cloned.1.call-done = bf16[256,2,512]{2,0,1:T(8,128)(2,1)} async-done(((bf16[4096,2,512]{2,0,1:T(8,128)(2,1)}), bf16[256,2,512]{2,0,1:T(8,128)(2,1)}) %reduce-scatter.5.cloned.1.call-update) | async-done | bytes 524304 | tf_op jit(solution)/shard_map/reduce_scatter | solution.py:55
  156.9 0.0 reduce-scatter.7.cloned.1.call-update
  156.9 0.0 reduce-scatter.9.cloned.1.call-start
  156.9 4.6 %collective-permute-start = (bf16[8,512,512]{1,2,0:T(8,128)(2,1)}, bf16[8,512,512]{1,2,0:T(8,128)(2,1)}, u32[]{:S(2)}, u32[]{:S(2)}) collective-permute-start(bf16[8,512,512]{1,2,0:T(8,128)(2,1)} %all_to_all.5), channel_id=1, source_target_pairs={{0,16},{16,0},{1,17},{17,1},{2,18},{18,2},{3,19},{19,3},{4,20},{20... | collective-permute-start | bytes 12582920 | tf_op jit(solution)/shard_map/ppermute | solution.py:68
  161.5 0.0 copy-done.1
  161.5 0.1 rev.3
  161.6 3.0 tile.4
  164.7 6.6 %tile.10 = f32[32,32896]{1,0:T(8,128)} reshape(f32[32,128,257]{2,1,0:T(8,128)} %tile.4) | data formatting | bytes 8421376 | tf_op jit(solution)/shard_map/tile | solution.py:34
  171.3 0.0 slice-start
  171.3 2.3 slice-done
  173.6 3.2 copy.21
  176.8 0.0 copy-start
  176.8 4.4 %fusion = (bf16[32,128,256]{2,1,0:T(8,128)(2,1)}, bf16[32,128,256]{2,1,0:T(8,128)(2,1)S(1)}) fusion(f32[4,8,128,256]{3,2,1,0:T(8,128)} %copy.21), kind=kLoop, calls=%fused_computation.4 | loop fusion | flops 4194304 | bytes 8388608 | tf_op jit(solution)/shard_map/convert_element_type | solution.py:36
  181.2 0.0 copy-done
  181.2 0.1 multiply_convert_fusion.1
  181.3 2.1 collective-permute-start.1
  183.4 0.1 fusion.32
  183.5 1.7 collective-permute-done.1
  185.2 0.1 pad_slice_fusion
  185.2 0.1 copy.12
  185.4 0.1 slice.42
  185.5 0.1 copy.13
  185.6 0.1 slice.44
  185.7 0.1 copy_dynamic-update-slice_fusion.1
  185.7 0.1 copy_dynamic-update-slice_fusion
  185.8 2.4 fusion.8
  188.2 0.0 copy-start.2
  188.2 0.8 fusion.19
  189.1 0.3 copy.16
  189.4 0.2 copy.17
  189.6 38.1 %reduce-scatter.7.cloned.1.call-done = bf16[256,512]{1,0:T(8,128)(2,1)} async-done(((bf16[4096,512]{1,0:T(8,128)(2,1)}), bf16[256,512]{1,0:T(8,128)(2,1)}) %reduce-scatter.7.cloned.1.call-update) | async-done | bytes 262160 | tf_op jit(solution)/shard_map/reduce_scatter | solution.py:58
  227.7 0.0 copy-done.2
  227.7 1.1 fusion.26
  228.8 0.0 collective-permute-done
  228.8 4.8 %convert_bitcast_fusion = bf16[8,256,512]{1,2,0:T(8,128)(2,1)} fusion(bf16[256,512,1]{1,0,2:T(8,128)(2,1)S(1)} %fusion.26, bf16[8,512,512]{1,2,0:T(8,128)(2,1)} %collective-permute-done, bf16[8,512,512]{1,2,0:T(8,128)(2,1)} %all_to_all.5, pred[]{:T(512)S(6)} %eq.4), kind=kOutput, calls=%fused_computation.16 | convolution fusion | flops 1076887552 | bytes 10747905 | tf_op jit(solution)/shard_map/tc,jco->jto/dot_general | solution.py:72
  233.6 0.0 reduce-scatter.9.cloned.1.call-update
  233.6 0.0 reduce-scatter.11.cloned.1.call-start
  233.7 4.8 %convert_bitcast_fusion.1 = bf16[8,256,512]{1,2,0:T(8,128)(2,1)} fusion(bf16[256,512,1]{1,0,2:T(8,128)(2,1)S(1)} %fusion.26, bf16[8,512,512]{1,2,0:T(8,128)(2,1)} %all_to_all.5, bf16[8,512,512]{1,2,0:T(8,128)(2,1)} %collective-permute-done, pred[]{:T(512)S(6)} %eq.4), kind=kOutput, calls=%fused_computation.17 | convolution fusion | flops 1076887552 | bytes 10747905 | tf_op jit(solution)/shard_map/tc,jco->jto/dot_general | solution.py:74
  238.5 36.4 %reduce-scatter.9.cloned.1.call-done = bf16[1,256,512]{1,2,0:T(8,128)(2,1)} async-done(((bf16[8,256,512]{1,2,0:T(8,128)(2,1)}), bf16[1,256,512]{1,2,0:T(8,128)(2,1)}) %reduce-scatter.9.cloned.1.call-update) | async-done | bytes 262160 | tf_op jit(solution)/shard_map/reduce_scatter | solution.py:73
  274.9 0.0 reduce-scatter.11.cloned.1.call-update
  274.9 2.7 collective-permute-start.2
  277.6 4.3 %collective-permute-done.2 = bf16[256,512]{0,1:T(8,128)(2,1)S(1)} collective-permute-done((bf16[256,512]{0,1:T(8,128)(2,1)}, bf16[256,512]{0,1:T(8,128)(2,1)S(1)}, u32[]{:S(2)}, u32[]{:S(2)}) %collective-permute-start.2) | collective-permute-done | bytes 262176 | tf_op jit(solution)/shard_map/ppermute | solution.py:76
  281.9 36.2 %reduce-scatter.11.cloned.1.call-done = bf16[1,256,512]{1,2,0:T(8,128)(2,1)} async-done(((bf16[8,256,512]{1,2,0:T(8,128)(2,1)}), bf16[1,256,512]{1,2,0:T(8,128)(2,1)}) %reduce-scatter.11.cloned.1.call-update) | async-done | bytes 262160 | tf_op jit(solution)/shard_map/reduce_scatter | solution.py:77
  318.1 1.0 fusion.23
  319.1 0.8 copy.18
  (3 shorter events, 0.1 us)
Async XLA Ops:
  6.5 69.3 %all-gather.2.cloned.1.call-start = ((), (), s32[]{:S(2)}) async-start(), calls=%async_computation.5 | async-start | bytes 4718592 | tf_op jit(solution)/shard_map/all_gather | solution.py:43
  18.1 138.8 %reduce-scatter.5.cloned.1.call-start = ((), (), s32[]{:S(2)}) async-start(), calls=%async_computation.6 | async-start | bytes 8912896 | tf_op jit(solution)/shard_map/reduce_scatter | solution.py:55
  19.8 56.1 %copy-start.3 = (bf16[3,512,512]{2,1,0:T(8,128)(2,1)S(1)}, bf16[3,512,512]{2,1,0:T(8,128)(2,1)}, u32[]{:S(2)}) copy-start(bf16[3,512,512]{2,1,0:T(8,128)(2,1)} %param.6) | copy-start | bytes 4718596
  84.8 142.9 %reduce-scatter.7.cloned.1.call-start = ((), (), s32[]{:S(2)}) async-start(), calls=%async_computation.7 | async-start | bytes 4456448 | tf_op jit(solution)/shard_map/reduce_scatter | solution.py:58
  91.4 70.1 %copy-start.1 = (f32[32,128]{1,0:T(8,128)S(1)}, f32[32,128]{1,0:T(8,128)}, u32[]{:S(2)}) copy-start(f32[32,128]{1,0:T(8,128)} %param.7) | copy-start | bytes 49156
  156.9 118.0 %reduce-scatter.9.cloned.1.call-start = ((), (), s32[]{:S(2)}) async-start(), calls=%async_computation.8 | async-start | bytes 2359296 | tf_op jit(solution)/shard_map/reduce_scatter | solution.py:73
  156.9 71.8 %collective-permute-start = (bf16[8,512,512]{1,2,0:T(8,128)(2,1)}, bf16[8,512,512]{1,2,0:T(8,128)(2,1)}, u32[]{:S(2)}, u32[]{:S(2)}) collective-permute-start(bf16[8,512,512]{1,2,0:T(8,128)(2,1)} %all_to_all.5), channel_id=1, source_target_pairs={{0,16},{16,0},{1,17},{17,1},{2,18},{18,2},{3,19},{19,3},{4,20},{20... | collective-permute-start | bytes 12582920 | tf_op jit(solution)/shard_map/ppermute | solution.py:68
  171.3 2.3 slice-start
  176.8 4.4 %copy-start = (bf16[256,2,512]{2,0,1:T(8,128)(2,1)S(1)}, bf16[256,2,512]{2,0,1:T(8,128)(2,1)}, u32[]{:S(2)}) copy-start(bf16[256,2,512]{2,0,1:T(8,128)(2,1)} %reduce-scatter.5.cloned.1.call-done) | copy-start | bytes 1572868
  181.3 3.9 %collective-permute-start.1 = (bf16[127,512]{1,0:T(8,128)(2,1)S(1)}, bf16[127,512]{1,0:T(8,128)(2,1)S(1)}, u32[]{:S(2)}, u32[]{:S(2)}) collective-permute-start(bf16[127,512]{1,0:T(8,128)(2,1)S(1)} %slice_bitcast_fusion), channel_id=1, source_target_pairs={{0,16},{16,32},{32,48},{48,64},{64,80},{80,96},{96,112},{112,128},... | collective-permute-start | bytes 390152 | tf_op jit(solution)/shard_map/ppermute | solution.py:21
  188.2 39.4 %copy-start.2 = (f32[512]{0:T(512)S(1)}, f32[512]{0:T(512)}, u32[]{:S(2)}) copy-start(f32[512]{0:T(512)} %param.8) | copy-start | bytes 6148
  233.6 84.5 %reduce-scatter.11.cloned.1.call-start = ((), (), s32[]{:S(2)}) async-start(), calls=%async_computation.9 | async-start | bytes 2359296 | tf_op jit(solution)/shard_map/reduce_scatter | solution.py:77
  274.9 7.0 %collective-permute-start.2 = (bf16[256,512]{0,1:T(8,128)(2,1)}, bf16[256,512]{0,1:T(8,128)(2,1)S(1)}, u32[]{:S(2)}, u32[]{:S(2)}) collective-permute-start(bf16[256,512]{0,1:T(8,128)(2,1)} %bitcast.63), channel_id=1, source_target_pairs={{0,1},{1,0},{2,3},{3,2},{4,5},{5,4},{6,7},{7,6},{8,9},{9,8},{10,11... | collective-permute-start | bytes 786440 | tf_op jit(solution)/shard_map/ppermute | solution.py:76
Sparse Core Ops, SparseCore 0:
  18.2 57.5 all-gather.1
  84.9 71.8 reduce-scatter.4
  159.4 68.1 reduce-scatter.6
  233.7 41.1 reduce-scatter.8
  277.3 40.7 reduce-scatter.10

commit v5 on v3

--- a/solution.py
+++ b/solution.py
@@ -34,8 +34,9 @@
     toe = jnp.tile(w, (1, taps))[:, : taps * 2 * taps].reshape(groups, taps, 2 * taps)
     hi = toe.astype(jnp.bfloat16)
     lo = (toe - hi.astype(jnp.float32)).astype(jnp.bfloat16)
-    out = jnp.einsum("gts,isgc->itgc", hi, win, preferred_element_type=jnp.float32)
-    out = out + jnp.einsum("gts,isgc->itgc", lo, win, preferred_element_type=jnp.float32)
+    both = jnp.concatenate([hi, lo], axis=2)
+    twice = jnp.concatenate([win, win], axis=1)
+    out = jnp.einsum("gts,isgc->itgc", both, twice, preferred_element_type=jnp.float32)
     return out.reshape(tok, channels)
 
 

time: 267 us -> 265 us (level)
  transfers between devices with their start and end apart: 6 -> 6, of which waited for: 5 -> 5; matrix products, arithmetic and copies ran while one was open for 9% -> 8% of each run, Pallas kernels for 0% -> 0%
where the time goes in v5:
time: 265 us
  waiting for transfers between devices  135 us (51%)
  blocking collectives  63.7 us (24%)
  matrix products  22.9 us (9%)
  local copies, waits for them, and re-layouts  17.7 us (7%)
  between operations  13.3 us (5%)
  other arithmetic  6.34 us (2%)
  starting transfers between devices  5.91 us (2%)
    reduce_scatter x1, waiting for transfers between devices, per_device(): lax.psum_scatter(jnp.einsum('rf,sfc->rsc', gathered, in_weight, preferred...  63.4 us
    reduce_scatter x1, waiting for transfers between devices, per_device(): lax.psum_scatter(partial_out, 'z', scatter_dimension=0, tiled=True)[0]  59 us
    all_to_all x1, blocking collectives, per_device(): w_mine = lax.all_to_all(spread, ('xlo', 'y'), 0, 0, tiled=True)  52 us
    dot_general x1, matrix products, per_device(): jnp.einsum('rf,sfc->rsc', gathered, in_weight, preferred_element_type=jnp...  11.8 us
    all_gather x1, blocking collectives, per_device(): lax.all_gather(tokens, 'xhi', axis=0, tiled=True)  11.7 us
    another operation x2, local copies, waits for them, and re-layouts, toeplitz_conv(): jnp.tile(w, (1, taps))[:, :taps * 2 * taps].reshape(groups, taps, 2 * taps)  9.67 us
    dot_general x1, matrix products, per_device(): jnp.einsum('tc,jmco->jmto', gated, jnp.stack([w_mine, w_other], axis=1),...  7.94 us
    ppermute x1, waiting for transfers between devices, per_device(): got = lax.ppermute(give, 'xhi', [(0, 1), (1, 0)])  6.04 us
  transfers between devices with their start and end apart: 6, of which 5 were waited for; matrix products, arithmetic and copies ran while one was open for 8% of the time, Pallas kernels for 0%

profile of v5, /device:TPU:1, one launch (start us, length us, event | category | flops | bytes accessed | tf_op | source)
XLA Modules:
  0.0 265.0 jit_solution(11785831794427501597)
XLA Ops:
  6.5 0.0 copy-start
  6.5 0.0 all-gather.2.cloned.1.call-start
  6.5 11.7 %all_gather.6 = bf16[512,512]{1,0:T(8,128)(2,1)} all-gather(bf16[256,512]{1,0:T(8,128)(2,1)} %param.5), channel_id=1, replica_groups=mesh['xlo'=2,'y'=4,'core'=2,'z'=8,'xhi'=2] {'xhi'}, dimensions={0}, use_global_device_ids=true | all-gather | bytes 786432 | tf_op jit(solution)/shard_map/all_gather | solution.py:44
  18.2 0.0 all-gather.2.cloned.1.call-update
  18.3 0.0 reduce-scatter.3.cloned.1.call-start
  18.3 1.3 copy.14
  19.6 0.4 broadcast_in_dim.2
  19.9 52.0 %all_to_all.5 = bf16[8,512,512]{1,2,0:T(8,128)(2,1)} all-to-all(bf16[8,512,512]{1,2,0:T(8,128)(2,1)S(1)} %broadcast_in_dim.2), channel_id=1, replica_groups=mesh['xlo'=2,'y'=4,'core'=2,'z'=8,'xhi'=2] {'xlo','y'}, dimensions={0} | all-to-all | bytes 8388608 | tf_op jit(solution)/shard_map/all_to_all | solution.py:47
  71.9 4.1 %all-gather.2.cloned.1.call-done = bf16[4096,512]{1,0:T(8,128)(2,1)} async-done(((bf16[512,512]{1,0:T(8,128)(2,1)}), bf16[4096,512]{1,0:T(8,128)(2,1)}) %all-gather.2.cloned.1.call-update) | async-done | bytes 4194320 | tf_op jit(solution)/shard_map/all_gather | solution.py:44
  76.0 0.0 copy-done
  76.0 11.8 %convolution_convert_fusion = bf16[4096,3,512]{2,0,1:T(8,128)(2,1)} fusion(bf16[3,512,512]{2,1,0:T(8,128)(2,1)S(1)} %copy-done, bf16[4096,512]{1,0:T(8,128)(2,1)} %all-gather.2.cloned.1.call-done), kind=kOutput, calls=%fused_computation | convolution fusion | flops 6448742400 | bytes 18350080 | tf_op jit(solution)/shard_map/rf,sfc->rsc/dot_general | solution.py:54
  87.8 0.0 copy-start.2
  87.8 0.0 reduce-scatter.3.cloned.1.call-update
  87.8 0.0 reduce-scatter.5.cloned.1.call-start
  87.9 0.8 collective-permute-start
  88.6 0.0 copy-done.2
  88.6 0.1 rev.3
  88.7 3.0 %tile.4 = f32[32,128,257]{2,1,0:T(8,128)} broadcast(f32[32,257]{1,0:T(8,128)S(1)} %pad.5), dimensions={0,2} | broadcast | bytes 4243584 | tf_op jit(solution)/shard_map/tile | solution.py:34
  91.7 6.7 %tile.10 = f32[32,32896]{1,0:T(8,128)} reshape(f32[32,128,257]{2,1,0:T(8,128)} %tile.4) | data formatting | bytes 8421376 | tf_op jit(solution)/shard_map/tile | solution.py:34
  98.4 0.0 slice-start
  98.4 2.2 slice-done
  100.6 1.3 copy.27
  101.9 3.1 %fusion.4 = (bf16[32,128,256]{2,1,0:T(8,128)(2,1)}, bf16[32,128,256]{2,1,0:T(8,128)(2,1)}) fusion(f32[4,8,128,256]{3,2,1,0:T(8,128)S(1)} %copy.27), kind=kLoop, calls=%fused_computation.7 | loop fusion | flops 4194304 | bytes 8388608 | tf_op jit(solution)/shard_map/convert_element_type | solution.py:36
  105.0 63.4 %reduce-scatter.3.cloned.1.call-done = bf16[256,3,512]{2,0,1:T(8,128)(2,1)} async-done(((bf16[4096,3,512]{2,0,1:T(8,128)(2,1)}), bf16[256,3,512]{2,0,1:T(8,128)(2,1)}) %reduce-scatter.3.cloned.1.call-update) | async-done | bytes 786448 | tf_op jit(solution)/shard_map/reduce_scatter | solution.py:53
  168.4 1.1 multiply_convert_fusion
  169.5 2.3 collective-permute-start.1
  171.8 1.1 fusion.28
  172.9 2.6 collective-permute-done.1
  175.5 0.1 pad_maximum_fusion
  175.6 0.1 copy.16
  175.7 0.1 slice.41
  175.9 0.1 copy.17
  176.0 0.1 slice.43
  176.1 0.0 copy-start.3
  176.1 3.1 %fusion.11 = f32[2,128,32,16]{1,3,0,2:T(8,128)S(1)} fusion(bf16[32,128,256]{2,1,0:T(8,128)(2,1)} %get-tuple-element.9, bf16[32,128,256]{2,1,0:T(8,128)(2,1)} %get-tuple-element.10, bf16[2,128,32,16]{1,3,0,2:T(8,128)(2,1)S(1)} %copy.19, bf16[2,128,32,16]{1,3,0,2:T(8,128)(2,1)S(1)} %copy.18), kind=kOutput, calls=%fused_computation.14 | convolution fusion | flops 146800640 | bytes 5242880 | tf_op jit(solution)/shard_map/gts,isgc->itgc/dot_general | solution.py:39
  179.3 0.3 copy.22
  179.6 0.2 copy.23
  179.8 0.0 collective-permute-done
  179.8 0.0 copy-done.3
  179.8 0.0 copy-start.1
  179.8 7.9 %convert_bitcast_fusion = bf16[8,2,256,512]{2,3,1,0:T(8,128)(2,1)} fusion(bf16[8,1,512,512]{2,3,1,0:T(8,128)(2,1)} %bitcast.2, bf16[8,1,512,512]{2,3,1,0:T(8,128)(2,1)} %bitcast.62, f32[256,512]{1,0:T(8,128)S(1)} %copy.23, bf16[256,3,512]{2,0,1:T(8,128)(2,1)} %reduce-scatter.3.cloned.1.call-done, f32[512]{0:T(512)S(1)} %copy-done.3, ...), kind=kOutput, calls=%fused_computation.13 | convolution fusion | flops 2154561536 | bytes 13633536 | tf_op jit(solution)/shard_map/tc,jmco->jmto/dot_general | solution.py:72
  187.8 0.0 reduce-scatter.5.cloned.1.call-update
  187.8 59.0 %reduce-scatter.5.cloned.1.call-done = bf16[1,2,256,512]{2,3,1,0:T(8,128)(2,1)} async-done(((bf16[8,2,256,512]{2,3,1,0:T(8,128)(2,1)}), bf16[1,2,256,512]{2,3,1,0:T(8,128)(2,1)}) %reduce-scatter.5.cloned.1.call-update) | async-done | bytes 524304 | tf_op jit(solution)/shard_map/reduce_scatter | solution.py:75
  246.8 1.0 dynamic-slice_bitcast_fusion
  247.8 2.8 %collective-permute-start.2 = (bf16[256,512]{0,1:T(8,128)(2,1)S(1)}, bf16[256,512]{0,1:T(8,128)(2,1)S(1)}, u32[]{:S(2)}, u32[]{:S(2)}) collective-permute-start(bf16[256,512]{0,1:T(8,128)(2,1)S(1)} %dynamic-slice_bitcast_fusion), channel_id=1, source_target_pairs={{0,1},{1,0},{2,3},{3,2},{4,5},{5,4},{6,7},{7,6},{8,9},{9,8},{10,11... | collective-permute-start | bytes 786440 | tf_op jit(solution)/shard_map/ppermute | solution.py:79
  250.6 6.0 %collective-permute-done.2 = bf16[256,512]{0,1:T(8,128)(2,1)S(1)} collective-permute-done((bf16[256,512]{0,1:T(8,128)(2,1)S(1)}, bf16[256,512]{0,1:T(8,128)(2,1)S(1)}, u32[]{:S(2)}, u32[]{:S(2)}) %collective-permute-start.2) | collective-permute-done | bytes 262176 | tf_op jit(solution)/shard_map/ppermute | solution.py:79
  256.6 1.0 fusion.19
  257.6 0.8 copy.24
  258.5 0.0 copy-done.1
  (5 shorter events, 0.2 us)
Async XLA Ops:
  6.5 69.5 %copy-start = (bf16[3,512,512]{2,1,0:T(8,128)(2,1)S(1)}, bf16[3,512,512]{2,1,0:T(8,128)(2,1)}, u32[]{:S(2)}) copy-start(bf16[3,512,512]{2,1,0:T(8,128)(2,1)} %param.6) | copy-start | bytes 4718596
  6.5 69.5 %all-gather.2.cloned.1.call-start = ((), (), s32[]{:S(2)}) async-start(), calls=%async_computation.3 | async-start | bytes 4718592 | tf_op jit(solution)/shard_map/all_gather | solution.py:44
  18.3 150.1 %reduce-scatter.3.cloned.1.call-start = ((), (), s32[]{:S(2)}) async-start(), calls=%async_computation.4 | async-start | bytes 13369344 | tf_op jit(solution)/shard_map/reduce_scatter | solution.py:53
  87.8 0.8 copy-start.2
  87.8 159.0 %reduce-scatter.5.cloned.1.call-start = ((), (), s32[]{:S(2)}) async-start(), calls=%async_computation.5 | async-start | bytes 4718592 | tf_op jit(solution)/shard_map/reduce_scatter | solution.py:75
  87.9 92.0 %collective-permute-start = (bf16[8,512,512]{1,2,0:T(8,128)(2,1)}, bf16[8,512,512]{1,2,0:T(8,128)(2,1)}, u32[]{:S(2)}, u32[]{:S(2)}) collective-permute-start(bf16[8,512,512]{1,2,0:T(8,128)(2,1)} %all_to_all.5), channel_id=1, source_target_pairs={{0,16},{16,0},{1,17},{17,1},{2,18},{18,2},{3,19},{19,3},{4,20},{20... | collective-permute-start | bytes 12582920 | tf_op jit(solution)/shard_map/ppermute | solution.py:71
  98.4 2.2 slice-start
  169.5 6.0 %collective-permute-start.1 = (bf16[127,512]{1,0:T(8,128)(2,1)S(1)}, bf16[127,512]{1,0:T(8,128)(2,1)S(1)}, u32[]{:S(2)}, u32[]{:S(2)}) collective-permute-start(bf16[127,512]{1,0:T(8,128)(2,1)S(1)} %slice_bitcast_fusion.2), channel_id=1, source_target_pairs={{0,16},{16,32},{32,48},{48,64},{64,80},{80,96},{96,112},{112,128},... | collective-permute-start | bytes 390152 | tf_op jit(solution)/shard_map/ppermute | solution.py:21
  176.1 3.7 %copy-start.3 = (f32[512]{0:T(512)S(1)}, f32[512]{0:T(512)}, u32[]{:S(2)}) copy-start(f32[512]{0:T(512)} %param.8) | copy-start | bytes 6148
  179.8 78.6 %copy-start.1 = (bf16[3,512,512]{2,1,0:T(8,128)(2,1)S(1)}, bf16[3,512,512]{2,1,0:T(8,128)(2,1)}, u32[]{:S(2)}) copy-start(bf16[3,512,512]{2,1,0:T(8,128)(2,1)} %param.6) | copy-start | bytes 4718596
  247.8 8.8 %collective-permute-start.2 = (bf16[256,512]{0,1:T(8,128)(2,1)S(1)}, bf16[256,512]{0,1:T(8,128)(2,1)S(1)}, u32[]{:S(2)}, u32[]{:S(2)}) collective-permute-start(bf16[256,512]{0,1:T(8,128)(2,1)S(1)} %dynamic-slice_bitcast_fusion), channel_id=1, source_target_pairs={{0,1},{1,0},{2,3},{3,2},{4,5},{5,4},{6,7},{7,6},{8,9},{9,8},{10,11... | collective-permute-start | bytes 786440 | tf_op jit(solution)/shard_map/ppermute | solution.py:79
Sparse Core Ops, SparseCore 0:
  18.4 57.5 all-gather.1
  87.9 80.4 reduce-scatter.2
  187.9 58.8 reduce-scatter.4

commit v6 on v5

--- a/solution.py
+++ b/solution.py
@@ -1,6 +1,8 @@
 import jax
 import jax.numpy as jnp
 from jax import lax
+from jax.experimental import pallas as pl
+from jax.experimental.pallas import tpu as pltpu
 from jax.sharding import Mesh, PartitionSpec as P
 
 
@@ -40,6 +42,31 @@
     return out.reshape(tok, channels)
 
 
+def out_proj_kernel(g_ref, wm_ref, wo_ref, out_ref):
+    g = g_ref[...]
+    for jj in range(wm_ref.shape[0]):
+        out_ref[jj, 0] = jnp.dot(g, wm_ref[jj], preferred_element_type=jnp.float32).astype(out_ref.dtype)
+        out_ref[jj, 1] = jnp.dot(g, wo_ref[jj], preferred_element_type=jnp.float32).astype(out_ref.dtype)
+
+
+def out_proj(gated, w_mine, w_other, per_step=2):
+    rows, depth = gated.shape
+    blocks, _, width = w_mine.shape
+    w_spec = pl.BlockSpec((per_step, depth, width), lambda i: (i, 0, 0))
+    return pl.pallas_call(
+        out_proj_kernel,
+        out_shape=jax.ShapeDtypeStruct((blocks, 2, rows, width), jnp.bfloat16),
+        grid=(blocks // per_step,),
+        in_specs=[pl.BlockSpec((rows, depth), lambda i: (0, 0)), w_spec, w_spec],
+        out_specs=pl.BlockSpec((per_step, 2, rows, width), lambda i: (i, 0, 0, 0)),
+        cost_estimate=pl.CostEstimate(
+            flops=2 * rows * depth * width * blocks * 2,
+            bytes_accessed=2 * (rows * depth + 2 * blocks * depth * width + 2 * blocks * rows * width),
+            transcendentals=0,
+        ),
+    )(gated, w_mine, w_other)
+
+
 def per_device(tokens, in_weight, filters, skip_gain, out_weight):
     gathered = lax.all_gather(lax.all_gather(tokens, "xhi", axis=0, tiled=True), "z", axis=0, tiled=True)
     chips = axis_size(("xlo", "y"))
@@ -69,9 +96,7 @@
     conv = conv + skip_gain[None, :] * product_f
     gated = (query_rows.astype(jnp.float32) * conv).astype(jnp.bfloat16)
     w_other = lax.ppermute(w_mine, "core", [(0, 1), (1, 0)])
-    partial_out = jnp.einsum(
-        "tc,jmco->jmto", gated, jnp.stack([w_mine, w_other], axis=1), preferred_element_type=jnp.float32
-    ).astype(jnp.bfloat16)
+    partial_out = out_proj(gated, w_mine, w_other)
     by_z = lax.psum_scatter(partial_out, "z", scatter_dimension=0, tiled=True)[0]
     keep_at = (lax.axis_index("xhi") != lax.axis_index("core")).astype(jnp.int32)
     keep = lax.dynamic_index_in_dim(by_z, keep_at, 0, keepdims=False)

time: 265 us -> 265 us (level)
  matrix products: 22.9 us -> 15 us
  Pallas kernels: 0 us -> 7.04 us
    dot_general x1 -> x0, matrix products: 7.94 us -> none  [per_device(): jnp.einsum('tc,jmco->jmto', gated, jnp.stack([w_mine, w_other], axis=1),...]
    pallas_call x0 -> x1, Pallas kernels: none -> 7.04 us  [out_proj(): pl.pallas_call(out_proj_kernel, out_shape=jax.ShapeDtypeStruct((blocks, 2...]
  transfers between devices with their start and end apart: 6 -> 6, of which waited for: 5 -> 5; matrix products, arithmetic and copies ran while one was open for 8% -> 9% of each run, Pallas kernels for 0% -> 0%
where the time goes in v6:
time: 265 us
  waiting for transfers between devices  136 us (51%)
  blocking collectives  63.7 us (24%)
  local copies, waits for them, and re-layouts  16.7 us (6%)
  matrix products  15 us (6%)
  between operations  13.3 us (5%)
  other arithmetic  7.89 us (3%)
  Pallas kernels  7.04 us (3%)
  starting transfers between devices  5.75 us (2%)
    reduce_scatter x1, waiting for transfers between devices, per_device(): lax.psum_scatter(jnp.einsum('rf,sfc->rsc', gathered, in_weight, preferred...  63.5 us
    reduce_scatter x1, waiting for transfers between devices, per_device(): lax.psum_scatter(partial_out, 'z', scatter_dimension=0, tiled=True)[0]  59 us
    all_to_all x1, blocking collectives, per_device(): w_mine = lax.all_to_all(spread, ('xlo', 'y'), 0, 0, tiled=True)  52 us
    dot_general x1, matrix products, per_device(): jnp.einsum('rf,sfc->rsc', gathered, in_weight, preferred_element_type=jnp...  11.8 us
    all_gather x1, blocking collectives, per_device(): lax.all_gather(tokens, 'xhi', axis=0, tiled=True)  11.7 us
    another operation x2, local copies, waits for them, and re-layouts, toeplitz_conv(): jnp.tile(w, (1, taps))[:, :taps * 2 * taps].reshape(groups, taps, 2 * taps)  9.67 us
    pallas_call x1, Pallas kernels, out_proj(): pl.pallas_call(out_proj_kernel, out_shape=jax.ShapeDtypeStruct((blocks, 2...  7.04 us
    ppermute x1, waiting for transfers between devices, per_device(): got = lax.ppermute(give, 'xhi', [(0, 1), (1, 0)])  6.02 us
  transfers between devices with their start and end apart: 6, of which 5 were waited for; matrix products, arithmetic and copies ran while one was open for 9% of the time, Pallas kernels for 0%

profile of v6, /device:TPU:1, one launch (start us, length us, event | category | flops | bytes accessed | tf_op | source)
XLA Modules:
  0.0 264.9 jit_solution(8783883643555363252)
XLA Ops:
  6.5 0.0 copy-start
  6.5 0.0 all-gather.2.cloned.1.call-start
  6.5 11.7 %all_gather.6 = bf16[512,512]{1,0:T(8,128)(2,1)} all-gather(bf16[256,512]{1,0:T(8,128)(2,1)} %param.5), channel_id=1, replica_groups=mesh['xlo'=2,'y'=4,'core'=2,'z'=8,'xhi'=2] {'xhi'}, dimensions={0}, use_global_device_ids=true | all-gather | bytes 786432 | tf_op jit(solution)/shard_map/all_gather | solution.py:71
  18.2 0.0 all-gather.2.cloned.1.call-update
  18.3 0.0 reduce-scatter.3.cloned.1.call-start
  18.3 1.4 broadcast_in_dim.2
  19.7 52.0 %all_to_all.5.wm_ref = bf16[8,512,512]{2,1,0:T(8,128)(2,1)} all-to-all(bf16[8,512,512]{2,1,0:T(8,128)(2,1)S(1)} %broadcast_in_dim.2), channel_id=1, replica_groups=mesh['xlo'=2,'y'=4,'core'=2,'z'=8,'xhi'=2] {'xlo','y'}, dimensions={0} | all-to-all | bytes 8388608 | tf_op jit(solution)/shard_map/all_to_all | solution.py:74
  71.7 4.3 %all-gather.2.cloned.1.call-done = bf16[4096,512]{1,0:T(8,128)(2,1)} async-done(((bf16[512,512]{1,0:T(8,128)(2,1)}), bf16[4096,512]{1,0:T(8,128)(2,1)}) %all-gather.2.cloned.1.call-update) | async-done | bytes 4194320 | tf_op jit(solution)/shard_map/all_gather | solution.py:71
  76.0 0.0 copy-done
  76.0 11.8 %convolution_convert_fusion = bf16[4096,3,512]{2,0,1:T(8,128)(2,1)} fusion(bf16[3,512,512]{2,1,0:T(8,128)(2,1)S(1)} %copy-done, bf16[4096,512]{1,0:T(8,128)(2,1)} %all-gather.2.cloned.1.call-done), kind=kOutput, calls=%fused_computation | convolution fusion | flops 6448742400 | bytes 18350080 | tf_op jit(solution)/shard_map/rf,sfc->rsc/dot_general | solution.py:81
  87.8 0.0 copy-start.2
  87.8 0.0 reduce-scatter.3.cloned.1.call-update
  87.8 0.0 reduce-scatter.5.cloned.1.call-start
  87.9 0.8 collective-permute-start.1
  88.6 0.0 copy-done.2
  88.6 0.1 rev.3
  88.7 3.0 %tile.4 = f32[32,128,257]{2,1,0:T(8,128)} broadcast(f32[32,257]{1,0:T(8,128)S(1)} %pad.5), dimensions={0,2} | broadcast | bytes 4243584 | tf_op jit(solution)/shard_map/tile | solution.py:36
  91.7 6.7 %tile.10 = f32[32,32896]{1,0:T(8,128)} reshape(f32[32,128,257]{2,1,0:T(8,128)} %tile.4) | data formatting | bytes 8421376 | tf_op jit(solution)/shard_map/tile | solution.py:36
  98.4 0.0 slice-start
  98.4 2.2 slice-done
  100.6 1.3 copy.20
  101.9 3.1 %fusion = (bf16[32,128,256]{2,1,0:T(8,128)(2,1)}, bf16[32,128,256]{2,1,0:T(8,128)(2,1)}) fusion(f32[4,8,128,256]{3,2,1,0:T(8,128)S(1)} %copy.20), kind=kLoop, calls=%fused_computation.3 | loop fusion | flops 4194304 | bytes 8388608 | tf_op jit(solution)/shard_map/convert_element_type | solution.py:38
  105.0 63.5 %reduce-scatter.3.cloned.1.call-done = bf16[256,3,512]{2,0,1:T(8,128)(2,1)} async-done(((bf16[4096,3,512]{2,0,1:T(8,128)(2,1)}), bf16[256,3,512]{2,0,1:T(8,128)(2,1)}) %reduce-scatter.3.cloned.1.call-update) | async-done | bytes 786448 | tf_op jit(solution)/shard_map/reduce_scatter | solution.py:80
  168.4 1.1 multiply_convert_fusion
  169.6 2.1 collective-permute-start
  171.7 1.1 fusion.17
  172.8 2.8 %collective-permute-done = bf16[127,512]{1,0:T(8,128)(2,1)S(1)} collective-permute-done((bf16[127,512]{1,0:T(8,128)(2,1)S(1)}, bf16[127,512]{1,0:T(8,128)(2,1)S(1)}, u32[]{:S(2)}, u32[]{:S(2)}) %collective-permute-start) | collective-permute-done | bytes 130080 | tf_op jit(solution)/shard_map/ppermute | solution.py:23
  175.6 0.1 pad_maximum_fusion
  175.6 0.1 copy.11
  175.8 0.1 slice.41
  175.9 0.1 copy.12
  176.0 0.1 slice.43
  176.2 0.0 copy-start.1
  176.2 0.0 copy-start.3
  176.2 3.2 %fusion.5 = f32[2,128,32,16]{1,3,0,2:T(8,128)S(1)} fusion(bf16[32,128,256]{2,1,0:T(8,128)(2,1)} %get-tuple-element.9, bf16[32,128,256]{2,1,0:T(8,128)(2,1)} %get-tuple-element.10, bf16[2,128,32,16]{1,3,0,2:T(8,128)(2,1)S(1)} %copy.14, bf16[2,128,32,16]{1,3,0,2:T(8,128)(2,1)S(1)} %copy.13), kind=kOutput, calls=%fused_computation.9 | convolution fusion | flops 146800640 | bytes 5242880 | tf_op jit(solution)/shard_map/gts,isgc->itgc/dot_general | solution.py:41
  179.4 0.3 copy.17
  179.7 0.2 copy.18
  179.9 0.0 copy-done.1
  179.9 0.0 copy-done.3
  179.9 0.8 fusion.14.g_ref
  180.8 0.0 collective-permute-done.1.wo_ref
  180.8 7.0 %shard_map.55 = bf16[8,2,256,512]{3,2,1,0:T(8,128)(2,1)} custom-call(bf16[256,512]{1,0:T(8,128)(2,1)} %fusion.14.g_ref, bf16[8,512,512]{2,1,0:T(8,128)(2,1)} %all_to_all.5.wm_ref, bf16[8,512,512]{2,1,0:T(8,128)(2,1)} %collective-permute-done.1.wo_ref), custom_call_target="tpu_custom_call" | custom-call | flops 2147483648 | bytes 12845056 | tf_op jit(solution)/shard_map/pallas_call | solution.py:56
  187.8 0.0 reduce-scatter.5.cloned.1.call-update
  187.9 59.0 %reduce-scatter.5.cloned.1.call-done = bf16[1,2,256,512]{3,2,1,0:T(8,128)(2,1)} async-done(((bf16[8,2,256,512]{3,2,1,0:T(8,128)(2,1)}), bf16[1,2,256,512]{3,2,1,0:T(8,128)(2,1)}) %reduce-scatter.5.cloned.1.call-update) | async-done | bytes 524304 | tf_op jit(solution)/shard_map/reduce_scatter | solution.py:100
  246.9 1.0 dynamic-slice_bitcast_fusion
  247.8 2.8 %collective-permute-start.2 = (bf16[256,512]{1,0:T(8,128)(2,1)S(1)}, bf16[256,512]{1,0:T(8,128)(2,1)S(1)}, u32[]{:S(2)}, u32[]{:S(2)}) collective-permute-start(bf16[256,512]{1,0:T(8,128)(2,1)S(1)} %dynamic-slice_bitcast_fusion), channel_id=1, source_target_pairs={{0,1},{1,0},{2,3},{3,2},{4,5},{5,4},{6,7},{7,6},{8,9},{9,8},{10,11... | collective-permute-start | bytes 786440 | tf_op jit(solution)/shard_map/ppermute | solution.py:104
  250.6 6.0 %collective-permute-done.2 = bf16[256,512]{1,0:T(8,128)(2,1)S(1)} collective-permute-done((bf16[256,512]{1,0:T(8,128)(2,1)S(1)}, bf16[256,512]{1,0:T(8,128)(2,1)S(1)}, u32[]{:S(2)}, u32[]{:S(2)}) %collective-permute-start.2) | collective-permute-done | bytes 262176 | tf_op jit(solution)/shard_map/ppermute | solution.py:104
  256.7 1.7 fusion.13
  (5 shorter events, 0.2 us)
Async XLA Ops:
  6.5 69.5 %copy-start = (bf16[3,512,512]{2,1,0:T(8,128)(2,1)S(1)}, bf16[3,512,512]{2,1,0:T(8,128)(2,1)}, u32[]{:S(2)}) copy-start(bf16[3,512,512]{2,1,0:T(8,128)(2,1)} %param.6) | copy-start | bytes 4718596
  6.5 69.5 %all-gather.2.cloned.1.call-start = ((), (), s32[]{:S(2)}) async-start(), calls=%async_computation.3 | async-start | bytes 4718592 | tf_op jit(solution)/shard_map/all_gather | solution.py:71
  18.3 150.2 %reduce-scatter.3.cloned.1.call-start = ((), (), s32[]{:S(2)}) async-start(), calls=%async_computation.4 | async-start | bytes 13369344 | tf_op jit(solution)/shard_map/reduce_scatter | solution.py:80
  87.8 0.8 copy-start.2
  87.8 159.1 %reduce-scatter.5.cloned.1.call-start = ((), (), s32[]{:S(2)}) async-start(), calls=%async_computation.5 | async-start | bytes 4718592 | tf_op jit(solution)/shard_map/reduce_scatter | solution.py:100
  87.9 92.9 %collective-permute-start.1 = (bf16[8,512,512]{2,1,0:T(8,128)(2,1)}, bf16[8,512,512]{2,1,0:T(8,128)(2,1)}, u32[]{:S(2)}, u32[]{:S(2)}) collective-permute-start(bf16[8,512,512]{2,1,0:T(8,128)(2,1)} %all_to_all.5.wm_ref), channel_id=1, source_target_pairs={{0,16},{16,0},{1,17},{17,1},{2,18},{18,2},{3,19},{19,3},{4,20},{20... | collective-permute-start | bytes 12582920 | tf_op jit(solution)/shard_map/ppermute | solution.py:98
  98.4 2.2 slice-start
  169.6 6.0 %collective-permute-start = (bf16[127,512]{1,0:T(8,128)(2,1)S(1)}, bf16[127,512]{1,0:T(8,128)(2,1)S(1)}, u32[]{:S(2)}, u32[]{:S(2)}) collective-permute-start(bf16[127,512]{1,0:T(8,128)(2,1)S(1)} %slice_bitcast_fusion.1), channel_id=1, source_target_pairs={{0,16},{16,32},{32,48},{48,64},{64,80},{80,96},{96,112},{112,128},... | collective-permute-start | bytes 390152 | tf_op jit(solution)/shard_map/ppermute | solution.py:23
  176.2 3.8 %copy-start.1 = (bf16[256,3,512]{2,0,1:T(8,128)(2,1)S(1)}, bf16[256,3,512]{2,0,1:T(8,128)(2,1)}, u32[]{:S(2)}) copy-start(bf16[256,3,512]{2,0,1:T(8,128)(2,1)} %reduce-scatter.3.cloned.1.call-done) | copy-start | bytes 2359300
  176.2 3.8 %copy-start.3 = (f32[512]{0:T(512)S(1)}, f32[512]{0:T(512)}, u32[]{:S(2)}) copy-start(f32[512]{0:T(512)} %param.8) | copy-start | bytes 6148
  247.8 8.8 %collective-permute-start.2 = (bf16[256,512]{1,0:T(8,128)(2,1)S(1)}, bf16[256,512]{1,0:T(8,128)(2,1)S(1)}, u32[]{:S(2)}, u32[]{:S(2)}) collective-permute-start(bf16[256,512]{1,0:T(8,128)(2,1)S(1)} %dynamic-slice_bitcast_fusion), channel_id=1, source_target_pairs={{0,1},{1,0},{2,3},{3,2},{4,5},{5,4},{6,7},{7,6},{8,9},{9,8},{10,11... | collective-permute-start | bytes 786440 | tf_op jit(solution)/shard_map/ppermute | solution.py:104
Sparse Core Ops, SparseCore 0:
  18.4 57.5 all-gather.1
  87.9 80.4 reduce-scatter.2
  188.0 58.8 reduce-scatter.4

commit v7 on v5

--- a/solution.py
+++ b/solution.py
@@ -1,6 +1,8 @@
 import jax
 import jax.numpy as jnp
 from jax import lax
+from jax.experimental import pallas as pl
+from jax.experimental.pallas import tpu as pltpu
 from jax.sharding import Mesh, PartitionSpec as P
 
 
@@ -40,6 +42,34 @@
     return out.reshape(tok, channels)
 
 
+def out_proj_kernel(gt_ref, wm_ref, wo_ref, out_ref):
+    gt = gt_ref[...]
+    step, width, depth = wm_ref.shape
+    for m, w_ref in enumerate((wm_ref, wo_ref)):
+        res = jnp.dot(w_ref[...].reshape(step * width, depth), gt, preferred_element_type=jnp.float32)
+        res = res.astype(out_ref.dtype).reshape(step, width, gt.shape[1])
+        for jj in range(step):
+            out_ref[jj, m] = res[jj]
+
+
+def out_proj(gated_t, wt_mine, wt_other, per_step=4):
+    depth, rows = gated_t.shape
+    blocks, width, _ = wt_mine.shape
+    w_spec = pl.BlockSpec((per_step, width, depth), lambda i: (i, 0, 0))
+    return pl.pallas_call(
+        out_proj_kernel,
+        out_shape=jax.ShapeDtypeStruct((blocks, 2, width, rows), jnp.bfloat16),
+        grid=(blocks // per_step,),
+        in_specs=[pl.BlockSpec((depth, rows), lambda i: (0, 0)), w_spec, w_spec],
+        out_specs=pl.BlockSpec((per_step, 2, width, rows), lambda i: (i, 0, 0, 0)),
+        cost_estimate=pl.CostEstimate(
+            flops=2 * rows * depth * width * blocks * 2,
+            bytes_accessed=2 * (rows * depth + 2 * blocks * depth * width + 2 * blocks * rows * width),
+            transcendentals=0,
+        ),
+    )(gated_t, wt_mine, wt_other)
+
+
 def per_device(tokens, in_weight, filters, skip_gain, out_weight):
     gathered = lax.all_gather(lax.all_gather(tokens, "xhi", axis=0, tiled=True), "z", axis=0, tiled=True)
     chips = axis_size(("xlo", "y"))
@@ -69,15 +99,13 @@
     conv = conv + skip_gain[None, :] * product_f
     gated = (query_rows.astype(jnp.float32) * conv).astype(jnp.bfloat16)
     w_other = lax.ppermute(w_mine, "core", [(0, 1), (1, 0)])
-    partial_out = jnp.einsum(
-        "tc,jmco->jmto", gated, jnp.stack([w_mine, w_other], axis=1), preferred_element_type=jnp.float32
-    ).astype(jnp.bfloat16)
+    partial_out = out_proj(gated.T, jnp.swapaxes(w_mine, 1, 2), jnp.swapaxes(w_other, 1, 2))
     by_z = lax.psum_scatter(partial_out, "z", scatter_dimension=0, tiled=True)[0]
     keep_at = (lax.axis_index("xhi") != lax.axis_index("core")).astype(jnp.int32)
     keep = lax.dynamic_index_in_dim(by_z, keep_at, 0, keepdims=False)
     give = lax.dynamic_index_in_dim(by_z, 1 - keep_at, 0, keepdims=False)
     got = lax.ppermute(give, "xhi", [(0, 1), (1, 0)])
-    return (keep.astype(jnp.float32) + got.astype(jnp.float32)).astype(jnp.bfloat16)
+    return (keep.astype(jnp.float32) + got.astype(jnp.float32)).astype(jnp.bfloat16).T
 
 
 def solution(mesh):

time: 265 us -> 264 us (level)
  matrix products: 22.9 us -> 15 us
  Pallas kernels: 0 us -> 6.13 us
    dot_general x1 -> x0, matrix products: 7.94 us -> none  [per_device(): jnp.einsum('tc,jmco->jmto', gated, jnp.stack([w_mine, w_other], axis=1),...]
    pallas_call x0 -> x1, Pallas kernels: none -> 6.13 us  [out_proj(): pl.pallas_call(out_proj_kernel, out_shape=jax.ShapeDtypeStruct((blocks, 2...]
  transfers between devices with their start and end apart: 6 -> 6, of which waited for: 5 -> 5; matrix products, arithmetic and copies ran while one was open for 8% -> 9% of each run, Pallas kernels for 0% -> 0%
where the time goes in v7:
time: 264 us
  waiting for transfers between devices  135 us (51%)
  blocking collectives  63.7 us (24%)
  local copies, waits for them, and re-layouts  17.3 us (7%)
  matrix products  15 us (6%)
  between operations  13.2 us (5%)
  other arithmetic  7.36 us (3%)
  Pallas kernels  6.13 us (2%)
  starting transfers between devices  5.71 us (2%)
    reduce_scatter x1, waiting for transfers between devices, per_device(): lax.psum_scatter(jnp.einsum('rf,sfc->rsc', gathered, in_weight, preferred...  63.4 us
    reduce_scatter x1, waiting for transfers between devices, per_device(): lax.psum_scatter(partial_out, 'z', scatter_dimension=0, tiled=True)[0]  59 us
    all_to_all x1, blocking collectives, per_device(): w_mine = lax.all_to_all(spread, ('xlo', 'y'), 0, 0, tiled=True)  52 us
    dot_general x1, matrix products, per_device(): jnp.einsum('rf,sfc->rsc', gathered, in_weight, preferred_element_type=jnp...  11.8 us
    all_gather x1, blocking collectives, per_device(): lax.all_gather(tokens, 'xhi', axis=0, tiled=True)  11.7 us
    another operation x2, local copies, waits for them, and re-layouts, toeplitz_conv(): jnp.tile(w, (1, taps))[:, :taps * 2 * taps].reshape(groups, taps, 2 * taps)  9.67 us
    pallas_call x1, Pallas kernels, out_proj(): pl.pallas_call(out_proj_kernel, out_shape=jax.ShapeDtypeStruct((blocks, 2...  6.13 us
    ppermute x1, waiting for transfers between devices, per_device(): got = lax.ppermute(give, 'xhi', [(0, 1), (1, 0)])  6.03 us
  transfers between devices with their start and end apart: 6, of which 5 were waited for; matrix products, arithmetic and copies ran while one was open for 9% of the time, Pallas kernels for 0%

profile of v7, /device:TPU:1, one launch (start us, length us, event | category | flops | bytes accessed | tf_op | source)
XLA Modules:
  0.0 263.8 jit_solution(384639974749320805)
XLA Ops:
  6.5 0.0 copy-start
  6.5 0.0 all-gather.2.cloned.1.call-start
  6.5 11.7 %all_gather.6 = bf16[512,512]{1,0:T(8,128)(2,1)} all-gather(bf16[256,512]{1,0:T(8,128)(2,1)} %param.5), channel_id=1, replica_groups=mesh['xlo'=2,'y'=4,'core'=2,'z'=8,'xhi'=2] {'xhi'}, dimensions={0}, use_global_device_ids=true | all-gather | bytes 786432 | tf_op jit(solution)/shard_map/all_gather | solution.py:74
  18.2 0.0 all-gather.2.cloned.1.call-update
  18.3 0.0 reduce-scatter.3.cloned.1.call-start
  18.3 1.3 copy.14
  19.6 0.4 broadcast_in_dim.2
  19.9 52.0 %all_to_all.5 = bf16[8,512,512]{1,2,0:T(8,128)(2,1)} all-to-all(bf16[8,512,512]{1,2,0:T(8,128)(2,1)S(1)} %broadcast_in_dim.2), channel_id=1, replica_groups=mesh['xlo'=2,'y'=4,'core'=2,'z'=8,'xhi'=2] {'xlo','y'}, dimensions={0} | all-to-all | bytes 8388608 | tf_op jit(solution)/shard_map/all_to_all | solution.py:77
  71.9 4.1 %all-gather.2.cloned.1.call-done = bf16[4096,512]{1,0:T(8,128)(2,1)} async-done(((bf16[512,512]{1,0:T(8,128)(2,1)}), bf16[4096,512]{1,0:T(8,128)(2,1)}) %all-gather.2.cloned.1.call-update) | async-done | bytes 4194320 | tf_op jit(solution)/shard_map/all_gather | solution.py:74
  76.0 0.0 copy-done
  76.0 11.8 %convolution_convert_fusion = bf16[4096,3,512]{0,2,1:T(8,128)(2,1)} fusion(bf16[3,512,512]{2,1,0:T(8,128)(2,1)S(1)} %copy-done, bf16[4096,512]{1,0:T(8,128)(2,1)} %all-gather.2.cloned.1.call-done), kind=kOutput, calls=%fused_computation | convolution fusion | flops 6448742400 | bytes 18350080 | tf_op jit(solution)/shard_map/rf,sfc->rsc/dot_general | solution.py:84
  87.8 0.0 copy-start.2
  87.8 0.0 reduce-scatter.3.cloned.1.call-update
  87.9 0.0 reduce-scatter.5.cloned.1.call-start
  87.9 0.8 collective-permute-start.1
  88.7 0.0 copy-done.2
  88.7 0.1 rev.3
  88.8 3.0 %tile.4 = f32[32,128,257]{2,1,0:T(8,128)} broadcast(f32[32,257]{1,0:T(8,128)S(1)} %pad.5), dimensions={0,2} | broadcast | bytes 4243584 | tf_op jit(solution)/shard_map/tile | solution.py:36
  91.7 6.7 %tile.10 = f32[32,32896]{1,0:T(8,128)} reshape(f32[32,128,257]{2,1,0:T(8,128)} %tile.4) | data formatting | bytes 8421376 | tf_op jit(solution)/shard_map/tile | solution.py:36
  98.4 0.0 slice-start
  98.4 2.2 slice-done
  100.7 1.3 copy.24
  101.9 3.1 %fusion = (bf16[32,128,256]{2,1,0:T(8,128)(2,1)}, bf16[32,128,256]{2,1,0:T(8,128)(2,1)}) fusion(f32[4,8,128,256]{3,2,1,0:T(8,128)S(1)} %copy.24), kind=kLoop, calls=%fused_computation.3 | loop fusion | flops 4194304 | bytes 8388608 | tf_op jit(solution)/shard_map/convert_element_type | solution.py:38
  105.0 63.4 %reduce-scatter.3.cloned.1.call-done = bf16[256,3,512]{0,2,1:T(8,128)(2,1)} async-done(((bf16[4096,3,512]{0,2,1:T(8,128)(2,1)}), bf16[256,3,512]{0,2,1:T(8,128)(2,1)}) %reduce-scatter.3.cloned.1.call-update) | async-done | bytes 786448 | tf_op jit(solution)/shard_map/reduce_scatter | solution.py:83
  168.4 1.1 multiply_convert_fusion
  169.5 0.1 slice_bitcast_fusion.1
  169.6 2.1 collective-permute-start
  171.7 1.1 fusion.20
  172.8 2.8 %collective-permute-done = bf16[127,512]{0,1:T(8,128)(2,1)S(1)} collective-permute-done((bf16[127,512]{0,1:T(8,128)(2,1)S(1)}, bf16[127,512]{0,1:T(8,128)(2,1)S(1)}, u32[]{:S(2)}, u32[]{:S(2)}) %collective-permute-start) | collective-permute-done | bytes 130080 | tf_op jit(solution)/shard_map/ppermute | solution.py:23
  175.6 0.2 pad_maximum_fusion
  175.8 0.1 slice.41
  176.0 0.1 slice.43
  176.1 0.0 copy-start.1
  176.1 0.0 copy-start.3
  176.1 3.2 %fusion.5 = f32[2,128,32,16]{1,3,0,2:T(8,128)S(1)} fusion(bf16[32,128,256]{2,1,0:T(8,128)(2,1)} %get-tuple-element.9, bf16[32,128,256]{2,1,0:T(8,128)(2,1)} %get-tuple-element.10, bf16[2,128,32,16]{1,3,0,2:T(8,128)(2,1)S(1)} %copy.17, bf16[2,128,32,16]{1,3,0,2:T(8,128)(2,1)S(1)} %copy.16), kind=kOutput, calls=%fused_computation.9 | convolution fusion | flops 146800640 | bytes 5242880 | tf_op jit(solution)/shard_map/gts,isgc->itgc/dot_general | solution.py:41
  179.3 0.3 copy.20
  179.6 0.0 copy-done.1
  179.6 0.0 copy-done.3
  179.6 0.9 fusion.17.gt_ref
  180.5 0.0 collective-permute-done.1
  180.5 6.1 %shard_map.55 = bf16[8,2,512,256]{3,2,1,0:T(8,128)(2,1)} custom-call(bf16[512,256]{1,0:T(8,128)(2,1)} %fusion.17.gt_ref, bf16[8,512,512]{2,1,0:T(8,128)(2,1)} %bitcast.58, bf16[8,512,512]{2,1,0:T(8,128)(2,1)} %bitcast.9.wo_ref), custom_call_target="tpu_custom_call" | custom-call | flops 2147483648 | bytes 12845056 | tf_op jit(solution)/shard_map/pallas_call | solution.py:59
  186.6 0.0 reduce-scatter.5.cloned.1.call-update
  186.6 59.0 %reduce-scatter.5.cloned.1.call-done = bf16[1,2,512,256]{3,2,1,0:T(8,128)(2,1)} async-done(((bf16[8,2,512,256]{3,2,1,0:T(8,128)(2,1)}), bf16[1,2,512,256]{3,2,1,0:T(8,128)(2,1)}) %reduce-scatter.5.cloned.1.call-update) | async-done | bytes 524304 | tf_op jit(solution)/shard_map/reduce_scatter | solution.py:103
  245.7 1.0 dynamic-slice_bitcast_fusion
  246.6 2.8 %collective-permute-start.2 = (bf16[512,256]{1,0:T(8,128)(2,1)S(1)}, bf16[512,256]{1,0:T(8,128)(2,1)S(1)}, u32[]{:S(2)}, u32[]{:S(2)}) collective-permute-start(bf16[512,256]{1,0:T(8,128)(2,1)S(1)} %dynamic-slice_bitcast_fusion), channel_id=1, source_target_pairs={{0,1},{1,0},{2,3},{3,2},{4,5},{5,4},{6,7},{7,6},{8,9},{9,8},{10,11... | collective-permute-start | bytes 786440 | tf_op jit(solution)/shard_map/ppermute | solution.py:107
  249.4 6.0 %collective-permute-done.2 = bf16[512,256]{1,0:T(8,128)(2,1)S(1)} collective-permute-done((bf16[512,256]{1,0:T(8,128)(2,1)S(1)}, bf16[512,256]{1,0:T(8,128)(2,1)S(1)}, u32[]{:S(2)}, u32[]{:S(2)}) %collective-permute-start.2) | collective-permute-done | bytes 262176 | tf_op jit(solution)/shard_map/ppermute | solution.py:107
  255.4 1.0 fusion.16
  256.5 0.8 copy.21
  (3 shorter events, 0.1 us)
Async XLA Ops:
  6.5 69.5 %copy-start = (bf16[3,512,512]{2,1,0:T(8,128)(2,1)S(1)}, bf16[3,512,512]{2,1,0:T(8,128)(2,1)}, u32[]{:S(2)}) copy-start(bf16[3,512,512]{2,1,0:T(8,128)(2,1)} %param.6) | copy-start | bytes 4718596
  6.5 69.5 %all-gather.2.cloned.1.call-start = ((), (), s32[]{:S(2)}) async-start(), calls=%async_computation.3 | async-start | bytes 4718592 | tf_op jit(solution)/shard_map/all_gather | solution.py:74
  18.3 150.2 %reduce-scatter.3.cloned.1.call-start = ((), (), s32[]{:S(2)}) async-start(), calls=%async_computation.4 | async-start | bytes 13369344 | tf_op jit(solution)/shard_map/reduce_scatter | solution.py:83
  87.8 0.8 copy-start.2
  87.9 157.8 %reduce-scatter.5.cloned.1.call-start = ((), (), s32[]{:S(2)}) async-start(), calls=%async_computation.5 | async-start | bytes 4718592 | tf_op jit(solution)/shard_map/reduce_scatter | solution.py:103
  87.9 92.6 %collective-permute-start.1 = (bf16[8,512,512]{1,2,0:T(8,128)(2,1)}, bf16[8,512,512]{1,2,0:T(8,128)(2,1)}, u32[]{:S(2)}, u32[]{:S(2)}) collective-permute-start(bf16[8,512,512]{1,2,0:T(8,128)(2,1)} %all_to_all.5), channel_id=1, source_target_pairs={{0,16},{16,0},{1,17},{17,1},{2,18},{18,2},{3,19},{19,3},{4,20},{20... | collective-permute-start | bytes 12582920 | tf_op jit(solution)/shard_map/ppermute | solution.py:101
  98.4 2.2 slice-start
  169.6 6.0 %collective-permute-start = (bf16[127,512]{0,1:T(8,128)(2,1)S(1)}, bf16[127,512]{0,1:T(8,128)(2,1)S(1)}, u32[]{:S(2)}, u32[]{:S(2)}) collective-permute-start(bf16[127,512]{0,1:T(8,128)(2,1)S(1)} %slice_bitcast_fusion.1), channel_id=1, source_target_pairs={{0,16},{16,32},{32,48},{48,64},{64,80},{80,96},{96,112},{112,128},... | collective-permute-start | bytes 390152 | tf_op jit(solution)/shard_map/ppermute | solution.py:23
  176.1 3.5 %copy-start.1 = (bf16[256,3,512]{0,2,1:T(8,128)(2,1)S(1)}, bf16[256,3,512]{0,2,1:T(8,128)(2,1)}, u32[]{:S(2)}) copy-start(bf16[256,3,512]{0,2,1:T(8,128)(2,1)} %reduce-scatter.3.cloned.1.call-done) | copy-start | bytes 2359300
  176.1 3.5 %copy-start.3 = (f32[512]{0:T(512)S(1)}, f32[512]{0:T(512)}, u32[]{:S(2)}) copy-start(f32[512]{0:T(512)} %param.8) | copy-start | bytes 6148
  246.6 8.8 %collective-permute-start.2 = (bf16[512,256]{1,0:T(8,128)(2,1)S(1)}, bf16[512,256]{1,0:T(8,128)(2,1)S(1)}, u32[]{:S(2)}, u32[]{:S(2)}) collective-permute-start(bf16[512,256]{1,0:T(8,128)(2,1)S(1)} %dynamic-slice_bitcast_fusion), channel_id=1, source_target_pairs={{0,1},{1,0},{2,3},{3,2},{4,5},{5,4},{6,7},{7,6},{8,9},{9,8},{10,11... | collective-permute-start | bytes 786440 | tf_op jit(solution)/shard_map/ppermute | solution.py:107
Sparse Core Ops, SparseCore 0:
  18.4 57.5 all-gather.1
  88.0 80.4 reduce-scatter.2
  186.8 58.8 reduce-scatter.4

commit v8 on v5

--- a/solution.py
+++ b/solution.py
@@ -1,6 +1,8 @@
 import jax
 import jax.numpy as jnp
 from jax import lax
+from jax.experimental import pallas as pl
+from jax.experimental.pallas import tpu as pltpu
 from jax.sharding import Mesh, PartitionSpec as P
 
 
@@ -40,6 +42,39 @@
     return out.reshape(tok, channels)
 
 
+def out_proj_kernel(gt_ref, w_ref, *rest):
+    out_ref = rest[-1]
+    step, width, depth = w_ref.shape
+    res = jnp.dot(w_ref[...].reshape(step * width, depth), gt_ref[...], preferred_element_type=jnp.float32)
+    res = res.reshape(step, width, gt_ref.shape[1])
+    if len(rest) == 2:
+        res = res + rest[0][...].astype(jnp.float32)
+    out_ref[...] = res.astype(out_ref.dtype)
+
+
+def out_proj(gated_t, weight_t, acc=None, per_step=4):
+    depth, rows = gated_t.shape
+    blocks, width, _ = weight_t.shape
+    block = pl.BlockSpec((per_step, width, rows), lambda i: (i, 0, 0))
+    specs = [pl.BlockSpec((depth, rows), lambda i: (0, 0)), pl.BlockSpec((per_step, width, depth), lambda i: (i, 0, 0))]
+    operands = [gated_t, weight_t]
+    if acc is not None:
+        specs.append(block)
+        operands.append(acc)
+    return pl.pallas_call(
+        out_proj_kernel,
+        out_shape=jax.ShapeDtypeStruct((blocks, width, rows), jnp.bfloat16),
+        grid=(blocks // per_step,),
+        in_specs=specs,
+        out_specs=block,
+        cost_estimate=pl.CostEstimate(
+            flops=2 * rows * depth * width * blocks,
+            bytes_accessed=2 * (rows * depth + blocks * depth * width + len(operands) * blocks * rows * width),
+            transcendentals=0,
+        ),
+    )(*operands)
+
+
 def per_device(tokens, in_weight, filters, skip_gain, out_weight):
     gathered = lax.all_gather(lax.all_gather(tokens, "xhi", axis=0, tiled=True), "z", axis=0, tiled=True)
     chips = axis_size(("xlo", "y"))
@@ -69,15 +104,16 @@
     conv = conv + skip_gain[None, :] * product_f
     gated = (query_rows.astype(jnp.float32) * conv).astype(jnp.bfloat16)
     w_other = lax.ppermute(w_mine, "core", [(0, 1), (1, 0)])
-    partial_out = jnp.einsum(
-        "tc,jmco->jmto", gated, jnp.stack([w_mine, w_other], axis=1), preferred_element_type=jnp.float32
-    ).astype(jnp.bfloat16)
-    by_z = lax.psum_scatter(partial_out, "z", scatter_dimension=0, tiled=True)[0]
-    keep_at = (lax.axis_index("xhi") != lax.axis_index("core")).astype(jnp.int32)
-    keep = lax.dynamic_index_in_dim(by_z, keep_at, 0, keepdims=False)
-    give = lax.dynamic_index_in_dim(by_z, 1 - keep_at, 0, keepdims=False)
-    got = lax.ppermute(give, "xhi", [(0, 1), (1, 0)])
-    return (keep.astype(jnp.float32) + got.astype(jnp.float32)).astype(jnp.bfloat16)
+    swap = [(0, 1), (1, 0)]
+    same = lax.axis_index("xhi") == lax.axis_index("core")
+    keep_w = jnp.where(same, w_mine, w_other)
+    give_w = jnp.where(same, w_other, w_mine)
+    recv_w = lax.ppermute(give_w, "xhi", swap)
+    recv_g = lax.ppermute(gated, "xhi", swap)
+    mine = out_proj(gated.T, jnp.swapaxes(keep_w, 1, 2))
+    both = out_proj(recv_g.T, jnp.swapaxes(recv_w, 1, 2), mine)
+    summed = lax.psum_scatter(both, "z", scatter_dimension=0, tiled=True)[0]
+    return summed.T
 
 
 def solution(mesh):

time: 265 us -> 332 us (1.25); the launches traced: 265 us -> 329 us
  waiting for transfers between devices: 135 us -> 188 us
  Pallas kernels: 0 us -> 8.68 us
  matrix products: 22.9 us -> 15 us
  other arithmetic: 6.34 us -> 13.2 us
    reduce_scatter x1, waiting for transfers between devices: 63.4 us -> 132 us  [per_device(): lax.psum_scatter(jnp.einsum('rf,sfc->rsc', gathered, in_weight, preferred...]
    reduce_scatter x1, waiting for transfers between devices: 59 us -> 39.9 us  [per_device(): summed = lax.psum_scatter(both, 'z', scatter_dimension=0, tiled=True)[0]]
    pallas_call x0 -> x2, Pallas kernels: none -> 8.68 us  [out_proj(): pl.pallas_call(out_proj_kernel, out_shape=jax.ShapeDtypeStruct((blocks, w...]
    dot_general x1 -> x0, matrix products: 7.94 us -> none  [per_device(): jnp.einsum('tc,jmco->jmto', gated, jnp.stack([w_mine, w_other], axis=1),...]
    transpose x0 -> x1, other arithmetic: none -> 7.55 us  [per_device(): mine = out_proj(gated.T, jnp.swapaxes(keep_w, 1, 2))]
    ppermute x1, waiting for transfers between devices: 0.01 us -> 7.13 us  [per_device(): w_other = lax.ppermute(w_mine, 'core', [(0, 1), (1, 0)])]
    ppermute x1 -> x2, waiting for transfers between devices: 6.04 us -> 2.44 us  [the longest x1 2.44 us: per_device(): recv_g = lax.ppermute(gated, 'xhi', swap)]
  transfers between devices with their start and end apart: 6 -> 7, of which waited for: 5 -> 6; matrix products, arithmetic and copies ran while one was open for 8% -> 9% of each run, Pallas kernels for 0% -> 1%
where the time goes in v8:
time: 332 us; the launch traced here: 329 us
  waiting for transfers between devices  188 us (57%)
  blocking collectives  63.7 us (19%)
  local copies, waits for them, and re-layouts  18.1 us (5%)
  matrix products  15 us (5%)
  other arithmetic  13.2 us (4%)
  between operations  13.2 us (4%)
  starting transfers between devices  8.72 us (3%)
  Pallas kernels  8.68 us (3%)
    reduce_scatter x1, waiting for transfers between devices, per_device(): lax.psum_scatter(jnp.einsum('rf,sfc->rsc', gathered, in_weight, preferred...  132 us
    all_to_all x1, blocking collectives, per_device(): w_mine = lax.all_to_all(spread, ('xlo', 'y'), 0, 0, tiled=True)  52.1 us
    reduce_scatter x1, waiting for transfers between devices, per_device(): summed = lax.psum_scatter(both, 'z', scatter_dimension=0, tiled=True)[0]  39.9 us
    dot_general x1, matrix products, per_device(): jnp.einsum('rf,sfc->rsc', gathered, in_weight, preferred_element_type=jnp...  11.8 us
    all_gather x1, blocking collectives, per_device(): lax.all_gather(tokens, 'xhi', axis=0, tiled=True)  11.6 us
    another operation x2, local copies, waits for them, and re-layouts, toeplitz_conv(): jnp.tile(w, (1, taps))[:, :taps * 2 * taps].reshape(groups, taps, 2 * taps)  9.79 us
    pallas_call x2, Pallas kernels, out_proj(): pl.pallas_call(out_proj_kernel, out_shape=jax.ShapeDtypeStruct((blocks, w...  8.68 us
    transpose x1, other arithmetic, per_device(): mine = out_proj(gated.T, jnp.swapaxes(keep_w, 1, 2))  7.55 us
  transfers between devices with their start and end apart: 7, of which 6 were waited for; matrix products, arithmetic and copies ran while one was open for 9% of the time, Pallas kernels for 1%

profile of v8, /device:TPU:1, one launch (start us, length us, event | category | flops | bytes accessed | tf_op | source)
XLA Modules:
  0.0 328.6 jit_solution(658512485764020773)
XLA Ops:
  6.5 0.0 copy-start
  6.5 0.0 all-gather.2.cloned.1.call-start
  6.5 11.6 %all_gather.6 = bf16[512,512]{1,0:T(8,128)(2,1)} all-gather(bf16[256,512]{1,0:T(8,128)(2,1)} %param.5), channel_id=1, replica_groups=mesh['xlo'=2,'y'=4,'core'=2,'z'=8,'xhi'=2] {'xhi'}, dimensions={0}, use_global_device_ids=true | all-gather | bytes 786432 | tf_op jit(solution)/shard_map/all_gather | solution.py:79
  18.2 0.0 all-gather.2.cloned.1.call-update
  18.2 0.0 reduce-scatter.3.cloned.1.call-start
  18.3 1.3 copy.14
  19.5 0.4 broadcast_in_dim.2
  19.9 52.1 %all_to_all.5 = bf16[8,512,512]{1,2,0:T(8,128)(2,1)} all-to-all(bf16[8,512,512]{1,2,0:T(8,128)(2,1)S(1)} %broadcast_in_dim.2), channel_id=1, replica_groups=mesh['xlo'=2,'y'=4,'core'=2,'z'=8,'xhi'=2] {'xlo','y'}, dimensions={0} | all-to-all | bytes 8388608 | tf_op jit(solution)/shard_map/all_to_all | solution.py:82
  71.9 4.1 %all-gather.2.cloned.1.call-done = bf16[4096,512]{1,0:T(8,128)(2,1)} async-done(((bf16[512,512]{1,0:T(8,128)(2,1)}), bf16[4096,512]{1,0:T(8,128)(2,1)}) %all-gather.2.cloned.1.call-update) | async-done | bytes 4194320 | tf_op jit(solution)/shard_map/all_gather | solution.py:79
  76.0 0.0 copy-done
  76.0 11.8 %convolution_convert_fusion = bf16[4096,3,512]{0,2,1:T(8,128)(2,1)} fusion(bf16[3,512,512]{2,1,0:T(8,128)(2,1)S(1)} %copy-done, bf16[4096,512]{1,0:T(8,128)(2,1)} %all-gather.2.cloned.1.call-done), kind=kOutput, calls=%fused_computation | convolution fusion | flops 6448742400 | bytes 18350080 | tf_op jit(solution)/shard_map/rf,sfc->rsc/dot_general | solution.py:89
  87.8 0.0 reduce-scatter.3.cloned.1.call-update
  87.8 0.0 reduce-scatter.5.cloned.1.call-start
  87.9 0.8 collective-permute-start.2
  88.6 0.0 copy-start.5
  88.6 7.1 %collective-permute-done.2 = bf16[8,512,512]{1,2,0:T(8,128)(2,1)} collective-permute-done((bf16[8,512,512]{1,2,0:T(8,128)(2,1)}, bf16[8,512,512]{1,2,0:T(8,128)(2,1)}, u32[]{:S(2)}, u32[]{:S(2)}) %collective-permute-start.2) | collective-permute-done | bytes 4194336 | tf_op jit(solution)/shard_map/ppermute | solution.py:106
  95.8 7.5 %select_bitcast_fusion = (bf16[8,512,512]{2,1,0:T(8,128)(2,1)}, bf16[8,512,512]{1,2,0:T(8,128)(2,1)}) fusion(bf16[8,512,512]{1,2,0:T(8,128)(2,1)} %all_to_all.5, bf16[8,512,512]{1,2,0:T(8,128)(2,1)} %collective-permute-done.2, pred[]{:T(512)S(6)} %eq.3), kind=kLoop, calls=%fused_computation.9 | loop fusion | flops 4194304 | bytes 16777216 | tf_op jit(solution)/shard_map/transpose | solution.py:113
  103.3 2.5 collective-permute-start.3
  105.8 0.0 copy-done.5
  105.8 0.1 rev.3
  105.9 3.0 tile.4
  108.9 6.8 %tile.10 = f32[32,32896]{1,0:T(8,128)} reshape(f32[32,128,257]{2,1,0:T(8,128)} %tile.4) | data formatting | bytes 8421376 | tf_op jit(solution)/shard_map/tile | solution.py:36
  115.6 0.0 slice-start
  115.7 2.2 slice-done
  117.8 1.3 copy.24
  119.1 3.1 fusion
  122.2 132.2 %reduce-scatter.3.cloned.1.call-done = bf16[256,3,512]{0,2,1:T(8,128)(2,1)} async-done(((bf16[4096,3,512]{0,2,1:T(8,128)(2,1)}), bf16[256,3,512]{0,2,1:T(8,128)(2,1)}) %reduce-scatter.3.cloned.1.call-update) | async-done | bytes 786448 | tf_op jit(solution)/shard_map/reduce_scatter | solution.py:88
  254.4 1.1 multiply_convert_fusion
  255.5 0.1 slice_bitcast_fusion.1
  255.6 1.9 collective-permute-start
  257.6 1.1 fusion.17
  258.7 2.2 collective-permute-done
  260.8 0.2 pad_maximum_fusion
  261.1 0.1 slice.41
  261.2 0.1 slice.43
  261.3 0.0 copy-start.2
  261.3 0.0 copy-start.6
  261.3 3.2 fusion.5
  264.5 0.3 copy.20
  264.8 0.0 copy-done.2
  264.8 0.0 copy-done.6
  264.8 0.2 fusion.14
  265.0 0.0 copy-start.3
  265.0 3.5 %collective-permute-start.1 = (bf16[256,512]{0,1:T(8,128)(2,1)S(1)}, bf16[256,512]{0,1:T(8,128)(2,1)S(1)}, u32[]{:S(2)}, u32[]{:S(2)}) collective-permute-start(bf16[256,512]{0,1:T(8,128)(2,1)S(1)} %fusion.14), channel_id=1, source_target_pairs={{0,1},{1,0},{2,3},{3,2},{4,5},{5,4},{6,7},{7,6},{8,9},{9,8},{10,11... | collective-permute-start | bytes 786440 | tf_op jit(solution)/shard_map/ppermute | solution.py:112
  268.5 0.0 copy-done.3
  268.5 4.0 %shard_map.55.rest_0_ = bf16[8,512,256]{2,1,0:T(8,128)(2,1)} custom-call(bf16[512,256]{1,0:T(8,128)(2,1)} %bitcast.54, bf16[8,512,512]{2,1,0:T(8,128)(2,1)} %get-tuple-element.11.w_ref), custom_call_target="tpu_custom_call" | custom-call | flops 1073741824 | bytes 8650752 | tf_op jit(solution)/shard_map/pallas_call | solution.py:64
  272.5 0.0 collective-permute-done.3
  272.5 2.4 collective-permute-done.1
  275.0 0.0 copy-start.4
  275.0 0.0 copy-start.1
  275.0 0.7 copy-done.4
  275.7 4.7 %shard_map.56 = bf16[8,512,256]{2,1,0:T(8,128)(2,1)} custom-call(bf16[512,256]{1,0:T(8,128)(2,1)} %bitcast.55, bf16[8,512,512]{2,1,0:T(8,128)(2,1)} %bitcast.8.w_ref, bf16[8,512,256]{2,1,0:T(8,128)(2,1)} %shard_map.55.rest_0_), custom_call_target="tpu_custom_call" | custom-call | flops 1073741824 | bytes 10747904 | tf_op jit(solution)/shard_map/pallas_call | solution.py:64
  280.3 0.0 reduce-scatter.5.cloned.1.call-update
  280.4 39.9 %reduce-scatter.5.cloned.1.call-done = bf16[1,512,256]{2,1,0:T(8,128)(2,1)} async-done(((bf16[8,512,256]{2,1,0:T(8,128)(2,1)}), bf16[1,512,256]{2,1,0:T(8,128)(2,1)}) %reduce-scatter.5.cloned.1.call-update) | async-done | bytes 262160 | tf_op jit(solution)/shard_map/reduce_scatter | solution.py:115
  320.3 1.8 copy.21
  322.1 0.0 copy-done.1
  (3 shorter events, 0.1 us)
Async XLA Ops:
  6.5 69.5 %copy-start = (bf16[3,512,512]{2,1,0:T(8,128)(2,1)S(1)}, bf16[3,512,512]{2,1,0:T(8,128)(2,1)}, u32[]{:S(2)}) copy-start(bf16[3,512,512]{2,1,0:T(8,128)(2,1)} %param.6) | copy-start | bytes 4718596
  6.5 69.5 %all-gather.2.cloned.1.call-start = ((), (), s32[]{:S(2)}) async-start(), calls=%async_computation.3 | async-start | bytes 4718592 | tf_op jit(solution)/shard_map/all_gather | solution.py:79
  18.2 236.2 %reduce-scatter.3.cloned.1.call-start = ((), (), s32[]{:S(2)}) async-start(), calls=%async_computation.4 | async-start | bytes 13369344 | tf_op jit(solution)/shard_map/reduce_scatter | solution.py:88
  87.8 232.4 %reduce-scatter.5.cloned.1.call-start = ((), (), s32[]{:S(2)}) async-start(), calls=%async_computation.5 | async-start | bytes 2359296 | tf_op jit(solution)/shard_map/reduce_scatter | solution.py:115
  87.9 7.9 %collective-permute-start.2 = (bf16[8,512,512]{1,2,0:T(8,128)(2,1)}, bf16[8,512,512]{1,2,0:T(8,128)(2,1)}, u32[]{:S(2)}, u32[]{:S(2)}) collective-permute-start(bf16[8,512,512]{1,2,0:T(8,128)(2,1)} %all_to_all.5), channel_id=1, source_target_pairs={{0,16},{16,0},{1,17},{17,1},{2,18},{18,2},{3,19},{19,3},{4,20},{20... | collective-permute-start | bytes 12582920 | tf_op jit(solution)/shard_map/ppermute | solution.py:106
  88.6 17.1 %copy-start.5 = (f32[32,128]{1,0:T(8,128)S(1)}, f32[32,128]{1,0:T(8,128)}, u32[]{:S(2)}) copy-start(f32[32,128]{1,0:T(8,128)} %param.7) | copy-start | bytes 49156
  103.3 169.2 %collective-permute-start.3 = (bf16[8,512,512]{1,2,0:T(8,128)(2,1)}, bf16[8,512,512]{1,2,0:T(8,128)(2,1)}, u32[]{:S(2)}, u32[]{:S(2)}) collective-permute-start(bf16[8,512,512]{1,2,0:T(8,128)(2,1)} %get-tuple-element.12), channel_id=1, source_target_pairs={{0,1},{1,0},{2,3},{3,2},{4,5},{5,4},{6,7},{7,6},{8,9},{9,8},{10,11... | collective-permute-start | bytes 12582920 | tf_op jit(solution)/shard_map/ppermute | solution.py:111
  115.6 2.2 slice-start
  255.6 5.2 %collective-permute-start = (bf16[127,512]{0,1:T(8,128)(2,1)S(1)}, bf16[127,512]{0,1:T(8,128)(2,1)S(1)}, u32[]{:S(2)}, u32[]{:S(2)}) collective-permute-start(bf16[127,512]{0,1:T(8,128)(2,1)S(1)} %slice_bitcast_fusion.1), channel_id=1, source_target_pairs={{0,16},{16,32},{32,48},{48,64},{64,80},{80,96},{96,112},{112,128},... | collective-permute-start | bytes 390152 | tf_op jit(solution)/shard_map/ppermute | solution.py:23
  261.3 3.5 %copy-start.2 = (bf16[256,3,512]{0,2,1:T(8,128)(2,1)S(1)}, bf16[256,3,512]{0,2,1:T(8,128)(2,1)}, u32[]{:S(2)}) copy-start(bf16[256,3,512]{0,2,1:T(8,128)(2,1)} %reduce-scatter.3.cloned.1.call-done) | copy-start | bytes 2359300
  261.3 3.5 %copy-start.6 = (f32[512]{0:T(512)S(1)}, f32[512]{0:T(512)}, u32[]{:S(2)}) copy-start(f32[512]{0:T(512)} %param.8) | copy-start | bytes 6148
  265.0 3.5 %copy-start.3 = (bf16[256,512]{0,1:T(8,128)(2,1)}, bf16[256,512]{0,1:T(8,128)(2,1)S(1)}, u32[]{:S(2)}) copy-start(bf16[256,512]{0,1:T(8,128)(2,1)S(1)} %fusion.14) | copy-start | bytes 786436
  265.0 9.9 %collective-permute-start.1 = (bf16[256,512]{0,1:T(8,128)(2,1)S(1)}, bf16[256,512]{0,1:T(8,128)(2,1)S(1)}, u32[]{:S(2)}, u32[]{:S(2)}) collective-permute-start(bf16[256,512]{0,1:T(8,128)(2,1)S(1)} %fusion.14), channel_id=1, source_target_pairs={{0,1},{1,0},{2,3},{3,2},{4,5},{5,4},{6,7},{7,6},{8,9},{9,8},{10,11... | collective-permute-start | bytes 786440 | tf_op jit(solution)/shard_map/ppermute | solution.py:112
  275.0 0.7 copy-start.4
  275.0 47.1 %copy-start.1 = (bf16[3,512,512]{2,1,0:T(8,128)(2,1)S(1)}, bf16[3,512,512]{2,1,0:T(8,128)(2,1)}, u32[]{:S(2)}) copy-start(bf16[3,512,512]{2,1,0:T(8,128)(2,1)} %param.6) | copy-start | bytes 4718596
Sparse Core Ops, SparseCore 0:
  18.3 57.6 all-gather.1
  87.9 166.4 reduce-scatter.2
  280.5 39.7 reduce-scatter.4

commit v9 on v8

--- a/solution.py
+++ b/solution.py
@@ -77,10 +77,14 @@
 
 def per_device(tokens, in_weight, filters, skip_gain, out_weight):
     gathered = lax.all_gather(lax.all_gather(tokens, "xhi", axis=0, tiled=True), "z", axis=0, tiled=True)
+    swap = [(0, 1), (1, 0)]
+    same = lax.axis_index("xhi") == lax.axis_index("core")
+    across = lax.ppermute(lax.ppermute(out_weight, "xhi", swap), "core", swap)
+    chunk = jnp.where(same, out_weight, across)
     chips = axis_size(("xlo", "y"))
-    spread = jnp.broadcast_to(out_weight[None], (chips,) + out_weight.shape)
-    w_mine = lax.all_to_all(spread, ("xlo", "y"), 0, 0, tiled=True)
-    gathered, w_mine = lax.optimization_barrier((gathered, w_mine))
+    spread = jnp.broadcast_to(chunk[None], (chips,) + chunk.shape)
+    plane = lax.all_to_all(spread, ("xlo", "y"), 0, 0, tiled=True)
+    gathered, plane = lax.optimization_barrier((gathered, plane))
     tok_dev = gathered.shape[0] // axis_size(SEQ)
     channels = in_weight.shape[2]
     taps_count = filters.shape[1]
@@ -103,12 +107,9 @@
     conv = toeplitz_conv(extended, filters)
     conv = conv + skip_gain[None, :] * product_f
     gated = (query_rows.astype(jnp.float32) * conv).astype(jnp.bfloat16)
-    w_other = lax.ppermute(w_mine, "core", [(0, 1), (1, 0)])
-    swap = [(0, 1), (1, 0)]
-    same = lax.axis_index("xhi") == lax.axis_index("core")
-    keep_w = jnp.where(same, w_mine, w_other)
-    give_w = jnp.where(same, w_other, w_mine)
-    recv_w = lax.ppermute(give_w, "xhi", swap)
+    plane_other = lax.ppermute(plane, "core", swap)
+    keep_w = jnp.where(same, plane, plane_other)
+    recv_w = jnp.where(same, plane_other, plane)
     recv_g = lax.ppermute(gated, "xhi", swap)
     mine = out_proj(gated.T, jnp.swapaxes(keep_w, 1, 2))
     both = out_proj(recv_g.T, jnp.swapaxes(recv_w, 1, 2), mine)

time: 332 us -> 267 us (0.80)
  waiting for transfers between devices: 188 us -> 123 us
  starting transfers between devices: 8.72 us -> 12.4 us
    reduce_scatter x1, waiting for transfers between devices: 132 us -> 66.1 us  [per_device(): lax.psum_scatter(jnp.einsum('rf,sfc->rsc', gathered, in_weight, preferred...]
    ppermute x2 -> x3, waiting for transfers between devices: 7.13 us -> 13.4 us  [the longest x2 13.4 us: per_device(): across = lax.ppermute(lax.ppermute(out_weight, 'xhi', swap), 'core', swap)]
    ppermute x2 -> x3, starting transfers between devices: 3.23 us -> 7.87 us  [the longest x2 4.23 us: per_device(): across = lax.ppermute(lax.ppermute(out_weight, 'xhi', swap), 'core', swap)]
    all_gather x1, waiting for transfers between devices: 4.07 us -> 0.01 us  [per_device(): lax.all_gather(lax.all_gather(tokens, 'xhi', axis=0, tiled=True), 'z', ax...]
  transfers between devices with their start and end apart: 7 -> 8, of which waited for: 6 -> 5; matrix products, arithmetic and copies ran while one was open for 9% -> 10% of each run, Pallas kernels for 1% -> 2%
where the time goes in v9:
time: 267 us; the launch traced here: 263 us
  waiting for transfers between devices  123 us (46%)
  blocking collectives  63.2 us (24%)
  local copies, waits for them, and re-layouts  16.9 us (6%)
  matrix products  15.1 us (6%)
  between operations  13.3 us (5%)
  starting transfers between devices  12.4 us (5%)
  other arithmetic  10.8 us (4%)
  Pallas kernels  8.59 us (3%)
    reduce_scatter x1, waiting for transfers between devices, per_device(): lax.psum_scatter(jnp.einsum('rf,sfc->rsc', gathered, in_weight, preferred...  66.1 us
    all_to_all x1, blocking collectives, per_device(): plane = lax.all_to_all(spread, ('xlo', 'y'), 0, 0, tiled=True)  51.6 us
    reduce_scatter x1, waiting for transfers between devices, per_device(): summed = lax.psum_scatter(both, 'z', scatter_dimension=0, tiled=True)[0]  40.6 us
    ppermute x2, waiting for transfers between devices, per_device(): across = lax.ppermute(lax.ppermute(out_weight, 'xhi', swap), 'core', swap)  13.4 us
    dot_general x1, matrix products, per_device(): jnp.einsum('rf,sfc->rsc', gathered, in_weight, preferred_element_type=jnp...  11.8 us
    all_gather x1, blocking collectives, per_device(): lax.all_gather(tokens, 'xhi', axis=0, tiled=True)  11.7 us
    another operation x2, local copies, waits for them, and re-layouts, toeplitz_conv(): jnp.tile(w, (1, taps))[:, :taps * 2 * taps].reshape(groups, taps, 2 * taps)  9.67 us
    pallas_call x2, Pallas kernels, out_proj(): pl.pallas_call(out_proj_kernel, out_shape=jax.ShapeDtypeStruct((blocks, w...  8.59 us
  transfers between devices with their start and end apart: 8, of which 5 were waited for; matrix products, arithmetic and copies ran while one was open for 10% of the time, Pallas kernels for 2%

profile of v9, /device:TPU:1, one launch (start us, length us, event | category | flops | bytes accessed | tf_op | source)
XLA Modules:
  0.0 263.3 jit_solution(14491926638933421662)
XLA Ops:
  6.5 0.0 copy-start
  6.5 0.0 all-gather.2.cloned.1.call-start
  6.5 11.7 %all_gather.6 = bf16[512,512]{1,0:T(8,128)(2,1)} all-gather(bf16[256,512]{1,0:T(8,128)(2,1)} %param.5), channel_id=1, replica_groups=mesh['xlo'=2,'y'=4,'core'=2,'z'=8,'xhi'=2] {'xhi'}, dimensions={0}, use_global_device_ids=true | all-gather | bytes 786432 | tf_op jit(solution)/shard_map/all_gather | solution.py:79
  18.2 0.0 all-gather.2.cloned.1.call-update
  18.2 0.0 reduce-scatter.3.cloned.1.call-start
  18.3 1.4 collective-permute-start
  19.7 11.9 %collective-permute-done = bf16[512,512]{1,0:T(8,128)(2,1)S(1)} collective-permute-done((bf16[512,512]{1,0:T(8,128)(2,1)}, bf16[512,512]{1,0:T(8,128)(2,1)S(1)}, u32[]{:S(2)}, u32[]{:S(2)}) %collective-permute-start) | collective-permute-done | bytes 524320 | tf_op jit(solution)/shard_map/ppermute | solution.py:82
  31.6 2.8 %collective-permute-start.1 = (bf16[512,512]{1,0:T(8,128)(2,1)S(1)}, bf16[512,512]{1,0:T(8,128)(2,1)S(1)}, u32[]{:S(2)}, u32[]{:S(2)}) collective-permute-start(bf16[512,512]{1,0:T(8,128)(2,1)S(1)} %collective-permute-done), channel_id=1, source_target_pairs={{0,16},{16,0},{1,17},{17,1},{2,18},{18,2},{3,19},{19,3},{4,20},{20... | collective-permute-start | bytes 1572872 | tf_op jit(solution)/shard_map/ppermute | solution.py:82
  34.4 1.5 collective-permute-done.1
  35.9 0.1 broadcast_select_fusion
  36.0 0.2 copy.14
  36.2 0.4 broadcast_in_dim.2
  36.6 51.6 %all_to_all.5 = bf16[8,512,512]{1,2,0:T(8,128)(2,1)} all-to-all(bf16[8,512,512]{1,2,0:T(8,128)(2,1)S(1)} %broadcast_in_dim.2), channel_id=1, replica_groups=mesh['xlo'=2,'y'=4,'core'=2,'z'=8,'xhi'=2] {'xlo','y'}, dimensions={0} | all-to-all | bytes 8388608 | tf_op jit(solution)/shard_map/all_to_all | solution.py:86
  88.1 0.0 all-gather.2.cloned.1.call-done
  88.2 0.0 copy-done
  88.2 11.8 %convolution_convert_fusion = bf16[4096,3,512]{0,2,1:T(8,128)(2,1)} fusion(bf16[3,512,512]{2,1,0:T(8,128)(2,1)S(1)} %copy-done, bf16[4096,512]{1,0:T(8,128)(2,1)} %all-gather.2.cloned.1.call-done), kind=kOutput, calls=%fused_computation | convolution fusion | flops 6448742400 | bytes 18350080 | tf_op jit(solution)/shard_map/rf,sfc->rsc/dot_general | solution.py:93
  99.9 0.0 copy-start.6
  99.9 0.0 reduce-scatter.3.cloned.1.call-update
  100.0 0.0 reduce-scatter.5.cloned.1.call-start
  100.0 3.6 %collective-permute-start.4 = (bf16[8,512,512]{1,2,0:T(8,128)(2,1)}, bf16[8,512,512]{1,2,0:T(8,128)(2,1)}, u32[]{:S(2)}, u32[]{:S(2)}) collective-permute-start(bf16[8,512,512]{1,2,0:T(8,128)(2,1)} %all_to_all.5), channel_id=1, source_target_pairs={{0,16},{16,0},{1,17},{17,1},{2,18},{18,2},{3,19},{19,3},{4,20},{20... | collective-permute-start | bytes 12582920 | tf_op jit(solution)/shard_map/ppermute | solution.py:110
  103.6 0.0 copy-done.6
  103.7 0.1 rev.3
  103.7 3.0 %tile.4 = f32[32,128,257]{2,1,0:T(8,128)} broadcast(f32[32,257]{1,0:T(8,128)S(1)} %pad.5), dimensions={0,2} | broadcast | bytes 4243584 | tf_op jit(solution)/shard_map/tile | solution.py:36
  106.7 6.7 %tile.10 = f32[32,32896]{1,0:T(8,128)} reshape(f32[32,128,257]{2,1,0:T(8,128)} %tile.4) | data formatting | bytes 8421376 | tf_op jit(solution)/shard_map/tile | solution.py:36
  113.4 0.0 slice-start
  113.4 2.2 slice-done
  115.6 1.3 copy.24
  116.9 3.1 %fusion = (bf16[32,128,256]{2,1,0:T(8,128)(2,1)}, bf16[32,128,256]{2,1,0:T(8,128)(2,1)}) fusion(f32[4,8,128,256]{3,2,1,0:T(8,128)S(1)} %copy.24), kind=kLoop, calls=%fused_computation.3 | loop fusion | flops 4194304 | bytes 8388608 | tf_op jit(solution)/shard_map/convert_element_type | solution.py:38
  120.0 66.1 %reduce-scatter.3.cloned.1.call-done = bf16[256,3,512]{0,2,1:T(8,128)(2,1)} async-done(((bf16[4096,3,512]{0,2,1:T(8,128)(2,1)}), bf16[256,3,512]{0,2,1:T(8,128)(2,1)}) %reduce-scatter.3.cloned.1.call-update) | async-done | bytes 786448 | tf_op jit(solution)/shard_map/reduce_scatter | solution.py:92
  186.1 1.1 multiply_convert_fusion
  187.2 0.1 slice_bitcast_fusion.1
  187.3 2.1 collective-permute-start.2
  189.4 1.1 fusion.17
  190.5 2.8 %collective-permute-done.2 = bf16[127,512]{0,1:T(8,128)(2,1)S(1)} collective-permute-done((bf16[127,512]{0,1:T(8,128)(2,1)S(1)}, bf16[127,512]{0,1:T(8,128)(2,1)S(1)}, u32[]{:S(2)}, u32[]{:S(2)}) %collective-permute-start.2) | collective-permute-done | bytes 130080 | tf_op jit(solution)/shard_map/ppermute | solution.py:23
  193.3 0.2 pad_maximum_fusion
  193.5 0.1 slice.41
  193.6 0.1 slice.43
  193.7 0.0 copy-start.3
  193.7 0.0 copy-start.7
  193.7 0.0 copy-start.2
  193.8 3.3 %fusion.5 = f32[2,128,32,16]{1,3,0,2:T(8,128)S(1)} fusion(bf16[32,128,256]{2,1,0:T(8,128)(2,1)} %get-tuple-element.9, bf16[32,128,256]{2,1,0:T(8,128)(2,1)} %get-tuple-element.10, bf16[2,128,32,16]{1,3,0,2:T(8,128)(2,1)S(1)} %copy.17, bf16[2,128,32,16]{1,3,0,2:T(8,128)(2,1)S(1)} %copy.16), kind=kOutput, calls=%fused_computation.11 | convolution fusion | flops 146800640 | bytes 5242880 | tf_op jit(solution)/shard_map/gts,isgc->itgc/dot_general | solution.py:41
  197.0 0.3 copy.20
  197.3 0.0 copy-done.3
  197.3 0.0 copy-done.7
  197.3 0.2 fusion.14
  197.5 0.0 copy-start.4
  197.5 2.4 collective-permute-start.3
  199.9 0.0 collective-permute-done.4
  199.9 0.0 copy-done.2
  199.9 5.1 %select_bitcast_fusion = (bf16[8,512,512]{2,1,0:T(8,128)(2,1)}, bf16[8,512,512]{2,1,0:T(8,128)(2,1)}) fusion(bf16[8,512,512]{1,2,0:T(8,128)(2,1)S(1)} %copy-done.2, bf16[8,512,512]{1,2,0:T(8,128)(2,1)} %collective-permute-done.4, pred[]{:T(512)S(6)} %eq.3), kind=kLoop, calls=%fused_computation.9 | loop fusion | flops 4194304 | bytes 16777216 | tf_op jit(solution)/shard_map/transpose | solution.py:114
  205.0 0.0 copy-done.4
  205.0 4.0 %shard_map.55.rest_0_ = bf16[8,512,256]{2,1,0:T(8,128)(2,1)} custom-call(bf16[512,256]{1,0:T(8,128)(2,1)} %bitcast.55, bf16[8,512,512]{2,1,0:T(8,128)(2,1)} %get-tuple-element.11.w_ref), custom_call_target="tpu_custom_call" | custom-call | flops 1073741824 | bytes 8650752 | tf_op jit(solution)/shard_map/pallas_call | solution.py:64
  209.1 0.0 collective-permute-done.3
  209.1 0.0 copy-start.5
  209.1 0.0 copy-start.1
  209.1 0.7 copy-done.5
  209.8 4.6 %shard_map.56 = bf16[8,512,256]{2,1,0:T(8,128)(2,1)} custom-call(bf16[512,256]{1,0:T(8,128)(2,1)} %bitcast.56, bf16[8,512,512]{2,1,0:T(8,128)(2,1)} %get-tuple-element.12.w_ref, bf16[8,512,256]{2,1,0:T(8,128)(2,1)} %shard_map.55.rest_0_), custom_call_target="tpu_custom_call" | custom-call | flops 1073741824 | bytes 10747904 | tf_op jit(solution)/shard_map/pallas_call | solution.py:64
  214.3 0.0 reduce-scatter.5.cloned.1.call-update
  214.4 40.6 %reduce-scatter.5.cloned.1.call-done = bf16[1,512,256]{2,1,0:T(8,128)(2,1)} async-done(((bf16[8,512,256]{2,1,0:T(8,128)(2,1)}), bf16[1,512,256]{2,1,0:T(8,128)(2,1)}) %reduce-scatter.5.cloned.1.call-update) | async-done | bytes 262160 | tf_op jit(solution)/shard_map/reduce_scatter | solution.py:116
  254.9 1.8 copy.21
  256.7 0.0 copy-done.1
  (3 shorter events, 0.1 us)
Async XLA Ops:
  6.5 81.6 %copy-start = (bf16[3,512,512]{2,1,0:T(8,128)(2,1)S(1)}, bf16[3,512,512]{2,1,0:T(8,128)(2,1)}, u32[]{:S(2)}) copy-start(bf16[3,512,512]{2,1,0:T(8,128)(2,1)} %param.6) | copy-start | bytes 4718596
  6.5 81.6 %all-gather.2.cloned.1.call-start = ((), (), s32[]{:S(2)}) async-start(), calls=%async_computation.3 | async-start | bytes 4718592 | tf_op jit(solution)/shard_map/all_gather | solution.py:79
  18.2 167.9 %reduce-scatter.3.cloned.1.call-start = ((), (), s32[]{:S(2)}) async-start(), calls=%async_computation.4 | async-start | bytes 13369344 | tf_op jit(solution)/shard_map/reduce_scatter | solution.py:92
  18.3 13.3 %collective-permute-start = (bf16[512,512]{1,0:T(8,128)(2,1)}, bf16[512,512]{1,0:T(8,128)(2,1)S(1)}, u32[]{:S(2)}, u32[]{:S(2)}) collective-permute-start(bf16[512,512]{1,0:T(8,128)(2,1)} %param.9), channel_id=1, source_target_pairs={{0,1},{1,0},{2,3},{3,2},{4,5},{5,4},{6,7},{7,6},{8,9},{9,8},{10,11... | collective-permute-start | bytes 1572872 | tf_op jit(solution)/shard_map/ppermute | solution.py:82
  31.6 4.4 %collective-permute-start.1 = (bf16[512,512]{1,0:T(8,128)(2,1)S(1)}, bf16[512,512]{1,0:T(8,128)(2,1)S(1)}, u32[]{:S(2)}, u32[]{:S(2)}) collective-permute-start(bf16[512,512]{1,0:T(8,128)(2,1)S(1)} %collective-permute-done), channel_id=1, source_target_pairs={{0,16},{16,0},{1,17},{17,1},{2,18},{18,2},{3,19},{19,3},{4,20},{20... | collective-permute-start | bytes 1572872 | tf_op jit(solution)/shard_map/ppermute | solution.py:82
  99.9 3.7 %copy-start.6 = (f32[32,128]{1,0:T(8,128)S(1)}, f32[32,128]{1,0:T(8,128)}, u32[]{:S(2)}) copy-start(f32[32,128]{1,0:T(8,128)} %param.7) | copy-start | bytes 49156
  100.0 155.0 %reduce-scatter.5.cloned.1.call-start = ((), (), s32[]{:S(2)}) async-start(), calls=%async_computation.5 | async-start | bytes 2359296 | tf_op jit(solution)/shard_map/reduce_scatter | solution.py:116
  100.0 99.9 %collective-permute-start.4 = (bf16[8,512,512]{1,2,0:T(8,128)(2,1)}, bf16[8,512,512]{1,2,0:T(8,128)(2,1)}, u32[]{:S(2)}, u32[]{:S(2)}) collective-permute-start(bf16[8,512,512]{1,2,0:T(8,128)(2,1)} %all_to_all.5), channel_id=1, source_target_pairs={{0,16},{16,0},{1,17},{17,1},{2,18},{18,2},{3,19},{19,3},{4,20},{20... | collective-permute-start | bytes 12582920 | tf_op jit(solution)/shard_map/ppermute | solution.py:110
  113.4 2.2 slice-start
  187.3 6.0 %collective-permute-start.2 = (bf16[127,512]{0,1:T(8,128)(2,1)S(1)}, bf16[127,512]{0,1:T(8,128)(2,1)S(1)}, u32[]{:S(2)}, u32[]{:S(2)}) collective-permute-start(bf16[127,512]{0,1:T(8,128)(2,1)S(1)} %slice_bitcast_fusion.1), channel_id=1, source_target_pairs={{0,16},{16,32},{32,48},{48,64},{64,80},{80,96},{96,112},{112,128},... | collective-permute-start | bytes 390152 | tf_op jit(solution)/shard_map/ppermute | solution.py:23
  193.7 3.6 %copy-start.3 = (bf16[256,3,512]{0,2,1:T(8,128)(2,1)S(1)}, bf16[256,3,512]{0,2,1:T(8,128)(2,1)}, u32[]{:S(2)}) copy-start(bf16[256,3,512]{0,2,1:T(8,128)(2,1)} %reduce-scatter.3.cloned.1.call-done) | copy-start | bytes 2359300
  193.7 3.6 %copy-start.7 = (f32[512]{0:T(512)S(1)}, f32[512]{0:T(512)}, u32[]{:S(2)}) copy-start(f32[512]{0:T(512)} %param.8) | copy-start | bytes 6148
  193.7 6.2 %copy-start.2 = (bf16[8,512,512]{1,2,0:T(8,128)(2,1)S(1)}, bf16[8,512,512]{1,2,0:T(8,128)(2,1)}, u32[]{:S(2)}) copy-start(bf16[8,512,512]{1,2,0:T(8,128)(2,1)} %all_to_all.5) | copy-start | bytes 12582916
  197.5 7.5 %copy-start.4 = (bf16[256,512]{0,1:T(8,128)(2,1)}, bf16[256,512]{0,1:T(8,128)(2,1)S(1)}, u32[]{:S(2)}) copy-start(bf16[256,512]{0,1:T(8,128)(2,1)S(1)} %fusion.14) | copy-start | bytes 786436
  197.5 11.6 %collective-permute-start.3 = (bf16[256,512]{0,1:T(8,128)(2,1)S(1)}, bf16[256,512]{0,1:T(8,128)(2,1)S(1)}, u32[]{:S(2)}, u32[]{:S(2)}) collective-permute-start(bf16[256,512]{0,1:T(8,128)(2,1)S(1)} %fusion.14), channel_id=1, source_target_pairs={{0,1},{1,0},{2,3},{3,2},{4,5},{5,4},{6,7},{7,6},{8,9},{9,8},{10,11... | collective-permute-start | bytes 786440 | tf_op jit(solution)/shard_map/ppermute | solution.py:113
  209.1 0.7 copy-start.5
  209.1 47.7 %copy-start.1 = (bf16[3,512,512]{2,1,0:T(8,128)(2,1)S(1)}, bf16[3,512,512]{2,1,0:T(8,128)(2,1)}, u32[]{:S(2)}) copy-start(bf16[3,512,512]{2,1,0:T(8,128)(2,1)} %param.6) | copy-start | bytes 4718596
Sparse Core Ops, SparseCore 0:
  18.3 57.6 all-gather.1
  100.1 85.9 reduce-scatter.2
  214.5 40.4 reduce-scatter.4

commit v10 on v9

--- a/solution.py
+++ b/solution.py
@@ -76,10 +76,14 @@
 
 
 def per_device(tokens, in_weight, filters, skip_gain, out_weight):
-    gathered = lax.all_gather(lax.all_gather(tokens, "xhi", axis=0, tiled=True), "z", axis=0, tiled=True)
     swap = [(0, 1), (1, 0)]
+    both_x = lax.ppermute(jnp.concatenate([tokens, out_weight]), "xhi", swap)
+    tokens_x, weight_x = both_x[: tokens.shape[0]], both_x[tokens.shape[0] :]
+    first = lax.axis_index("xhi") == 0
+    pair = jnp.where(first, jnp.concatenate([tokens, tokens_x]), jnp.concatenate([tokens_x, tokens]))
+    gathered = lax.all_gather(pair, "z", axis=0, tiled=True)
     same = lax.axis_index("xhi") == lax.axis_index("core")
-    across = lax.ppermute(lax.ppermute(out_weight, "xhi", swap), "core", swap)
+    across = lax.ppermute(weight_x, "core", swap)
     chunk = jnp.where(same, out_weight, across)
     chips = axis_size(("xlo", "y"))
     spread = jnp.broadcast_to(chunk[None], (chips,) + chunk.shape)
@@ -97,6 +101,10 @@
         scatter_dimension=0,
         tiled=True,
     ).astype(jnp.float32)
+    plane_other = lax.ppermute(plane, "core", swap)
+    keep_w = jnp.swapaxes(jnp.where(same, plane, plane_other), 1, 2)
+    recv_w = jnp.swapaxes(jnp.where(same, plane_other, plane), 1, 2)
+    summed, keep_w, recv_w = lax.optimization_barrier((summed, keep_w, recv_w))
     query_rows = summed[:, 0].astype(jnp.bfloat16)
     key_rows = summed[:, 1].astype(jnp.bfloat16)
     value_rows = summed[:, 2].astype(jnp.bfloat16)
@@ -107,12 +115,9 @@
     conv = toeplitz_conv(extended, filters)
     conv = conv + skip_gain[None, :] * product_f
     gated = (query_rows.astype(jnp.float32) * conv).astype(jnp.bfloat16)
-    plane_other = lax.ppermute(plane, "core", swap)
-    keep_w = jnp.where(same, plane, plane_other)
-    recv_w = jnp.where(same, plane_other, plane)
     recv_g = lax.ppermute(gated, "xhi", swap)
-    mine = out_proj(gated.T, jnp.swapaxes(keep_w, 1, 2))
-    both = out_proj(recv_g.T, jnp.swapaxes(recv_w, 1, 2), mine)
+    mine = out_proj(gated.T, keep_w)
+    both = out_proj(recv_g.T, recv_w, mine)
     summed = lax.psum_scatter(both, "z", scatter_dimension=0, tiled=True)[0]
     return summed.T
 

time: 267 us -> 264 us (0.989)
  blocking collectives: 63.2 us -> 53.4 us
  other arithmetic: 10.8 us -> 14.4 us
  local copies, waits for them, and re-layouts: 16.9 us -> 19.6 us
    all_gather x1 -> x0, blocking collectives: 11.7 us -> none  [per_device(): lax.all_gather(tokens, 'xhi', axis=0, tiled=True)]
    reduce_scatter x1, waiting for transfers between devices: 66.1 us -> 59.3 us  [per_device(): lax.psum_scatter(jnp.einsum('rf,sfc->rsc', gathered, in_weight, preferred...]
    ppermute x2, waiting for transfers between devices: 13.4 us -> 17.7 us  [the longest x1 16.2 us: per_device(): both_x = lax.ppermute(jnp.concatenate([tokens, out_weight]), 'xhi', swap)]
    ppermute x1, waiting for transfers between devices: 0.01 us -> 2.82 us  [per_device(): recv_g = lax.ppermute(gated, 'xhi', swap)]
  transfers between devices with their start and end apart: 8 -> 8, of which waited for: 5 -> 7; matrix products, arithmetic and copies ran while one was open for 10% -> 9% of each run, Pallas kernels for 2% -> 2%
where the time goes in v10:
time: 264 us; the launch traced here: 260 us
  waiting for transfers between devices  124 us (47%)
  blocking collectives  53.4 us (20%)
  local copies, waits for them, and re-layouts  19.6 us (7%)
  matrix products  15 us (6%)
  other arithmetic  14.4 us (5%)
  between operations  13.3 us (5%)
  starting transfers between devices  12.2 us (5%)
  Pallas kernels  8.58 us (3%)
    reduce_scatter x1, waiting for transfers between devices, per_device(): lax.psum_scatter(jnp.einsum('rf,sfc->rsc', gathered, in_weight, preferred...  59.3 us
    all_to_all x1, blocking collectives, per_device(): plane = lax.all_to_all(spread, ('xlo', 'y'), 0, 0, tiled=True)  53.4 us
    reduce_scatter x1, waiting for transfers between devices, per_device(): summed = lax.psum_scatter(both, 'z', scatter_dimension=0, tiled=True)[0]  40.5 us
    ppermute x1, waiting for transfers between devices, per_device(): both_x = lax.ppermute(jnp.concatenate([tokens, out_weight]), 'xhi', swap)  16.2 us
    dot_general x1, matrix products, per_device(): jnp.einsum('rf,sfc->rsc', gathered, in_weight, preferred_element_type=jnp...  11.8 us
    another operation x2, local copies, waits for them, and re-layouts, toeplitz_conv(): jnp.tile(w, (1, taps))[:, :taps * 2 * taps].reshape(groups, taps, 2 * taps)  9.78 us
    pallas_call x2, Pallas kernels, out_proj(): pl.pallas_call(out_proj_kernel, out_shape=jax.ShapeDtypeStruct((blocks, w...  8.58 us
    transpose x1, other arithmetic, per_device(): recv_w = jnp.swapaxes(jnp.where(same, plane_other, plane), 1, 2)  5.31 us
  transfers between devices with their start and end apart: 8, of which 7 were waited for; matrix products, arithmetic and copies ran while one was open for 9% of the time, Pallas kernels for 2%

profile of v10, /device:TPU:1, one launch (start us, length us, event | category | flops | bytes accessed | tf_op | source)
XLA Modules:
  0.0 260.3 jit_solution(10049653527909373815)
XLA Ops:
  6.5 0.0 copy-start
  6.5 0.0 copy-start.4
  6.5 0.0 all-gather.2.cloned.1.call-start
  6.5 1.3 pad_maximum_fusion
  7.9 3.7 %collective-permute-start = (bf16[768,512]{1,0:T(8,128)(2,1)S(1)}, bf16[768,512]{1,0:T(8,128)(2,1)}, u32[]{:S(2)}, u32[]{:S(2)}) collective-permute-start(bf16[768,512]{1,0:T(8,128)(2,1)S(1)} %pad_maximum_fusion), channel_id=1, source_target_pairs={{0,1},{1,0},{2,3},{3,2},{4,5},{5,4},{6,7},{7,6},{8,9},{9,8},{10,11... | collective-permute-start | bytes 2359304 | tf_op jit(solution)/shard_map/ppermute | solution.py:80
  11.5 16.2 %collective-permute-done = bf16[768,512]{1,0:T(8,128)(2,1)} collective-permute-done((bf16[768,512]{1,0:T(8,128)(2,1)S(1)}, bf16[768,512]{1,0:T(8,128)(2,1)}, u32[]{:S(2)}, u32[]{:S(2)}) %collective-permute-start) | collective-permute-done | bytes 786464 | tf_op jit(solution)/shard_map/ppermute | solution.py:80
  27.7 1.0 slice.53
  28.7 2.0 maximum_select_fusion
  30.7 0.0 all-gather.2.cloned.1.call-update
  30.8 0.0 reduce-scatter.3.cloned.1.call-start
  30.8 1.1 slice.54
  31.9 2.5 collective-permute-start.1
  34.4 1.5 collective-permute-done.1
  35.9 0.0 copy-done.4
  35.9 0.1 broadcast_select_fusion
  36.0 0.2 copy.14
  36.2 0.4 broadcast_in_dim.2
  36.5 53.4 %all_to_all.5 = bf16[8,512,512]{1,2,0:T(8,128)(2,1)} all-to-all(bf16[8,512,512]{1,2,0:T(8,128)(2,1)S(1)} %broadcast_in_dim.2), channel_id=1, replica_groups=mesh['xlo'=2,'y'=4,'core'=2,'z'=8,'xhi'=2] {'xlo','y'}, dimensions={0} | all-to-all | bytes 8388608 | tf_op jit(solution)/shard_map/all_to_all | solution.py:90
  89.9 0.7 all-gather.2.cloned.1.call-done
  90.6 0.0 copy-done
  90.6 11.8 %convolution_convert_fusion = bf16[4096,3,512]{0,2,1:T(8,128)(2,1)} fusion(bf16[3,512,512]{2,1,0:T(8,128)(2,1)S(1)} %copy-done, bf16[4096,512]{1,0:T(8,128)(2,1)} %all-gather.2.cloned.1.call-done), kind=kOutput, calls=%fused_computation | convolution fusion | flops 6448742400 | bytes 18350080 | tf_op jit(solution)/shard_map/rf,sfc->rsc/dot_general | solution.py:97
  102.5 0.0 copy-start.7
  102.5 0.0 reduce-scatter.3.cloned.1.call-update
  102.5 0.0 reduce-scatter.5.cloned.1.call-start
  102.5 1.5 collective-permute-start.2
  104.1 0.0 copy-done.7
  104.1 0.1 rev.3
  104.2 3.1 %tile.4 = f32[32,128,257]{2,1,0:T(8,128)} broadcast(f32[32,257]{1,0:T(8,128)S(1)} %pad.5), dimensions={0,2} | broadcast | bytes 4243584 | tf_op jit(solution)/shard_map/tile | solution.py:36
  107.3 6.7 %tile.10 = f32[32,32896]{1,0:T(8,128)} reshape(f32[32,128,257]{2,1,0:T(8,128)} %tile.4) | data formatting | bytes 8421376 | tf_op jit(solution)/shard_map/tile | solution.py:36
  114.0 0.0 slice-start
  114.0 2.8 %slice-done = f32[32,32768]{1,0:T(8,128)S(1)} async-done(((f32[32,32896]{1,0:T(8,128)}), f32[32,32768]{1,0:T(8,128)S(1)}, s32[]{:S(2)}) %slice-start) | async-done | bytes 4194328 | tf_op jit(solution)/shard_map/slice | solution.py:36
  116.7 1.3 copy.24
  118.0 0.0 copy-start.2
  118.0 3.1 %fusion = (bf16[32,128,256]{2,1,0:T(8,128)(2,1)}, bf16[32,128,256]{2,1,0:T(8,128)(2,1)}) fusion(f32[4,8,128,256]{3,2,1,0:T(8,128)S(1)} %copy.24), kind=kLoop, calls=%fused_computation.3 | loop fusion | flops 4194304 | bytes 8388608 | tf_op jit(solution)/shard_map/convert_element_type | solution.py:38
  121.1 0.0 collective-permute-done.2
  121.1 0.0 copy-done.2
  121.1 5.3 %select_bitcast_fusion = (bf16[8,512,512]{2,1,0:T(8,128)(2,1)}, bf16[8,512,512]{2,1,0:T(8,128)(2,1)}) fusion(bf16[8,512,512]{1,2,0:T(8,128)(2,1)} %collective-permute-done.2, bf16[8,512,512]{1,2,0:T(8,128)(2,1)S(1)} %copy-done.2, pred[]{:T(512)S(6)} %eq.7), kind=kLoop, calls=%fused_computation.9 | loop fusion | flops 4194304 | bytes 16777216 | tf_op jit(solution)/shard_map/transpose | solution.py:106
  126.4 59.3 %reduce-scatter.3.cloned.1.call-done = bf16[256,3,512]{0,2,1:T(8,128)(2,1)} async-done(((bf16[4096,3,512]{0,2,1:T(8,128)(2,1)}), bf16[256,3,512]{0,2,1:T(8,128)(2,1)}) %reduce-scatter.3.cloned.1.call-update) | async-done | bytes 786448 | tf_op jit(solution)/shard_map/reduce_scatter | solution.py:96
  185.6 1.1 multiply_convert_fusion
  186.7 0.1 slice_bitcast_fusion.1
  186.8 2.1 collective-permute-start.3
  188.9 1.1 fusion.17
  190.0 2.8 %collective-permute-done.3 = bf16[127,512]{0,1:T(8,128)(2,1)S(1)} collective-permute-done((bf16[127,512]{0,1:T(8,128)(2,1)S(1)}, bf16[127,512]{0,1:T(8,128)(2,1)S(1)}, u32[]{:S(2)}, u32[]{:S(2)}) %collective-permute-start.3) | collective-permute-done | bytes 130080 | tf_op jit(solution)/shard_map/ppermute | solution.py:23
  192.9 0.2 pad_maximum_fusion.1
  193.1 0.1 slice.49
  193.2 0.1 slice.51
  193.3 0.0 copy-start.3
  193.3 0.0 copy-start.8
  193.3 3.2 %fusion.5 = f32[2,128,32,16]{1,3,0,2:T(8,128)S(1)} fusion(bf16[32,128,256]{2,1,0:T(8,128)(2,1)} %get-tuple-element.15, bf16[32,128,256]{2,1,0:T(8,128)(2,1)} %get-tuple-element.16, bf16[2,128,32,16]{1,3,0,2:T(8,128)(2,1)S(1)} %copy.17, bf16[2,128,32,16]{1,3,0,2:T(8,128)(2,1)S(1)} %copy.16), kind=kOutput, calls=%fused_computation.11 | convolution fusion | flops 146800640 | bytes 5242880 | tf_op jit(solution)/shard_map/gts,isgc->itgc/dot_general | solution.py:41
  196.5 0.3 copy.20
  196.8 0.0 copy-done.3
  196.8 0.0 copy-done.8
  196.9 0.2 fusion.14
  197.0 0.0 copy-start.5
  197.0 2.3 collective-permute-start.4
  199.4 0.0 copy-done.5
  199.4 4.0 %shard_map.55.rest_0_ = bf16[8,512,256]{2,1,0:T(8,128)(2,1)} custom-call(bf16[512,256]{1,0:T(8,128)(2,1)} %bitcast.55, bf16[8,512,512]{2,1,0:T(8,128)(2,1)} %get-tuple-element.14.w_ref), custom_call_target="tpu_custom_call" | custom-call | flops 1073741824 | bytes 8650752 | tf_op jit(solution)/shard_map/pallas_call | solution.py:64
  203.4 2.8 %collective-permute-done.4 = bf16[256,512]{0,1:T(8,128)(2,1)S(1)} collective-permute-done((bf16[256,512]{0,1:T(8,128)(2,1)S(1)}, bf16[256,512]{0,1:T(8,128)(2,1)S(1)}, u32[]{:S(2)}, u32[]{:S(2)}) %collective-permute-start.4) | collective-permute-done | bytes 262176 | tf_op jit(solution)/shard_map/ppermute | solution.py:118
  206.2 0.7 copy-done.6
  206.9 4.5 %shard_map.56 = bf16[8,512,256]{2,1,0:T(8,128)(2,1)} custom-call(bf16[512,256]{1,0:T(8,128)(2,1)} %bitcast.56, bf16[8,512,512]{2,1,0:T(8,128)(2,1)} %get-tuple-element.13.w_ref, bf16[8,512,256]{2,1,0:T(8,128)(2,1)} %shard_map.55.rest_0_), custom_call_target="tpu_custom_call" | custom-call | flops 1073741824 | bytes 10747904 | tf_op jit(solution)/shard_map/pallas_call | solution.py:64
  211.5 0.0 reduce-scatter.5.cloned.1.call-update
  211.5 40.5 %reduce-scatter.5.cloned.1.call-done = bf16[1,512,256]{2,1,0:T(8,128)(2,1)} async-done(((bf16[8,512,256]{2,1,0:T(8,128)(2,1)}), bf16[1,512,256]{2,1,0:T(8,128)(2,1)}) %reduce-scatter.5.cloned.1.call-update) | async-done | bytes 262160 | tf_op jit(solution)/shard_map/reduce_scatter | solution.py:121
  252.0 1.8 copy.21
  253.8 0.0 copy-done.1
  (5 shorter events, 0.1 us)
Async XLA Ops:
  6.5 84.1 %copy-start = (bf16[3,512,512]{2,1,0:T(8,128)(2,1)S(1)}, bf16[3,512,512]{2,1,0:T(8,128)(2,1)}, u32[]{:S(2)}) copy-start(bf16[3,512,512]{2,1,0:T(8,128)(2,1)} %param.6) | copy-start | bytes 4718596
  6.5 29.4 %copy-start.4 = (bf16[512,512]{1,0:T(8,128)(2,1)S(1)}, bf16[512,512]{1,0:T(8,128)(2,1)}, u32[]{:S(2)}) copy-start(bf16[512,512]{1,0:T(8,128)(2,1)} %param.9) | copy-start | bytes 1572868
  6.5 84.1 %all-gather.2.cloned.1.call-start = ((), (), s32[]{:S(2)}) async-start(), calls=%async_computation.3 | async-start | bytes 4718592 | tf_op jit(solution)/shard_map/all_gather | solution.py:84
  7.9 19.9 %collective-permute-start = (bf16[768,512]{1,0:T(8,128)(2,1)S(1)}, bf16[768,512]{1,0:T(8,128)(2,1)}, u32[]{:S(2)}, u32[]{:S(2)}) collective-permute-start(bf16[768,512]{1,0:T(8,128)(2,1)S(1)} %pad_maximum_fusion), channel_id=1, source_target_pairs={{0,1},{1,0},{2,3},{3,2},{4,5},{5,4},{6,7},{7,6},{8,9},{9,8},{10,11... | collective-permute-start | bytes 2359304 | tf_op jit(solution)/shard_map/ppermute | solution.py:80
  30.8 154.9 %reduce-scatter.3.cloned.1.call-start = ((), (), s32[]{:S(2)}) async-start(), calls=%async_computation.4 | async-start | bytes 13369344 | tf_op jit(solution)/shard_map/reduce_scatter | solution.py:96
  31.9 4.0 %collective-permute-start.1 = (bf16[512,512]{1,0:T(8,128)(2,1)S(1)}, bf16[512,512]{1,0:T(8,128)(2,1)S(1)}, u32[]{:S(2)}, u32[]{:S(2)}) collective-permute-start(bf16[512,512]{1,0:T(8,128)(2,1)S(1)} %slice.54), channel_id=1, source_target_pairs={{0,16},{16,0},{1,17},{17,1},{2,18},{18,2},{3,19},{19,3},{4,20},{20... | collective-permute-start | bytes 1572872 | tf_op jit(solution)/shard_map/ppermute | solution.py:86
  102.5 1.6 copy-start.7
  102.5 149.5 %reduce-scatter.5.cloned.1.call-start = ((), (), s32[]{:S(2)}) async-start(), calls=%async_computation.5 | async-start | bytes 2359296 | tf_op jit(solution)/shard_map/reduce_scatter | solution.py:121
  102.5 18.5 %collective-permute-start.2 = (bf16[8,512,512]{1,2,0:T(8,128)(2,1)}, bf16[8,512,512]{1,2,0:T(8,128)(2,1)}, u32[]{:S(2)}, u32[]{:S(2)}) collective-permute-start(bf16[8,512,512]{1,2,0:T(8,128)(2,1)} %all_to_all.5), channel_id=1, source_target_pairs={{0,16},{16,0},{1,17},{17,1},{2,18},{18,2},{3,19},{19,3},{4,20},{20... | collective-permute-start | bytes 12582920 | tf_op jit(solution)/shard_map/ppermute | solution.py:104
  114.0 2.8 %slice-start = ((f32[32,32896]{1,0:T(8,128)}), f32[32,32768]{1,0:T(8,128)S(1)}, s32[]{:S(2)}) async-start(f32[32,32896]{1,0:T(8,128)} %tile.10), calls=%async_computation.6 | async-start | bytes 8388608 | tf_op jit(solution)/shard_map/slice | solution.py:36
  118.0 3.1 %copy-start.2 = (bf16[8,512,512]{1,2,0:T(8,128)(2,1)S(1)}, bf16[8,512,512]{1,2,0:T(8,128)(2,1)}, u32[]{:S(2)}) copy-start(bf16[8,512,512]{1,2,0:T(8,128)(2,1)} %all_to_all.5) | copy-start | bytes 12582916
  186.8 6.0 %collective-permute-start.3 = (bf16[127,512]{0,1:T(8,128)(2,1)S(1)}, bf16[127,512]{0,1:T(8,128)(2,1)S(1)}, u32[]{:S(2)}, u32[]{:S(2)}) collective-permute-start(bf16[127,512]{0,1:T(8,128)(2,1)S(1)} %slice_bitcast_fusion.1), channel_id=1, source_target_pairs={{0,16},{16,32},{32,48},{48,64},{64,80},{80,96},{96,112},{112,128},... | collective-permute-start | bytes 390152 | tf_op jit(solution)/shard_map/ppermute | solution.py:23
  193.3 3.5 %copy-start.3 = (bf16[256,3,512]{0,2,1:T(8,128)(2,1)S(1)}, bf16[256,3,512]{0,2,1:T(8,128)(2,1)}, u32[]{:S(2)}) copy-start(bf16[256,3,512]{0,2,1:T(8,128)(2,1)} %reduce-scatter.3.cloned.1.call-done) | copy-start | bytes 2359300
  193.3 3.5 %copy-start.8 = (f32[512]{0:T(512)S(1)}, f32[512]{0:T(512)}, u32[]{:S(2)}) copy-start(f32[512]{0:T(512)} %param.8) | copy-start | bytes 6148
  197.0 2.4 copy-start.5
  197.0 9.2 %collective-permute-start.4 = (bf16[256,512]{0,1:T(8,128)(2,1)S(1)}, bf16[256,512]{0,1:T(8,128)(2,1)S(1)}, u32[]{:S(2)}, u32[]{:S(2)}) collective-permute-start(bf16[256,512]{0,1:T(8,128)(2,1)S(1)} %fusion.14), channel_id=1, source_target_pairs={{0,1},{1,0},{2,3},{3,2},{4,5},{5,4},{6,7},{7,6},{8,9},{9,8},{10,11... | collective-permute-start | bytes 786440 | tf_op jit(solution)/shard_map/ppermute | solution.py:118
  206.2 0.7 copy-start.6
  206.2 47.5 %copy-start.1 = (bf16[3,512,512]{2,1,0:T(8,128)(2,1)S(1)}, bf16[3,512,512]{2,1,0:T(8,128)(2,1)}, u32[]{:S(2)}) copy-start(bf16[3,512,512]{2,1,0:T(8,128)(2,1)} %param.6) | copy-start | bytes 4718596
Sparse Core Ops, SparseCore 0:
  30.9 59.7 all-gather.1
  102.6 82.9 reduce-scatter.2
  211.6 40.2 reduce-scatter.4

commit v11 on v10

--- a/solution.py
+++ b/solution.py
@@ -77,8 +77,8 @@
 
 def per_device(tokens, in_weight, filters, skip_gain, out_weight):
     swap = [(0, 1), (1, 0)]
-    both_x = lax.ppermute(jnp.concatenate([tokens, out_weight]), "xhi", swap)
-    tokens_x, weight_x = both_x[: tokens.shape[0]], both_x[tokens.shape[0] :]
+    tokens_x = lax.ppermute(tokens, "xhi", swap)
+    weight_x = lax.ppermute(out_weight, ("core", "xhi"), [(1, 0), (2, 3)])
     first = lax.axis_index("xhi") == 0
     pair = jnp.where(first, jnp.concatenate([tokens, tokens_x]), jnp.concatenate([tokens_x, tokens]))
     gathered = lax.all_gather(pair, "z", axis=0, tiled=True)

time: 264 us -> 261 us (0.989)
  starting transfers between devices: 12.2 us -> 20.9 us
  waiting for transfers between devices: 124 us -> 118 us
    ppermute x1 -> x2, starting transfers between devices: 3.66 us -> 9.11 us  [the longest x1 5.54 us: per_device(): weight_x = lax.ppermute(out_weight, ('core', 'xhi'), [(1, 0), (2, 3)])]
    ppermute x1 -> x2, waiting for transfers between devices: 16.2 us -> 11.7 us  [the longest x1 6.39 us: per_device(): weight_x = lax.ppermute(out_weight, ('core', 'xhi'), [(1, 0), (2, 3)])]
  transfers between devices with their start and end apart: 8 -> 9, of which waited for: 7 -> 7; matrix products, arithmetic and copies ran while one was open for 9% -> 8% of each run, Pallas kernels for 2% -> 2%
where the time goes in v11:
time: 261 us; the launch traced here: 257 us
  waiting for transfers between devices  118 us (45%)
  blocking collectives  51.7 us (20%)
  starting transfers between devices  20.9 us (8%)
  local copies, waits for them, and re-layouts  17.3 us (7%)
  matrix products  15 us (6%)
  between operations  13.3 us (5%)
  other arithmetic  13 us (5%)
  Pallas kernels  8.59 us (3%)
    reduce_scatter x1, waiting for transfers between devices, per_device(): lax.psum_scatter(jnp.einsum('rf,sfc->rsc', gathered, in_weight, preferred...  58.7 us
    all_to_all x1, blocking collectives, per_device(): plane = lax.all_to_all(spread, ('xlo', 'y'), 0, 0, tiled=True)  51.7 us
    reduce_scatter x1, waiting for transfers between devices, per_device(): summed = lax.psum_scatter(both, 'z', scatter_dimension=0, tiled=True)[0]  40.3 us
    dot_general x1, matrix products, per_device(): jnp.einsum('rf,sfc->rsc', gathered, in_weight, preferred_element_type=jnp...  11.8 us
    another operation x2, local copies, waits for them, and re-layouts, toeplitz_conv(): jnp.tile(w, (1, taps))[:, :taps * 2 * taps].reshape(groups, taps, 2 * taps)  9.78 us
    pallas_call x2, Pallas kernels, out_proj(): pl.pallas_call(out_proj_kernel, out_shape=jax.ShapeDtypeStruct((blocks, w...  8.59 us
    ppermute x1, waiting for transfers between devices, per_device(): weight_x = lax.ppermute(out_weight, ('core', 'xhi'), [(1, 0), (2, 3)])  6.39 us
    ppermute x1, starting transfers between devices, per_device(): weight_x = lax.ppermute(out_weight, ('core', 'xhi'), [(1, 0), (2, 3)])  5.54 us
  transfers between devices with their start and end apart: 9, of which 7 were waited for; matrix products, arithmetic and copies ran while one was open for 8% of the time, Pallas kernels for 2%

profile of v11, /device:TPU:1, one launch (start us, length us, event | category | flops | bytes accessed | tf_op | source)
XLA Modules:
  0.0 257.4 jit_solution(18196857112061851130)
XLA Ops:
  6.5 0.0 copy-start
  6.5 0.0 all-gather.2.cloned.1.call-start
  6.5 3.6 %collective-permute-start = (bf16[256,512]{1,0:T(8,128)(2,1)}, bf16[256,512]{1,0:T(8,128)(2,1)S(1)}, u32[]{:S(2)}, u32[]{:S(2)}) collective-permute-start(bf16[256,512]{1,0:T(8,128)(2,1)} %param.5), channel_id=1, source_target_pairs={{0,1},{1,0},{2,3},{3,2},{4,5},{5,4},{6,7},{7,6},{8,9},{9,8},{10,11... | collective-permute-start | bytes 786440 | tf_op jit(solution)/shard_map/ppermute | solution.py:80
  10.1 5.3 %collective-permute-done = bf16[256,512]{1,0:T(8,128)(2,1)S(1)} collective-permute-done((bf16[256,512]{1,0:T(8,128)(2,1)}, bf16[256,512]{1,0:T(8,128)(2,1)S(1)}, u32[]{:S(2)}, u32[]{:S(2)}) %collective-permute-start) | collective-permute-done | bytes 262176 | tf_op jit(solution)/shard_map/ppermute | solution.py:80
  15.4 2.0 maximum_select_fusion
  17.4 0.0 all-gather.2.cloned.1.call-update
  17.5 0.0 reduce-scatter.3.cloned.1.call-start
  17.5 5.5 %collective-permute-start.1 = (bf16[512,512]{1,0:T(8,128)(2,1)}, bf16[512,512]{1,0:T(8,128)(2,1)S(1)}, u32[]{:S(2)}, u32[]{:S(2)}) collective-permute-start(bf16[512,512]{1,0:T(8,128)(2,1)} %param.9), channel_id=1, source_target_pairs={{1,0},{16,17},{3,2},{18,19},{5,4},{20,21},{7,6},{22,23},{9,8},{24,... | collective-permute-start | bytes 1572872 | tf_op jit(solution)/shard_map/ppermute | solution.py:81
  23.1 6.4 %collective-permute-done.1 = bf16[512,512]{1,0:T(8,128)(2,1)S(1)} collective-permute-done((bf16[512,512]{1,0:T(8,128)(2,1)}, bf16[512,512]{1,0:T(8,128)(2,1)S(1)}, u32[]{:S(2)}, u32[]{:S(2)}) %collective-permute-start.1) | collective-permute-done | bytes 524320 | tf_op jit(solution)/shard_map/ppermute | solution.py:81
  29.4 3.3 %collective-permute-start.2 = (bf16[512,512]{1,0:T(8,128)(2,1)S(1)}, bf16[512,512]{1,0:T(8,128)(2,1)S(1)}, u32[]{:S(2)}, u32[]{:S(2)}) collective-permute-start(bf16[512,512]{1,0:T(8,128)(2,1)S(1)} %collective-permute-done.1), channel_id=1, source_target_pairs={{0,16},{16,0},{1,17},{17,1},{2,18},{18,2},{3,19},{19,3},{4,20},{20... | collective-permute-start | bytes 1572872 | tf_op jit(solution)/shard_map/ppermute | solution.py:86
  32.8 1.5 collective-permute-done.2
  34.3 0.1 broadcast_select_fusion
  34.4 0.2 copy.14
  34.6 0.4 broadcast_in_dim.2
  34.9 51.7 %all_to_all.5 = bf16[8,512,512]{1,2,0:T(8,128)(2,1)} all-to-all(bf16[8,512,512]{1,2,0:T(8,128)(2,1)S(1)} %broadcast_in_dim.2), channel_id=1, replica_groups=mesh['xlo'=2,'y'=4,'core'=2,'z'=8,'xhi'=2] {'xlo','y'}, dimensions={0} | all-to-all | bytes 8388608 | tf_op jit(solution)/shard_map/all_to_all | solution.py:90
  86.7 0.0 all-gather.2.cloned.1.call-done
  86.7 0.0 copy-done
  86.7 11.8 %convolution_convert_fusion = bf16[4096,3,512]{0,2,1:T(8,128)(2,1)} fusion(bf16[3,512,512]{2,1,0:T(8,128)(2,1)S(1)} %copy-done, bf16[4096,512]{1,0:T(8,128)(2,1)} %all-gather.2.cloned.1.call-done), kind=kOutput, calls=%fused_computation | convolution fusion | flops 6448742400 | bytes 18350080 | tf_op jit(solution)/shard_map/rf,sfc->rsc/dot_general | solution.py:97
  98.5 0.0 copy-start.6
  98.5 0.0 reduce-scatter.3.cloned.1.call-update
  98.5 0.0 reduce-scatter.5.cloned.1.call-start
  98.6 3.6 %collective-permute-start.3 = (bf16[8,512,512]{1,2,0:T(8,128)(2,1)}, bf16[8,512,512]{1,2,0:T(8,128)(2,1)}, u32[]{:S(2)}, u32[]{:S(2)}) collective-permute-start(bf16[8,512,512]{1,2,0:T(8,128)(2,1)} %all_to_all.5), channel_id=1, source_target_pairs={{0,16},{16,0},{1,17},{17,1},{2,18},{18,2},{3,19},{19,3},{4,20},{20... | collective-permute-start | bytes 12582920 | tf_op jit(solution)/shard_map/ppermute | solution.py:104
  102.2 0.0 copy-done.6
  102.2 0.1 rev.3
  102.3 3.1 %tile.4 = f32[32,128,257]{2,1,0:T(8,128)} broadcast(f32[32,257]{1,0:T(8,128)S(1)} %pad.5), dimensions={0,2} | broadcast | bytes 4243584 | tf_op jit(solution)/shard_map/tile | solution.py:36
  105.4 6.7 %tile.10 = f32[32,32896]{1,0:T(8,128)} reshape(f32[32,128,257]{2,1,0:T(8,128)} %tile.4) | data formatting | bytes 8421376 | tf_op jit(solution)/shard_map/tile | solution.py:36
  112.1 0.0 slice-start
  112.1 2.5 slice-done
  114.6 1.3 copy.24
  115.9 0.0 copy-start.2
  115.9 3.1 %fusion = (bf16[32,128,256]{2,1,0:T(8,128)(2,1)}, bf16[32,128,256]{2,1,0:T(8,128)(2,1)}) fusion(f32[4,8,128,256]{3,2,1,0:T(8,128)S(1)} %copy.24), kind=kLoop, calls=%fused_computation.3 | loop fusion | flops 4194304 | bytes 8388608 | tf_op jit(solution)/shard_map/convert_element_type | solution.py:38
  118.9 0.0 collective-permute-done.3
  118.9 0.0 copy-done.2
  118.9 5.3 %select_bitcast_fusion = (bf16[8,512,512]{2,1,0:T(8,128)(2,1)}, bf16[8,512,512]{2,1,0:T(8,128)(2,1)}) fusion(bf16[8,512,512]{1,2,0:T(8,128)(2,1)} %collective-permute-done.3, bf16[8,512,512]{1,2,0:T(8,128)(2,1)S(1)} %copy-done.2, pred[]{:T(512)S(6)} %eq.7), kind=kLoop, calls=%fused_computation.9 | loop fusion | flops 4194304 | bytes 16777216 | tf_op jit(solution)/shard_map/transpose | solution.py:106
  124.2 58.7 %reduce-scatter.3.cloned.1.call-done = bf16[256,3,512]{0,2,1:T(8,128)(2,1)} async-done(((bf16[4096,3,512]{0,2,1:T(8,128)(2,1)}), bf16[256,3,512]{0,2,1:T(8,128)(2,1)}) %reduce-scatter.3.cloned.1.call-update) | async-done | bytes 786448 | tf_op jit(solution)/shard_map/reduce_scatter | solution.py:96
  182.9 1.1 multiply_convert_fusion
  184.0 0.1 slice_bitcast_fusion.1
  184.1 2.1 collective-permute-start.4
  186.2 1.1 fusion.17
  187.3 2.8 %collective-permute-done.4 = bf16[127,512]{0,1:T(8,128)(2,1)S(1)} collective-permute-done((bf16[127,512]{0,1:T(8,128)(2,1)S(1)}, bf16[127,512]{0,1:T(8,128)(2,1)S(1)}, u32[]{:S(2)}, u32[]{:S(2)}) %collective-permute-start.4) | collective-permute-done | bytes 130080 | tf_op jit(solution)/shard_map/ppermute | solution.py:23
  190.1 0.2 pad_maximum_fusion
  190.3 0.1 slice.41
  190.5 0.1 slice.43
  190.6 0.0 copy-start.3
  190.6 0.0 copy-start.7
  190.6 3.2 %fusion.5 = f32[2,128,32,16]{1,3,0,2:T(8,128)S(1)} fusion(bf16[32,128,256]{2,1,0:T(8,128)(2,1)} %get-tuple-element.15, bf16[32,128,256]{2,1,0:T(8,128)(2,1)} %get-tuple-element.16, bf16[2,128,32,16]{1,3,0,2:T(8,128)(2,1)S(1)} %copy.17, bf16[2,128,32,16]{1,3,0,2:T(8,128)(2,1)S(1)} %copy.16), kind=kOutput, calls=%fused_computation.11 | convolution fusion | flops 146800640 | bytes 5242880 | tf_op jit(solution)/shard_map/gts,isgc->itgc/dot_general | solution.py:41
  193.8 0.3 copy.20
  194.1 0.0 copy-done.3
  194.1 0.0 copy-done.7
  194.1 0.2 fusion.14
  194.3 0.0 copy-start.4
  194.3 2.6 %collective-permute-start.5 = (bf16[256,512]{0,1:T(8,128)(2,1)S(1)}, bf16[256,512]{0,1:T(8,128)(2,1)S(1)}, u32[]{:S(2)}, u32[]{:S(2)}) collective-permute-start(bf16[256,512]{0,1:T(8,128)(2,1)S(1)} %fusion.14), channel_id=1, source_target_pairs={{0,1},{1,0},{2,3},{3,2},{4,5},{5,4},{6,7},{7,6},{8,9},{9,8},{10,11... | collective-permute-start | bytes 786440 | tf_op jit(solution)/shard_map/ppermute | solution.py:118
  196.9 0.0 copy-done.4
  196.9 4.0 %shard_map.55.rest_0_ = bf16[8,512,256]{2,1,0:T(8,128)(2,1)} custom-call(bf16[512,256]{1,0:T(8,128)(2,1)} %bitcast.55, bf16[8,512,512]{2,1,0:T(8,128)(2,1)} %get-tuple-element.14.w_ref), custom_call_target="tpu_custom_call" | custom-call | flops 1073741824 | bytes 8650752 | tf_op jit(solution)/shard_map/pallas_call | solution.py:64
  200.9 2.5 collective-permute-done.5
  203.5 0.0 copy-start.5
  203.5 0.0 copy-start.1
  203.5 0.7 copy-done.5
  204.2 4.6 %shard_map.56 = bf16[8,512,256]{2,1,0:T(8,128)(2,1)} custom-call(bf16[512,256]{1,0:T(8,128)(2,1)} %bitcast.56, bf16[8,512,512]{2,1,0:T(8,128)(2,1)} %get-tuple-element.13.w_ref, bf16[8,512,256]{2,1,0:T(8,128)(2,1)} %shard_map.55.rest_0_), custom_call_target="tpu_custom_call" | custom-call | flops 1073741824 | bytes 10747904 | tf_op jit(solution)/shard_map/pallas_call | solution.py:64
  208.7 0.0 reduce-scatter.5.cloned.1.call-update
  208.8 40.3 %reduce-scatter.5.cloned.1.call-done = bf16[1,512,256]{2,1,0:T(8,128)(2,1)} async-done(((bf16[8,512,256]{2,1,0:T(8,128)(2,1)}), bf16[1,512,256]{2,1,0:T(8,128)(2,1)}) %reduce-scatter.5.cloned.1.call-update) | async-done | bytes 262160 | tf_op jit(solution)/shard_map/reduce_scatter | solution.py:121
  249.1 1.8 copy.21
  250.8 0.0 copy-done.1
  (3 shorter events, 0.1 us)
Async XLA Ops:
  6.5 80.1 %copy-start = (bf16[3,512,512]{2,1,0:T(8,128)(2,1)S(1)}, bf16[3,512,512]{2,1,0:T(8,128)(2,1)}, u32[]{:S(2)}) copy-start(bf16[3,512,512]{2,1,0:T(8,128)(2,1)} %param.6) | copy-start | bytes 4718596
  6.5 80.1 %all-gather.2.cloned.1.call-start = ((), (), s32[]{:S(2)}) async-start(), calls=%async_computation.3 | async-start | bytes 4718592 | tf_op jit(solution)/shard_map/all_gather | solution.py:84
  6.5 8.9 %collective-permute-start = (bf16[256,512]{1,0:T(8,128)(2,1)}, bf16[256,512]{1,0:T(8,128)(2,1)S(1)}, u32[]{:S(2)}, u32[]{:S(2)}) collective-permute-start(bf16[256,512]{1,0:T(8,128)(2,1)} %param.5), channel_id=1, source_target_pairs={{0,1},{1,0},{2,3},{3,2},{4,5},{5,4},{6,7},{7,6},{8,9},{9,8},{10,11... | collective-permute-start | bytes 786440 | tf_op jit(solution)/shard_map/ppermute | solution.py:80
  17.5 165.5 %reduce-scatter.3.cloned.1.call-start = ((), (), s32[]{:S(2)}) async-start(), calls=%async_computation.4 | async-start | bytes 13369344 | tf_op jit(solution)/shard_map/reduce_scatter | solution.py:96
  17.5 11.9 %collective-permute-start.1 = (bf16[512,512]{1,0:T(8,128)(2,1)}, bf16[512,512]{1,0:T(8,128)(2,1)S(1)}, u32[]{:S(2)}, u32[]{:S(2)}) collective-permute-start(bf16[512,512]{1,0:T(8,128)(2,1)} %param.9), channel_id=1, source_target_pairs={{1,0},{16,17},{3,2},{18,19},{5,4},{20,21},{7,6},{22,23},{9,8},{24,... | collective-permute-start | bytes 1572872 | tf_op jit(solution)/shard_map/ppermute | solution.py:81
  29.4 4.9 %collective-permute-start.2 = (bf16[512,512]{1,0:T(8,128)(2,1)S(1)}, bf16[512,512]{1,0:T(8,128)(2,1)S(1)}, u32[]{:S(2)}, u32[]{:S(2)}) collective-permute-start(bf16[512,512]{1,0:T(8,128)(2,1)S(1)} %collective-permute-done.1), channel_id=1, source_target_pairs={{0,16},{16,0},{1,17},{17,1},{2,18},{18,2},{3,19},{19,3},{4,20},{20... | collective-permute-start | bytes 1572872 | tf_op jit(solution)/shard_map/ppermute | solution.py:86
  98.5 3.7 %copy-start.6 = (f32[32,128]{1,0:T(8,128)S(1)}, f32[32,128]{1,0:T(8,128)}, u32[]{:S(2)}) copy-start(f32[32,128]{1,0:T(8,128)} %param.7) | copy-start | bytes 49156
  98.5 150.5 %reduce-scatter.5.cloned.1.call-start = ((), (), s32[]{:S(2)}) async-start(), calls=%async_computation.5 | async-start | bytes 2359296 | tf_op jit(solution)/shard_map/reduce_scatter | solution.py:121
  98.6 20.4 %collective-permute-start.3 = (bf16[8,512,512]{1,2,0:T(8,128)(2,1)}, bf16[8,512,512]{1,2,0:T(8,128)(2,1)}, u32[]{:S(2)}, u32[]{:S(2)}) collective-permute-start(bf16[8,512,512]{1,2,0:T(8,128)(2,1)} %all_to_all.5), channel_id=1, source_target_pairs={{0,16},{16,0},{1,17},{17,1},{2,18},{18,2},{3,19},{19,3},{4,20},{20... | collective-permute-start | bytes 12582920 | tf_op jit(solution)/shard_map/ppermute | solution.py:104
  112.1 2.5 slice-start
  115.9 3.1 %copy-start.2 = (bf16[8,512,512]{1,2,0:T(8,128)(2,1)S(1)}, bf16[8,512,512]{1,2,0:T(8,128)(2,1)}, u32[]{:S(2)}) copy-start(bf16[8,512,512]{1,2,0:T(8,128)(2,1)} %all_to_all.5) | copy-start | bytes 12582916
  184.1 6.0 %collective-permute-start.4 = (bf16[127,512]{0,1:T(8,128)(2,1)S(1)}, bf16[127,512]{0,1:T(8,128)(2,1)S(1)}, u32[]{:S(2)}, u32[]{:S(2)}) collective-permute-start(bf16[127,512]{0,1:T(8,128)(2,1)S(1)} %slice_bitcast_fusion.1), channel_id=1, source_target_pairs={{0,16},{16,32},{32,48},{48,64},{64,80},{80,96},{96,112},{112,128},... | collective-permute-start | bytes 390152 | tf_op jit(solution)/shard_map/ppermute | solution.py:23
  190.6 3.5 %copy-start.3 = (bf16[256,3,512]{0,2,1:T(8,128)(2,1)S(1)}, bf16[256,3,512]{0,2,1:T(8,128)(2,1)}, u32[]{:S(2)}) copy-start(bf16[256,3,512]{0,2,1:T(8,128)(2,1)} %reduce-scatter.3.cloned.1.call-done) | copy-start | bytes 2359300
  190.6 3.5 %copy-start.7 = (f32[512]{0:T(512)S(1)}, f32[512]{0:T(512)}, u32[]{:S(2)}) copy-start(f32[512]{0:T(512)} %param.8) | copy-start | bytes 6148
  194.3 2.6 %copy-start.4 = (bf16[256,512]{0,1:T(8,128)(2,1)}, bf16[256,512]{0,1:T(8,128)(2,1)S(1)}, u32[]{:S(2)}) copy-start(bf16[256,512]{0,1:T(8,128)(2,1)S(1)} %fusion.14) | copy-start | bytes 786436
  194.3 9.2 %collective-permute-start.5 = (bf16[256,512]{0,1:T(8,128)(2,1)S(1)}, bf16[256,512]{0,1:T(8,128)(2,1)S(1)}, u32[]{:S(2)}, u32[]{:S(2)}) collective-permute-start(bf16[256,512]{0,1:T(8,128)(2,1)S(1)} %fusion.14), channel_id=1, source_target_pairs={{0,1},{1,0},{2,3},{3,2},{4,5},{5,4},{6,7},{7,6},{8,9},{9,8},{10,11... | collective-permute-start | bytes 786440 | tf_op jit(solution)/shard_map/ppermute | solution.py:118
  203.5 0.7 copy-start.5
  203.5 47.4 %copy-start.1 = (bf16[3,512,512]{2,1,0:T(8,128)(2,1)S(1)}, bf16[3,512,512]{2,1,0:T(8,128)(2,1)}, u32[]{:S(2)}) copy-start(bf16[3,512,512]{2,1,0:T(8,128)(2,1)} %param.6) | copy-start | bytes 4718596
Sparse Core Ops, SparseCore 0:
  17.6 59.5 all-gather.1
  98.6 84.2 reduce-scatter.2
  208.9 40.1 reduce-scatter.4

commit v12 on v11

--- a/solution.py
+++ b/solution.py
@@ -79,8 +79,9 @@
     swap = [(0, 1), (1, 0)]
     tokens_x = lax.ppermute(tokens, "xhi", swap)
     weight_x = lax.ppermute(out_weight, ("core", "xhi"), [(1, 0), (2, 3)])
-    first = lax.axis_index("xhi") == 0
-    pair = jnp.where(first, jnp.concatenate([tokens, tokens_x]), jnp.concatenate([tokens_x, tokens]))
+    rows = tokens.shape[0]
+    ring = jnp.concatenate([tokens_x, tokens, tokens_x])
+    pair = lax.dynamic_slice_in_dim(ring, rows * (1 - lax.axis_index("xhi")), 2 * rows, 0)
     gathered = lax.all_gather(pair, "z", axis=0, tiled=True)
     same = lax.axis_index("xhi") == lax.axis_index("core")
     across = lax.ppermute(weight_x, "core", swap)

time: 261 us -> 262 us (level)
  no operation moved by 1% of the time
where the time goes in v12:
time: 262 us; the launch traced here: 258 us
  waiting for transfers between devices  117 us (45%)
  blocking collectives  51.7 us (20%)
  starting transfers between devices  21.1 us (8%)
  local copies, waits for them, and re-layouts  17.3 us (7%)
  matrix products  15 us (6%)
  other arithmetic  13.5 us (5%)
  between operations  13.3 us (5%)
  Pallas kernels  8.58 us (3%)
    reduce_scatter x1, waiting for transfers between devices, per_device(): lax.psum_scatter(jnp.einsum('rf,sfc->rsc', gathered, in_weight, preferred...  58.7 us
    all_to_all x1, blocking collectives, per_device(): plane = lax.all_to_all(spread, ('xlo', 'y'), 0, 0, tiled=True)  51.7 us
    reduce_scatter x1, waiting for transfers between devices, per_device(): summed = lax.psum_scatter(both, 'z', scatter_dimension=0, tiled=True)[0]  40.6 us
    dot_general x1, matrix products, per_device(): jnp.einsum('rf,sfc->rsc', gathered, in_weight, preferred_element_type=jnp...  11.8 us
    another operation x2, local copies, waits for them, and re-layouts, toeplitz_conv(): jnp.tile(w, (1, taps))[:, :taps * 2 * taps].reshape(groups, taps, 2 * taps)  9.78 us
    pallas_call x2, Pallas kernels, out_proj(): pl.pallas_call(out_proj_kernel, out_shape=jax.ShapeDtypeStruct((blocks, w...  8.58 us
    ppermute x1, waiting for transfers between devices, per_device(): weight_x = lax.ppermute(out_weight, ('core', 'xhi'), [(1, 0), (2, 3)])  6.39 us
    ppermute x1, starting transfers between devices, per_device(): weight_x = lax.ppermute(out_weight, ('core', 'xhi'), [(1, 0), (2, 3)])  5.54 us
  transfers between devices with their start and end apart: 9, of which 7 were waited for; matrix products, arithmetic and copies ran while one was open for 8% of the time, Pallas kernels for 2%

profile of v12, /device:TPU:1, one launch (start us, length us, event | category | flops | bytes accessed | tf_op | source)
XLA Modules:
  0.0 258.0 jit_solution(933619323190161581)
XLA Ops:
  6.5 0.0 copy-start
  6.5 0.0 all-gather.2.cloned.1.call-start
  6.5 3.6 %collective-permute-start = (bf16[256,512]{1,0:T(8,128)(2,1)}, bf16[256,512]{1,0:T(8,128)(2,1)S(1)}, u32[]{:S(2)}, u32[]{:S(2)}) collective-permute-start(bf16[256,512]{1,0:T(8,128)(2,1)} %param.5), channel_id=1, source_target_pairs={{0,1},{1,0},{2,3},{3,2},{4,5},{5,4},{6,7},{7,6},{8,9},{9,8},{10,11... | collective-permute-start | bytes 786440 | tf_op jit(solution)/shard_map/ppermute | solution.py:80
  10.1 5.3 %collective-permute-done = bf16[256,512]{1,0:T(8,128)(2,1)S(1)} collective-permute-done((bf16[256,512]{1,0:T(8,128)(2,1)}, bf16[256,512]{1,0:T(8,128)(2,1)S(1)}, u32[]{:S(2)}, u32[]{:S(2)}) %collective-permute-start) | collective-permute-done | bytes 262176 | tf_op jit(solution)/shard_map/ppermute | solution.py:80
  15.4 2.5 fusion.14
  17.9 0.0 all-gather.2.cloned.1.call-update
  17.9 0.0 reduce-scatter.3.cloned.1.call-start
  18.0 5.5 %collective-permute-start.1 = (bf16[512,512]{1,0:T(8,128)(2,1)}, bf16[512,512]{1,0:T(8,128)(2,1)S(1)}, u32[]{:S(2)}, u32[]{:S(2)}) collective-permute-start(bf16[512,512]{1,0:T(8,128)(2,1)} %param.9), channel_id=1, source_target_pairs={{1,0},{16,17},{3,2},{18,19},{5,4},{20,21},{7,6},{22,23},{9,8},{24,... | collective-permute-start | bytes 1572872 | tf_op jit(solution)/shard_map/ppermute | solution.py:81
  23.5 6.4 %collective-permute-done.1 = bf16[512,512]{1,0:T(8,128)(2,1)S(1)} collective-permute-done((bf16[512,512]{1,0:T(8,128)(2,1)}, bf16[512,512]{1,0:T(8,128)(2,1)S(1)}, u32[]{:S(2)}, u32[]{:S(2)}) %collective-permute-start.1) | collective-permute-done | bytes 524320 | tf_op jit(solution)/shard_map/ppermute | solution.py:81
  29.9 3.3 %collective-permute-start.2 = (bf16[512,512]{1,0:T(8,128)(2,1)S(1)}, bf16[512,512]{1,0:T(8,128)(2,1)S(1)}, u32[]{:S(2)}, u32[]{:S(2)}) collective-permute-start(bf16[512,512]{1,0:T(8,128)(2,1)S(1)} %collective-permute-done.1), channel_id=1, source_target_pairs={{0,16},{16,0},{1,17},{17,1},{2,18},{18,2},{3,19},{19,3},{4,20},{20... | collective-permute-start | bytes 1572872 | tf_op jit(solution)/shard_map/ppermute | solution.py:87
  33.3 1.5 collective-permute-done.2
  34.8 0.1 broadcast_select_fusion
  34.9 0.2 copy.14
  35.1 0.4 broadcast_in_dim.2
  35.4 51.7 %all_to_all.5 = bf16[8,512,512]{1,2,0:T(8,128)(2,1)} all-to-all(bf16[8,512,512]{1,2,0:T(8,128)(2,1)S(1)} %broadcast_in_dim.2), channel_id=1, replica_groups=mesh['xlo'=2,'y'=4,'core'=2,'z'=8,'xhi'=2] {'xlo','y'}, dimensions={0} | all-to-all | bytes 8388608 | tf_op jit(solution)/shard_map/all_to_all | solution.py:91
  87.1 0.0 all-gather.2.cloned.1.call-done
  87.1 0.0 copy-done
  87.1 11.8 %convolution_convert_fusion = bf16[4096,3,512]{0,2,1:T(8,128)(2,1)} fusion(bf16[3,512,512]{2,1,0:T(8,128)(2,1)S(1)} %copy-done, bf16[4096,512]{1,0:T(8,128)(2,1)} %all-gather.2.cloned.1.call-done), kind=kOutput, calls=%fused_computation | convolution fusion | flops 6448742400 | bytes 18350080 | tf_op jit(solution)/shard_map/rf,sfc->rsc/dot_general | solution.py:98
  99.0 0.0 copy-start.6
  99.0 0.0 reduce-scatter.3.cloned.1.call-update
  99.0 0.0 reduce-scatter.5.cloned.1.call-start
  99.0 3.6 %collective-permute-start.3 = (bf16[8,512,512]{1,2,0:T(8,128)(2,1)}, bf16[8,512,512]{1,2,0:T(8,128)(2,1)}, u32[]{:S(2)}, u32[]{:S(2)}) collective-permute-start(bf16[8,512,512]{1,2,0:T(8,128)(2,1)} %all_to_all.5), channel_id=1, source_target_pairs={{0,16},{16,0},{1,17},{17,1},{2,18},{18,2},{3,19},{19,3},{4,20},{20... | collective-permute-start | bytes 12582920 | tf_op jit(solution)/shard_map/ppermute | solution.py:105
  102.7 0.0 copy-done.6
  102.7 0.1 rev.3
  102.8 3.1 %tile.4 = f32[32,128,257]{2,1,0:T(8,128)} broadcast(f32[32,257]{1,0:T(8,128)S(1)} %pad.5), dimensions={0,2} | broadcast | bytes 4243584 | tf_op jit(solution)/shard_map/tile | solution.py:36
  105.9 6.7 %tile.10 = f32[32,32896]{1,0:T(8,128)} reshape(f32[32,128,257]{2,1,0:T(8,128)} %tile.4) | data formatting | bytes 8421376 | tf_op jit(solution)/shard_map/tile | solution.py:36
  112.6 0.0 slice-start
  112.6 2.5 slice-done
  115.1 1.3 copy.24
  116.3 0.0 copy-start.2
  116.4 3.1 %fusion = (bf16[32,128,256]{2,1,0:T(8,128)(2,1)}, bf16[32,128,256]{2,1,0:T(8,128)(2,1)}) fusion(f32[4,8,128,256]{3,2,1,0:T(8,128)S(1)} %copy.24), kind=kLoop, calls=%fused_computation.3 | loop fusion | flops 4194304 | bytes 8388608 | tf_op jit(solution)/shard_map/convert_element_type | solution.py:38
  119.4 0.0 collective-permute-done.3
  119.4 0.0 copy-done.2
  119.4 5.3 %select_bitcast_fusion = (bf16[8,512,512]{2,1,0:T(8,128)(2,1)}, bf16[8,512,512]{2,1,0:T(8,128)(2,1)}) fusion(bf16[8,512,512]{1,2,0:T(8,128)(2,1)} %collective-permute-done.3, bf16[8,512,512]{1,2,0:T(8,128)(2,1)S(1)} %copy-done.2, pred[]{:T(512)S(6)} %eq.3), kind=kLoop, calls=%fused_computation.9 | loop fusion | flops 4194304 | bytes 16777216 | tf_op jit(solution)/shard_map/transpose | solution.py:107
  124.7 58.7 %reduce-scatter.3.cloned.1.call-done = bf16[256,3,512]{0,2,1:T(8,128)(2,1)} async-done(((bf16[4096,3,512]{0,2,1:T(8,128)(2,1)}), bf16[256,3,512]{0,2,1:T(8,128)(2,1)}) %reduce-scatter.3.cloned.1.call-update) | async-done | bytes 786448 | tf_op jit(solution)/shard_map/reduce_scatter | solution.py:97
  183.4 1.1 multiply_convert_fusion
  184.5 0.1 slice_bitcast_fusion.1
  184.6 2.3 collective-permute-start.4
  186.9 1.1 fusion.19
  188.0 2.6 %collective-permute-done.4 = bf16[127,512]{0,1:T(8,128)(2,1)S(1)} collective-permute-done((bf16[127,512]{0,1:T(8,128)(2,1)S(1)}, bf16[127,512]{0,1:T(8,128)(2,1)S(1)}, u32[]{:S(2)}, u32[]{:S(2)}) %collective-permute-start.4) | collective-permute-done | bytes 130080 | tf_op jit(solution)/shard_map/ppermute | solution.py:23
  190.6 0.2 pad_maximum_fusion
  190.8 0.1 slice.41
  190.9 0.1 slice.43
  191.1 0.0 copy-start.3
  191.1 0.0 copy-start.7
  191.1 3.2 %fusion.5 = f32[2,128,32,16]{1,3,0,2:T(8,128)S(1)} fusion(bf16[32,128,256]{2,1,0:T(8,128)(2,1)} %get-tuple-element.15, bf16[32,128,256]{2,1,0:T(8,128)(2,1)} %get-tuple-element.16, bf16[2,128,32,16]{1,3,0,2:T(8,128)(2,1)S(1)} %copy.17, bf16[2,128,32,16]{1,3,0,2:T(8,128)(2,1)S(1)} %copy.16), kind=kOutput, calls=%fused_computation.11 | convolution fusion | flops 146800640 | bytes 5242880 | tf_op jit(solution)/shard_map/gts,isgc->itgc/dot_general | solution.py:41
  194.3 0.3 copy.20
  194.6 0.0 copy-done.3
  194.6 0.0 copy-done.7
  194.6 0.2 fusion.16
  194.8 0.0 copy-start.4
  194.8 2.6 %collective-permute-start.5 = (bf16[256,512]{0,1:T(8,128)(2,1)S(1)}, bf16[256,512]{0,1:T(8,128)(2,1)S(1)}, u32[]{:S(2)}, u32[]{:S(2)}) collective-permute-start(bf16[256,512]{0,1:T(8,128)(2,1)S(1)} %fusion.16), channel_id=1, source_target_pairs={{0,1},{1,0},{2,3},{3,2},{4,5},{5,4},{6,7},{7,6},{8,9},{9,8},{10,11... | collective-permute-start | bytes 786440 | tf_op jit(solution)/shard_map/ppermute | solution.py:119
  197.4 0.0 copy-done.4
  197.4 4.0 %shard_map.55.rest_0_ = bf16[8,512,256]{2,1,0:T(8,128)(2,1)} custom-call(bf16[512,256]{1,0:T(8,128)(2,1)} %bitcast.55, bf16[8,512,512]{2,1,0:T(8,128)(2,1)} %get-tuple-element.14.w_ref), custom_call_target="tpu_custom_call" | custom-call | flops 1073741824 | bytes 8650752 | tf_op jit(solution)/shard_map/pallas_call | solution.py:64
  201.4 2.3 collective-permute-done.5
  203.8 0.0 copy-start.5
  203.8 0.0 copy-start.1
  203.8 0.7 copy-done.5
  204.5 4.5 %shard_map.56 = bf16[8,512,256]{2,1,0:T(8,128)(2,1)} custom-call(bf16[512,256]{1,0:T(8,128)(2,1)} %bitcast.56, bf16[8,512,512]{2,1,0:T(8,128)(2,1)} %get-tuple-element.13.w_ref, bf16[8,512,256]{2,1,0:T(8,128)(2,1)} %shard_map.55.rest_0_), custom_call_target="tpu_custom_call" | custom-call | flops 1073741824 | bytes 10747904 | tf_op jit(solution)/shard_map/pallas_call | solution.py:64
  209.0 0.0 reduce-scatter.5.cloned.1.call-update
  209.0 40.6 %reduce-scatter.5.cloned.1.call-done = bf16[1,512,256]{2,1,0:T(8,128)(2,1)} async-done(((bf16[8,512,256]{2,1,0:T(8,128)(2,1)}), bf16[1,512,256]{2,1,0:T(8,128)(2,1)}) %reduce-scatter.5.cloned.1.call-update) | async-done | bytes 262160 | tf_op jit(solution)/shard_map/reduce_scatter | solution.py:122
  249.6 1.8 copy.21
  251.4 0.0 copy-done.1
  (3 shorter events, 0.1 us)
Async XLA Ops:
  6.5 80.6 %copy-start = (bf16[3,512,512]{2,1,0:T(8,128)(2,1)S(1)}, bf16[3,512,512]{2,1,0:T(8,128)(2,1)}, u32[]{:S(2)}) copy-start(bf16[3,512,512]{2,1,0:T(8,128)(2,1)} %param.6) | copy-start | bytes 4718596
  6.5 80.6 %all-gather.2.cloned.1.call-start = ((), (), s32[]{:S(2)}) async-start(), calls=%async_computation.3 | async-start | bytes 4718592 | tf_op jit(solution)/shard_map/all_gather | solution.py:85
  6.5 8.9 %collective-permute-start = (bf16[256,512]{1,0:T(8,128)(2,1)}, bf16[256,512]{1,0:T(8,128)(2,1)S(1)}, u32[]{:S(2)}, u32[]{:S(2)}) collective-permute-start(bf16[256,512]{1,0:T(8,128)(2,1)} %param.5), channel_id=1, source_target_pairs={{0,1},{1,0},{2,3},{3,2},{4,5},{5,4},{6,7},{7,6},{8,9},{9,8},{10,11... | collective-permute-start | bytes 786440 | tf_op jit(solution)/shard_map/ppermute | solution.py:80
  17.9 165.5 %reduce-scatter.3.cloned.1.call-start = ((), (), s32[]{:S(2)}) async-start(), calls=%async_computation.4 | async-start | bytes 13369344 | tf_op jit(solution)/shard_map/reduce_scatter | solution.py:97
  18.0 11.9 %collective-permute-start.1 = (bf16[512,512]{1,0:T(8,128)(2,1)}, bf16[512,512]{1,0:T(8,128)(2,1)S(1)}, u32[]{:S(2)}, u32[]{:S(2)}) collective-permute-start(bf16[512,512]{1,0:T(8,128)(2,1)} %param.9), channel_id=1, source_target_pairs={{1,0},{16,17},{3,2},{18,19},{5,4},{20,21},{7,6},{22,23},{9,8},{24,... | collective-permute-start | bytes 1572872 | tf_op jit(solution)/shard_map/ppermute | solution.py:81
  29.9 4.9 %collective-permute-start.2 = (bf16[512,512]{1,0:T(8,128)(2,1)S(1)}, bf16[512,512]{1,0:T(8,128)(2,1)S(1)}, u32[]{:S(2)}, u32[]{:S(2)}) collective-permute-start(bf16[512,512]{1,0:T(8,128)(2,1)S(1)} %collective-permute-done.1), channel_id=1, source_target_pairs={{0,16},{16,0},{1,17},{17,1},{2,18},{18,2},{3,19},{19,3},{4,20},{20... | collective-permute-start | bytes 1572872 | tf_op jit(solution)/shard_map/ppermute | solution.py:87
  99.0 3.7 %copy-start.6 = (f32[32,128]{1,0:T(8,128)S(1)}, f32[32,128]{1,0:T(8,128)}, u32[]{:S(2)}) copy-start(f32[32,128]{1,0:T(8,128)} %param.7) | copy-start | bytes 49156
  99.0 150.6 %reduce-scatter.5.cloned.1.call-start = ((), (), s32[]{:S(2)}) async-start(), calls=%async_computation.5 | async-start | bytes 2359296 | tf_op jit(solution)/shard_map/reduce_scatter | solution.py:122
  99.0 20.4 %collective-permute-start.3 = (bf16[8,512,512]{1,2,0:T(8,128)(2,1)}, bf16[8,512,512]{1,2,0:T(8,128)(2,1)}, u32[]{:S(2)}, u32[]{:S(2)}) collective-permute-start(bf16[8,512,512]{1,2,0:T(8,128)(2,1)} %all_to_all.5), channel_id=1, source_target_pairs={{0,16},{16,0},{1,17},{17,1},{2,18},{18,2},{3,19},{19,3},{4,20},{20... | collective-permute-start | bytes 12582920 | tf_op jit(solution)/shard_map/ppermute | solution.py:105
  112.6 2.5 slice-start
  116.3 3.1 %copy-start.2 = (bf16[8,512,512]{1,2,0:T(8,128)(2,1)S(1)}, bf16[8,512,512]{1,2,0:T(8,128)(2,1)}, u32[]{:S(2)}) copy-start(bf16[8,512,512]{1,2,0:T(8,128)(2,1)} %all_to_all.5) | copy-start | bytes 12582916
  184.6 6.0 %collective-permute-start.4 = (bf16[127,512]{0,1:T(8,128)(2,1)S(1)}, bf16[127,512]{0,1:T(8,128)(2,1)S(1)}, u32[]{:S(2)}, u32[]{:S(2)}) collective-permute-start(bf16[127,512]{0,1:T(8,128)(2,1)S(1)} %slice_bitcast_fusion.1), channel_id=1, source_target_pairs={{0,16},{16,32},{32,48},{48,64},{64,80},{80,96},{96,112},{112,128},... | collective-permute-start | bytes 390152 | tf_op jit(solution)/shard_map/ppermute | solution.py:23
  191.1 3.5 %copy-start.3 = (bf16[256,3,512]{0,2,1:T(8,128)(2,1)S(1)}, bf16[256,3,512]{0,2,1:T(8,128)(2,1)}, u32[]{:S(2)}) copy-start(bf16[256,3,512]{0,2,1:T(8,128)(2,1)} %reduce-scatter.3.cloned.1.call-done) | copy-start | bytes 2359300
  191.1 3.5 %copy-start.7 = (f32[512]{0:T(512)S(1)}, f32[512]{0:T(512)}, u32[]{:S(2)}) copy-start(f32[512]{0:T(512)} %param.8) | copy-start | bytes 6148
  194.8 2.6 %copy-start.4 = (bf16[256,512]{0,1:T(8,128)(2,1)}, bf16[256,512]{0,1:T(8,128)(2,1)S(1)}, u32[]{:S(2)}) copy-start(bf16[256,512]{0,1:T(8,128)(2,1)S(1)} %fusion.16) | copy-start | bytes 786436
  194.8 9.0 %collective-permute-start.5 = (bf16[256,512]{0,1:T(8,128)(2,1)S(1)}, bf16[256,512]{0,1:T(8,128)(2,1)S(1)}, u32[]{:S(2)}, u32[]{:S(2)}) collective-permute-start(bf16[256,512]{0,1:T(8,128)(2,1)S(1)} %fusion.16), channel_id=1, source_target_pairs={{0,1},{1,0},{2,3},{3,2},{4,5},{5,4},{6,7},{7,6},{8,9},{9,8},{10,11... | collective-permute-start | bytes 786440 | tf_op jit(solution)/shard_map/ppermute | solution.py:119
  203.8 0.7 copy-start.5
  203.8 47.7 %copy-start.1 = (bf16[3,512,512]{2,1,0:T(8,128)(2,1)S(1)}, bf16[3,512,512]{2,1,0:T(8,128)(2,1)}, u32[]{:S(2)}) copy-start(bf16[3,512,512]{2,1,0:T(8,128)(2,1)} %param.6) | copy-start | bytes 4718596
Sparse Core Ops, SparseCore 0:
  18.1 59.5 all-gather.1
  99.1 84.2 reduce-scatter.2
  209.1 40.4 reduce-scatter.4

commit v13 on v12

--- a/solution.py
+++ b/solution.py
@@ -49,13 +49,21 @@
     res = res.reshape(step, width, gt_ref.shape[1])
     if len(rest) == 2:
         res = res + rest[0][...].astype(jnp.float32)
-    out_ref[...] = res.astype(out_ref.dtype)
+        for jj in range(step):
+            out_ref[jj] = res[jj].T.astype(out_ref.dtype)
+    else:
+        out_ref[...] = res.astype(out_ref.dtype)
 
 
 def out_proj(gated_t, weight_t, acc=None, per_step=4):
     depth, rows = gated_t.shape
     blocks, width, _ = weight_t.shape
     block = pl.BlockSpec((per_step, width, rows), lambda i: (i, 0, 0))
+    shape = (blocks, width, rows)
+    out_block = block
+    if acc is not None:
+        shape = (blocks, rows, width)
+        out_block = pl.BlockSpec((per_step, rows, width), lambda i: (i, 0, 0))
     specs = [pl.BlockSpec((depth, rows), lambda i: (0, 0)), pl.BlockSpec((per_step, width, depth), lambda i: (i, 0, 0))]
     operands = [gated_t, weight_t]
     if acc is not None:
@@ -63,10 +71,10 @@
         operands.append(acc)
     return pl.pallas_call(
         out_proj_kernel,
-        out_shape=jax.ShapeDtypeStruct((blocks, width, rows), jnp.bfloat16),
+        out_shape=jax.ShapeDtypeStruct(shape, jnp.bfloat16),
         grid=(blocks // per_step,),
         in_specs=specs,
-        out_specs=block,
+        out_specs=out_block,
         cost_estimate=pl.CostEstimate(
             flops=2 * rows * depth * width * blocks,
             bytes_accessed=2 * (rows * depth + blocks * depth * width + len(operands) * blocks * rows * width),
@@ -120,7 +128,7 @@
     mine = out_proj(gated.T, keep_w)
     both = out_proj(recv_g.T, recv_w, mine)
     summed = lax.psum_scatter(both, "z", scatter_dimension=0, tiled=True)[0]
-    return summed.T
+    return summed
 
 
 def solution(mesh):

time: 262 us -> 260 us (level)
  no operation moved by 1% of the time
where the time goes in v13:
time: 260 us; the launch traced here: 256 us
  waiting for transfers between devices  117 us (45%)
  blocking collectives  51.7 us (20%)
  starting transfers between devices  21.1 us (8%)
  local copies, waits for them, and re-layouts  15.5 us (6%)
  matrix products  15 us (6%)
  other arithmetic  13.5 us (5%)
  between operations  13.3 us (5%)
  Pallas kernels  8.65 us (3%)
    reduce_scatter x1, waiting for transfers between devices, per_device(): lax.psum_scatter(jnp.einsum('rf,sfc->rsc', gathered, in_weight, preferred...  58.7 us
    all_to_all x1, blocking collectives, per_device(): plane = lax.all_to_all(spread, ('xlo', 'y'), 0, 0, tiled=True)  51.7 us
    reduce_scatter x1, waiting for transfers between devices, per_device(): summed = lax.psum_scatter(both, 'z', scatter_dimension=0, tiled=True)[0]  40.6 us
    dot_general x1, matrix products, per_device(): jnp.einsum('rf,sfc->rsc', gathered, in_weight, preferred_element_type=jnp...  11.8 us
    another operation x2, local copies, waits for them, and re-layouts, toeplitz_conv(): jnp.tile(w, (1, taps))[:, :taps * 2 * taps].reshape(groups, taps, 2 * taps)  9.78 us
    pallas_call x2, Pallas kernels, out_proj(): pl.pallas_call(out_proj_kernel, out_shape=jax.ShapeDtypeStruct(shape, jnp...  8.65 us
    ppermute x1, waiting for transfers between devices, per_device(): weight_x = lax.ppermute(out_weight, ('core', 'xhi'), [(1, 0), (2, 3)])  6.39 us
    ppermute x1, starting transfers between devices, per_device(): weight_x = lax.ppermute(out_weight, ('core', 'xhi'), [(1, 0), (2, 3)])  5.54 us
  transfers between devices with their start and end apart: 9, of which 7 were waited for; matrix products, arithmetic and copies ran while one was open for 8% of the time, Pallas kernels for 2%

profile of v13, /device:TPU:1, one launch (start us, length us, event | category | flops | bytes accessed | tf_op | source)
XLA Modules:
  0.0 256.2 jit_solution(5889553895784506312)
XLA Ops:
  6.5 0.0 copy-start
  6.5 0.0 all-gather.2.cloned.1.call-start
  6.5 3.6 %collective-permute-start = (bf16[256,512]{1,0:T(8,128)(2,1)}, bf16[256,512]{1,0:T(8,128)(2,1)S(1)}, u32[]{:S(2)}, u32[]{:S(2)}) collective-permute-start(bf16[256,512]{1,0:T(8,128)(2,1)} %param.5), channel_id=1, source_target_pairs={{0,1},{1,0},{2,3},{3,2},{4,5},{5,4},{6,7},{7,6},{8,9},{9,8},{10,11... | collective-permute-start | bytes 786440 | tf_op jit(solution)/shard_map/ppermute | solution.py:88
  10.1 5.3 %collective-permute-done = bf16[256,512]{1,0:T(8,128)(2,1)S(1)} collective-permute-done((bf16[256,512]{1,0:T(8,128)(2,1)}, bf16[256,512]{1,0:T(8,128)(2,1)S(1)}, u32[]{:S(2)}, u32[]{:S(2)}) %collective-permute-start) | collective-permute-done | bytes 262176 | tf_op jit(solution)/shard_map/ppermute | solution.py:88
  15.4 2.5 fusion.14
  17.9 0.0 all-gather.2.cloned.1.call-update
  17.9 0.0 reduce-scatter.3.cloned.1.call-start
  18.0 5.5 %collective-permute-start.1 = (bf16[512,512]{1,0:T(8,128)(2,1)}, bf16[512,512]{1,0:T(8,128)(2,1)S(1)}, u32[]{:S(2)}, u32[]{:S(2)}) collective-permute-start(bf16[512,512]{1,0:T(8,128)(2,1)} %param.9), channel_id=1, source_target_pairs={{1,0},{16,17},{3,2},{18,19},{5,4},{20,21},{7,6},{22,23},{9,8},{24,... | collective-permute-start | bytes 1572872 | tf_op jit(solution)/shard_map/ppermute | solution.py:89
  23.5 6.4 %collective-permute-done.1 = bf16[512,512]{1,0:T(8,128)(2,1)S(1)} collective-permute-done((bf16[512,512]{1,0:T(8,128)(2,1)}, bf16[512,512]{1,0:T(8,128)(2,1)S(1)}, u32[]{:S(2)}, u32[]{:S(2)}) %collective-permute-start.1) | collective-permute-done | bytes 524320 | tf_op jit(solution)/shard_map/ppermute | solution.py:89
  29.9 3.3 %collective-permute-start.2 = (bf16[512,512]{1,0:T(8,128)(2,1)S(1)}, bf16[512,512]{1,0:T(8,128)(2,1)S(1)}, u32[]{:S(2)}, u32[]{:S(2)}) collective-permute-start(bf16[512,512]{1,0:T(8,128)(2,1)S(1)} %collective-permute-done.1), channel_id=1, source_target_pairs={{0,16},{16,0},{1,17},{17,1},{2,18},{18,2},{3,19},{19,3},{4,20},{20... | collective-permute-start | bytes 1572872 | tf_op jit(solution)/shard_map/ppermute | solution.py:95
  33.3 1.5 collective-permute-done.2
  34.8 0.1 broadcast_select_fusion
  34.9 0.2 copy.13
  35.1 0.4 broadcast_in_dim.2
  35.4 51.7 %all_to_all.5 = bf16[8,512,512]{1,2,0:T(8,128)(2,1)} all-to-all(bf16[8,512,512]{1,2,0:T(8,128)(2,1)S(1)} %broadcast_in_dim.2), channel_id=1, replica_groups=mesh['xlo'=2,'y'=4,'core'=2,'z'=8,'xhi'=2] {'xlo','y'}, dimensions={0} | all-to-all | bytes 8388608 | tf_op jit(solution)/shard_map/all_to_all | solution.py:99
  87.1 0.0 all-gather.2.cloned.1.call-done
  87.1 0.0 copy-done
  87.1 11.8 %convolution_convert_fusion = bf16[4096,3,512]{0,2,1:T(8,128)(2,1)} fusion(bf16[3,512,512]{2,1,0:T(8,128)(2,1)S(1)} %copy-done, bf16[4096,512]{1,0:T(8,128)(2,1)} %all-gather.2.cloned.1.call-done), kind=kOutput, calls=%fused_computation | convolution fusion | flops 6448742400 | bytes 18350080 | tf_op jit(solution)/shard_map/rf,sfc->rsc/dot_general | solution.py:106
  99.0 0.0 copy-start.6
  99.0 0.0 reduce-scatter.3.cloned.1.call-update
  99.0 0.0 reduce-scatter.5.cloned.1.call-start
  99.0 3.6 %collective-permute-start.3 = (bf16[8,512,512]{1,2,0:T(8,128)(2,1)}, bf16[8,512,512]{1,2,0:T(8,128)(2,1)}, u32[]{:S(2)}, u32[]{:S(2)}) collective-permute-start(bf16[8,512,512]{1,2,0:T(8,128)(2,1)} %all_to_all.5), channel_id=1, source_target_pairs={{0,16},{16,0},{1,17},{17,1},{2,18},{18,2},{3,19},{19,3},{4,20},{20... | collective-permute-start | bytes 12582920 | tf_op jit(solution)/shard_map/ppermute | solution.py:113
  102.7 0.0 copy-done.6
  102.7 0.1 rev.3
  102.8 3.1 %tile.4 = f32[32,128,257]{2,1,0:T(8,128)} broadcast(f32[32,257]{1,0:T(8,128)S(1)} %pad.5), dimensions={0,2} | broadcast | bytes 4243584 | tf_op jit(solution)/shard_map/tile | solution.py:36
  105.9 6.7 %tile.10 = f32[32,32896]{1,0:T(8,128)} reshape(f32[32,128,257]{2,1,0:T(8,128)} %tile.4) | data formatting | bytes 8421376 | tf_op jit(solution)/shard_map/tile | solution.py:36
  112.6 0.0 slice-start
  112.6 2.5 slice-done
  115.1 1.3 copy.22
  116.3 0.0 copy-start.2
  116.4 3.1 %fusion = (bf16[32,128,256]{2,1,0:T(8,128)(2,1)}, bf16[32,128,256]{2,1,0:T(8,128)(2,1)}) fusion(f32[4,8,128,256]{3,2,1,0:T(8,128)S(1)} %copy.22), kind=kLoop, calls=%fused_computation.3 | loop fusion | flops 4194304 | bytes 8388608 | tf_op jit(solution)/shard_map/convert_element_type | solution.py:38
  119.4 0.0 collective-permute-done.3
  119.4 0.0 copy-done.2
  119.4 5.3 %select_bitcast_fusion = (bf16[8,512,512]{2,1,0:T(8,128)(2,1)}, bf16[8,512,512]{2,1,0:T(8,128)(2,1)}) fusion(bf16[8,512,512]{1,2,0:T(8,128)(2,1)} %collective-permute-done.3, bf16[8,512,512]{1,2,0:T(8,128)(2,1)S(1)} %copy-done.2, pred[]{:T(512)S(6)} %eq.3), kind=kLoop, calls=%fused_computation.9 | loop fusion | flops 4194304 | bytes 16777216 | tf_op jit(solution)/shard_map/transpose | solution.py:115
  124.7 58.7 %reduce-scatter.3.cloned.1.call-done = bf16[256,3,512]{0,2,1:T(8,128)(2,1)} async-done(((bf16[4096,3,512]{0,2,1:T(8,128)(2,1)}), bf16[256,3,512]{0,2,1:T(8,128)(2,1)}) %reduce-scatter.3.cloned.1.call-update) | async-done | bytes 786448 | tf_op jit(solution)/shard_map/reduce_scatter | solution.py:105
  183.4 1.1 multiply_convert_fusion
  184.5 0.1 slice_bitcast_fusion.1
  184.6 2.3 collective-permute-start.4
  186.9 1.1 fusion.19
  188.0 2.6 %collective-permute-done.4 = bf16[127,512]{0,1:T(8,128)(2,1)S(1)} collective-permute-done((bf16[127,512]{0,1:T(8,128)(2,1)S(1)}, bf16[127,512]{0,1:T(8,128)(2,1)S(1)}, u32[]{:S(2)}, u32[]{:S(2)}) %collective-permute-start.4) | collective-permute-done | bytes 130080 | tf_op jit(solution)/shard_map/ppermute | solution.py:23
  190.6 0.2 pad_maximum_fusion
  190.8 0.1 slice.41
  190.9 0.1 slice.43
  191.1 0.0 copy-start.3
  191.1 0.0 copy-start.7
  191.1 3.2 %fusion.5 = f32[2,128,32,16]{1,3,0,2:T(8,128)S(1)} fusion(bf16[32,128,256]{2,1,0:T(8,128)(2,1)} %get-tuple-element.15, bf16[32,128,256]{2,1,0:T(8,128)(2,1)} %get-tuple-element.16, bf16[2,128,32,16]{1,3,0,2:T(8,128)(2,1)S(1)} %copy.16, bf16[2,128,32,16]{1,3,0,2:T(8,128)(2,1)S(1)} %copy.15), kind=kOutput, calls=%fused_computation.11 | convolution fusion | flops 146800640 | bytes 5242880 | tf_op jit(solution)/shard_map/gts,isgc->itgc/dot_general | solution.py:41
  194.3 0.3 copy.19
  194.6 0.0 copy-done.3
  194.6 0.0 copy-done.7
  194.6 0.2 fusion.16
  194.8 0.0 copy-start.4
  194.8 2.6 %collective-permute-start.5 = (bf16[256,512]{0,1:T(8,128)(2,1)S(1)}, bf16[256,512]{0,1:T(8,128)(2,1)S(1)}, u32[]{:S(2)}, u32[]{:S(2)}) collective-permute-start(bf16[256,512]{0,1:T(8,128)(2,1)S(1)} %fusion.16), channel_id=1, source_target_pairs={{0,1},{1,0},{2,3},{3,2},{4,5},{5,4},{6,7},{7,6},{8,9},{9,8},{10,11... | collective-permute-start | bytes 786440 | tf_op jit(solution)/shard_map/ppermute | solution.py:127
  197.4 0.0 copy-done.4
  197.4 4.0 %shard_map.55.rest_0_ = bf16[8,512,256]{2,1,0:T(8,128)(2,1)} custom-call(bf16[512,256]{1,0:T(8,128)(2,1)} %bitcast.53, bf16[8,512,512]{2,1,0:T(8,128)(2,1)} %get-tuple-element.14.w_ref), custom_call_target="tpu_custom_call" | custom-call | flops 1073741824 | bytes 8650752 | tf_op jit(solution)/shard_map/pallas_call | solution.py:72
  201.4 2.3 collective-permute-done.5
  203.8 0.0 copy-start.5
  203.8 0.0 copy-start.1
  203.8 0.7 copy-done.5
  204.5 4.6 %shard_map.56 = bf16[8,256,512]{2,1,0:T(8,128)(2,1)} custom-call(bf16[512,256]{1,0:T(8,128)(2,1)} %bitcast.54, bf16[8,512,512]{2,1,0:T(8,128)(2,1)} %get-tuple-element.13.w_ref, bf16[8,512,256]{2,1,0:T(8,128)(2,1)} %shard_map.55.rest_0_), custom_call_target="tpu_custom_call" | custom-call | flops 1073741824 | bytes 10747904 | tf_op jit(solution)/shard_map/pallas_call | solution.py:72
  209.1 0.0 reduce-scatter.5.cloned.1.call-update
  209.1 40.6 %reduce-scatter.5.cloned.1.call-done = bf16[1,256,512]{2,1,0:T(8,128)(2,1)} async-done(((bf16[8,256,512]{2,1,0:T(8,128)(2,1)}), bf16[1,256,512]{2,1,0:T(8,128)(2,1)}) %reduce-scatter.5.cloned.1.call-update) | async-done | bytes 262160 | tf_op jit(solution)/shard_map/reduce_scatter | solution.py:130
  249.7 0.0 copy-done.1
  (3 shorter events, 0.1 us)
Async XLA Ops:
  6.5 80.6 %copy-start = (bf16[3,512,512]{2,1,0:T(8,128)(2,1)S(1)}, bf16[3,512,512]{2,1,0:T(8,128)(2,1)}, u32[]{:S(2)}) copy-start(bf16[3,512,512]{2,1,0:T(8,128)(2,1)} %param.6) | copy-start | bytes 4718596
  6.5 80.6 %all-gather.2.cloned.1.call-start = ((), (), s32[]{:S(2)}) async-start(), calls=%async_computation.3 | async-start | bytes 4718592 | tf_op jit(solution)/shard_map/all_gather | solution.py:93
  6.5 8.9 %collective-permute-start = (bf16[256,512]{1,0:T(8,128)(2,1)}, bf16[256,512]{1,0:T(8,128)(2,1)S(1)}, u32[]{:S(2)}, u32[]{:S(2)}) collective-permute-start(bf16[256,512]{1,0:T(8,128)(2,1)} %param.5), channel_id=1, source_target_pairs={{0,1},{1,0},{2,3},{3,2},{4,5},{5,4},{6,7},{7,6},{8,9},{9,8},{10,11... | collective-permute-start | bytes 786440 | tf_op jit(solution)/shard_map/ppermute | solution.py:88
  17.9 165.5 %reduce-scatter.3.cloned.1.call-start = ((), (), s32[]{:S(2)}) async-start(), calls=%async_computation.4 | async-start | bytes 13369344 | tf_op jit(solution)/shard_map/reduce_scatter | solution.py:105
  18.0 11.9 %collective-permute-start.1 = (bf16[512,512]{1,0:T(8,128)(2,1)}, bf16[512,512]{1,0:T(8,128)(2,1)S(1)}, u32[]{:S(2)}, u32[]{:S(2)}) collective-permute-start(bf16[512,512]{1,0:T(8,128)(2,1)} %param.9), channel_id=1, source_target_pairs={{1,0},{16,17},{3,2},{18,19},{5,4},{20,21},{7,6},{22,23},{9,8},{24,... | collective-permute-start | bytes 1572872 | tf_op jit(solution)/shard_map/ppermute | solution.py:89
  29.9 4.9 %collective-permute-start.2 = (bf16[512,512]{1,0:T(8,128)(2,1)S(1)}, bf16[512,512]{1,0:T(8,128)(2,1)S(1)}, u32[]{:S(2)}, u32[]{:S(2)}) collective-permute-start(bf16[512,512]{1,0:T(8,128)(2,1)S(1)} %collective-permute-done.1), channel_id=1, source_target_pairs={{0,16},{16,0},{1,17},{17,1},{2,18},{18,2},{3,19},{19,3},{4,20},{20... | collective-permute-start | bytes 1572872 | tf_op jit(solution)/shard_map/ppermute | solution.py:95
  99.0 3.7 %copy-start.6 = (f32[32,128]{1,0:T(8,128)S(1)}, f32[32,128]{1,0:T(8,128)}, u32[]{:S(2)}) copy-start(f32[32,128]{1,0:T(8,128)} %param.7) | copy-start | bytes 49156
  99.0 150.7 %reduce-scatter.5.cloned.1.call-start = ((), (), s32[]{:S(2)}) async-start(), calls=%async_computation.5 | async-start | bytes 2359296 | tf_op jit(solution)/shard_map/reduce_scatter | solution.py:130
  99.0 20.4 %collective-permute-start.3 = (bf16[8,512,512]{1,2,0:T(8,128)(2,1)}, bf16[8,512,512]{1,2,0:T(8,128)(2,1)}, u32[]{:S(2)}, u32[]{:S(2)}) collective-permute-start(bf16[8,512,512]{1,2,0:T(8,128)(2,1)} %all_to_all.5), channel_id=1, source_target_pairs={{0,16},{16,0},{1,17},{17,1},{2,18},{18,2},{3,19},{19,3},{4,20},{20... | collective-permute-start | bytes 12582920 | tf_op jit(solution)/shard_map/ppermute | solution.py:113
  112.6 2.5 slice-start
  116.3 3.1 %copy-start.2 = (bf16[8,512,512]{1,2,0:T(8,128)(2,1)S(1)}, bf16[8,512,512]{1,2,0:T(8,128)(2,1)}, u32[]{:S(2)}) copy-start(bf16[8,512,512]{1,2,0:T(8,128)(2,1)} %all_to_all.5) | copy-start | bytes 12582916
  184.6 6.0 %collective-permute-start.4 = (bf16[127,512]{0,1:T(8,128)(2,1)S(1)}, bf16[127,512]{0,1:T(8,128)(2,1)S(1)}, u32[]{:S(2)}, u32[]{:S(2)}) collective-permute-start(bf16[127,512]{0,1:T(8,128)(2,1)S(1)} %slice_bitcast_fusion.1), channel_id=1, source_target_pairs={{0,16},{16,32},{32,48},{48,64},{64,80},{80,96},{96,112},{112,128},... | collective-permute-start | bytes 390152 | tf_op jit(solution)/shard_map/ppermute | solution.py:23
  191.1 3.5 %copy-start.3 = (bf16[256,3,512]{0,2,1:T(8,128)(2,1)S(1)}, bf16[256,3,512]{0,2,1:T(8,128)(2,1)}, u32[]{:S(2)}) copy-start(bf16[256,3,512]{0,2,1:T(8,128)(2,1)} %reduce-scatter.3.cloned.1.call-done) | copy-start | bytes 2359300
  191.1 3.5 %copy-start.7 = (f32[512]{0:T(512)S(1)}, f32[512]{0:T(512)}, u32[]{:S(2)}) copy-start(f32[512]{0:T(512)} %param.8) | copy-start | bytes 6148
  194.8 2.6 %copy-start.4 = (bf16[256,512]{0,1:T(8,128)(2,1)}, bf16[256,512]{0,1:T(8,128)(2,1)S(1)}, u32[]{:S(2)}) copy-start(bf16[256,512]{0,1:T(8,128)(2,1)S(1)} %fusion.16) | copy-start | bytes 786436
  194.8 9.0 %collective-permute-start.5 = (bf16[256,512]{0,1:T(8,128)(2,1)S(1)}, bf16[256,512]{0,1:T(8,128)(2,1)S(1)}, u32[]{:S(2)}, u32[]{:S(2)}) collective-permute-start(bf16[256,512]{0,1:T(8,128)(2,1)S(1)} %fusion.16), channel_id=1, source_target_pairs={{0,1},{1,0},{2,3},{3,2},{4,5},{5,4},{6,7},{7,6},{8,9},{9,8},{10,11... | collective-permute-start | bytes 786440 | tf_op jit(solution)/shard_map/ppermute | solution.py:127
  203.8 0.7 copy-start.5
  203.8 46.0 %copy-start.1 = (bf16[3,512,512]{2,1,0:T(8,128)(2,1)S(1)}, bf16[3,512,512]{2,1,0:T(8,128)(2,1)}, u32[]{:S(2)}) copy-start(bf16[3,512,512]{2,1,0:T(8,128)(2,1)} %param.6) | copy-start | bytes 4718596
Sparse Core Ops, SparseCore 0:
  18.1 59.5 all-gather.1
  99.1 84.2 reduce-scatter.2
  209.2 40.4 reduce-scatter.4

commit v14 on v13

--- a/solution.py
+++ b/solution.py
@@ -55,7 +55,7 @@
         out_ref[...] = res.astype(out_ref.dtype)
 
 
-def out_proj(gated_t, weight_t, acc=None, per_step=4):
+def out_proj(gated_t, weight_t, acc=None, per_step=2):
     depth, rows = gated_t.shape
     blocks, width, _ = weight_t.shape
     block = pl.BlockSpec((per_step, width, rows), lambda i: (i, 0, 0))

time: 260 us -> 261 us (level)
  no operation moved by 1% of the time
where the time goes in v14:
time: 261 us; the launch traced here: 257 us
  waiting for transfers between devices  116 us (44%)
  blocking collectives  51.7 us (20%)
  starting transfers between devices  21.1 us (8%)
  local copies, waits for them, and re-layouts  15.5 us (6%)
  matrix products  15 us (6%)
  other arithmetic  13.5 us (5%)
  between operations  13.3 us (5%)
  Pallas kernels  10.6 us (4%)
    reduce_scatter x1, waiting for transfers between devices, per_device(): lax.psum_scatter(jnp.einsum('rf,sfc->rsc', gathered, in_weight, preferred...  58.7 us
    all_to_all x1, blocking collectives, per_device(): plane = lax.all_to_all(spread, ('xlo', 'y'), 0, 0, tiled=True)  51.7 us
    reduce_scatter x1, waiting for transfers between devices, per_device(): summed = lax.psum_scatter(both, 'z', scatter_dimension=0, tiled=True)[0]  40.6 us
    dot_general x1, matrix products, per_device(): jnp.einsum('rf,sfc->rsc', gathered, in_weight, preferred_element_type=jnp...  11.8 us
    pallas_call x2, Pallas kernels, out_proj(): pl.pallas_call(out_proj_kernel, out_shape=jax.ShapeDtypeStruct(shape, jnp...  10.6 us
    another operation x2, local copies, waits for them, and re-layouts, toeplitz_conv(): jnp.tile(w, (1, taps))[:, :taps * 2 * taps].reshape(groups, taps, 2 * taps)  9.78 us
    ppermute x1, waiting for transfers between devices, per_device(): weight_x = lax.ppermute(out_weight, ('core', 'xhi'), [(1, 0), (2, 3)])  6.39 us
    ppermute x1, starting transfers between devices, per_device(): weight_x = lax.ppermute(out_weight, ('core', 'xhi'), [(1, 0), (2, 3)])  5.54 us
  transfers between devices with their start and end apart: 9, of which 7 were waited for; matrix products, arithmetic and copies ran while one was open for 8% of the time, Pallas kernels for 2%

profile of v14, /device:TPU:1, one launch (start us, length us, event | category | flops | bytes accessed | tf_op | source)
XLA Modules:
  0.0 257.2 jit_solution(7519764087677052981)
XLA Ops:
  6.5 0.0 copy-start
  6.5 0.0 all-gather.2.cloned.1.call-start
  6.5 3.6 %collective-permute-start = (bf16[256,512]{1,0:T(8,128)(2,1)}, bf16[256,512]{1,0:T(8,128)(2,1)S(1)}, u32[]{:S(2)}, u32[]{:S(2)}) collective-permute-start(bf16[256,512]{1,0:T(8,128)(2,1)} %param.5), channel_id=1, source_target_pairs={{0,1},{1,0},{2,3},{3,2},{4,5},{5,4},{6,7},{7,6},{8,9},{9,8},{10,11... | collective-permute-start | bytes 786440 | tf_op jit(solution)/shard_map/ppermute | solution.py:88
  10.1 5.3 %collective-permute-done = bf16[256,512]{1,0:T(8,128)(2,1)S(1)} collective-permute-done((bf16[256,512]{1,0:T(8,128)(2,1)}, bf16[256,512]{1,0:T(8,128)(2,1)S(1)}, u32[]{:S(2)}, u32[]{:S(2)}) %collective-permute-start) | collective-permute-done | bytes 262176 | tf_op jit(solution)/shard_map/ppermute | solution.py:88
  15.4 2.5 fusion.14
  17.9 0.0 all-gather.2.cloned.1.call-update
  17.9 0.0 reduce-scatter.3.cloned.1.call-start
  18.0 5.5 %collective-permute-start.1 = (bf16[512,512]{1,0:T(8,128)(2,1)}, bf16[512,512]{1,0:T(8,128)(2,1)S(1)}, u32[]{:S(2)}, u32[]{:S(2)}) collective-permute-start(bf16[512,512]{1,0:T(8,128)(2,1)} %param.9), channel_id=1, source_target_pairs={{1,0},{16,17},{3,2},{18,19},{5,4},{20,21},{7,6},{22,23},{9,8},{24,... | collective-permute-start | bytes 1572872 | tf_op jit(solution)/shard_map/ppermute | solution.py:89
  23.5 6.4 %collective-permute-done.1 = bf16[512,512]{1,0:T(8,128)(2,1)S(1)} collective-permute-done((bf16[512,512]{1,0:T(8,128)(2,1)}, bf16[512,512]{1,0:T(8,128)(2,1)S(1)}, u32[]{:S(2)}, u32[]{:S(2)}) %collective-permute-start.1) | collective-permute-done | bytes 524320 | tf_op jit(solution)/shard_map/ppermute | solution.py:89
  29.9 3.3 %collective-permute-start.2 = (bf16[512,512]{1,0:T(8,128)(2,1)S(1)}, bf16[512,512]{1,0:T(8,128)(2,1)S(1)}, u32[]{:S(2)}, u32[]{:S(2)}) collective-permute-start(bf16[512,512]{1,0:T(8,128)(2,1)S(1)} %collective-permute-done.1), channel_id=1, source_target_pairs={{0,16},{16,0},{1,17},{17,1},{2,18},{18,2},{3,19},{19,3},{4,20},{20... | collective-permute-start | bytes 1572872 | tf_op jit(solution)/shard_map/ppermute | solution.py:95
  33.3 1.5 collective-permute-done.2
  34.8 0.1 broadcast_select_fusion
  34.9 0.2 copy.13
  35.1 0.4 broadcast_in_dim.2
  35.4 51.7 %all_to_all.5 = bf16[8,512,512]{1,2,0:T(8,128)(2,1)} all-to-all(bf16[8,512,512]{1,2,0:T(8,128)(2,1)S(1)} %broadcast_in_dim.2), channel_id=1, replica_groups=mesh['xlo'=2,'y'=4,'core'=2,'z'=8,'xhi'=2] {'xlo','y'}, dimensions={0} | all-to-all | bytes 8388608 | tf_op jit(solution)/shard_map/all_to_all | solution.py:99
  87.1 0.0 all-gather.2.cloned.1.call-done
  87.1 0.0 copy-done
  87.1 11.8 %convolution_convert_fusion = bf16[4096,3,512]{0,2,1:T(8,128)(2,1)} fusion(bf16[3,512,512]{2,1,0:T(8,128)(2,1)S(1)} %copy-done, bf16[4096,512]{1,0:T(8,128)(2,1)} %all-gather.2.cloned.1.call-done), kind=kOutput, calls=%fused_computation | convolution fusion | flops 6448742400 | bytes 18350080 | tf_op jit(solution)/shard_map/rf,sfc->rsc/dot_general | solution.py:106
  99.0 0.0 copy-start.6
  99.0 0.0 reduce-scatter.3.cloned.1.call-update
  99.0 0.0 reduce-scatter.5.cloned.1.call-start
  99.0 3.6 %collective-permute-start.3 = (bf16[8,512,512]{1,2,0:T(8,128)(2,1)}, bf16[8,512,512]{1,2,0:T(8,128)(2,1)}, u32[]{:S(2)}, u32[]{:S(2)}) collective-permute-start(bf16[8,512,512]{1,2,0:T(8,128)(2,1)} %all_to_all.5), channel_id=1, source_target_pairs={{0,16},{16,0},{1,17},{17,1},{2,18},{18,2},{3,19},{19,3},{4,20},{20... | collective-permute-start | bytes 12582920 | tf_op jit(solution)/shard_map/ppermute | solution.py:113
  102.7 0.0 copy-done.6
  102.7 0.1 rev.3
  102.8 3.1 %tile.4 = f32[32,128,257]{2,1,0:T(8,128)} broadcast(f32[32,257]{1,0:T(8,128)S(1)} %pad.5), dimensions={0,2} | broadcast | bytes 4243584 | tf_op jit(solution)/shard_map/tile | solution.py:36
  105.9 6.7 %tile.10 = f32[32,32896]{1,0:T(8,128)} reshape(f32[32,128,257]{2,1,0:T(8,128)} %tile.4) | data formatting | bytes 8421376 | tf_op jit(solution)/shard_map/tile | solution.py:36
  112.6 0.0 slice-start
  112.6 2.5 slice-done
  115.1 1.3 copy.22
  116.3 0.0 copy-start.2
  116.4 3.1 %fusion = (bf16[32,128,256]{2,1,0:T(8,128)(2,1)}, bf16[32,128,256]{2,1,0:T(8,128)(2,1)}) fusion(f32[4,8,128,256]{3,2,1,0:T(8,128)S(1)} %copy.22), kind=kLoop, calls=%fused_computation.3 | loop fusion | flops 4194304 | bytes 8388608 | tf_op jit(solution)/shard_map/convert_element_type | solution.py:38
  119.4 0.0 collective-permute-done.3
  119.4 0.0 copy-done.2
  119.4 5.3 %select_bitcast_fusion = (bf16[8,512,512]{2,1,0:T(8,128)(2,1)}, bf16[8,512,512]{2,1,0:T(8,128)(2,1)}) fusion(bf16[8,512,512]{1,2,0:T(8,128)(2,1)} %collective-permute-done.3, bf16[8,512,512]{1,2,0:T(8,128)(2,1)S(1)} %copy-done.2, pred[]{:T(512)S(6)} %eq.3), kind=kLoop, calls=%fused_computation.9 | loop fusion | flops 4194304 | bytes 16777216 | tf_op jit(solution)/shard_map/transpose | solution.py:115
  124.7 58.7 %reduce-scatter.3.cloned.1.call-done = bf16[256,3,512]{0,2,1:T(8,128)(2,1)} async-done(((bf16[4096,3,512]{0,2,1:T(8,128)(2,1)}), bf16[256,3,512]{0,2,1:T(8,128)(2,1)}) %reduce-scatter.3.cloned.1.call-update) | async-done | bytes 786448 | tf_op jit(solution)/shard_map/reduce_scatter | solution.py:105
  183.4 1.1 multiply_convert_fusion
  184.5 0.1 slice_bitcast_fusion.1
  184.6 2.3 collective-permute-start.4
  186.9 1.1 fusion.19
  188.0 2.6 %collective-permute-done.4 = bf16[127,512]{0,1:T(8,128)(2,1)S(1)} collective-permute-done((bf16[127,512]{0,1:T(8,128)(2,1)S(1)}, bf16[127,512]{0,1:T(8,128)(2,1)S(1)}, u32[]{:S(2)}, u32[]{:S(2)}) %collective-permute-start.4) | collective-permute-done | bytes 130080 | tf_op jit(solution)/shard_map/ppermute | solution.py:23
  190.6 0.2 pad_maximum_fusion
  190.8 0.1 slice.41
  190.9 0.1 slice.43
  191.1 0.0 copy-start.3
  191.1 0.0 copy-start.7
  191.1 3.2 %fusion.5 = f32[2,128,32,16]{1,3,0,2:T(8,128)S(1)} fusion(bf16[32,128,256]{2,1,0:T(8,128)(2,1)} %get-tuple-element.15, bf16[32,128,256]{2,1,0:T(8,128)(2,1)} %get-tuple-element.16, bf16[2,128,32,16]{1,3,0,2:T(8,128)(2,1)S(1)} %copy.16, bf16[2,128,32,16]{1,3,0,2:T(8,128)(2,1)S(1)} %copy.15), kind=kOutput, calls=%fused_computation.11 | convolution fusion | flops 146800640 | bytes 5242880 | tf_op jit(solution)/shard_map/gts,isgc->itgc/dot_general | solution.py:41
  194.3 0.3 copy.19
  194.6 0.0 copy-done.3
  194.6 0.0 copy-done.7
  194.6 0.2 fusion.16
  194.8 0.0 copy-start.4
  194.8 2.6 %collective-permute-start.5 = (bf16[256,512]{0,1:T(8,128)(2,1)S(1)}, bf16[256,512]{0,1:T(8,128)(2,1)S(1)}, u32[]{:S(2)}, u32[]{:S(2)}) collective-permute-start(bf16[256,512]{0,1:T(8,128)(2,1)S(1)} %fusion.16), channel_id=1, source_target_pairs={{0,1},{1,0},{2,3},{3,2},{4,5},{5,4},{6,7},{7,6},{8,9},{9,8},{10,11... | collective-permute-start | bytes 786440 | tf_op jit(solution)/shard_map/ppermute | solution.py:127
  197.4 0.0 copy-done.4
  197.4 5.1 %shard_map.55.rest_0_ = bf16[8,512,256]{2,1,0:T(8,128)(2,1)} custom-call(bf16[512,256]{1,0:T(8,128)(2,1)} %bitcast.53, bf16[8,512,512]{2,1,0:T(8,128)(2,1)} %get-tuple-element.14.w_ref), custom_call_target="tpu_custom_call" | custom-call | flops 1073741824 | bytes 8650752 | tf_op jit(solution)/shard_map/pallas_call | solution.py:72
  202.5 1.3 collective-permute-done.5
  203.8 0.0 copy-start.5
  203.8 0.0 copy-start.1
  203.8 0.7 copy-done.5
  204.5 5.6 %shard_map.56 = bf16[8,256,512]{2,1,0:T(8,128)(2,1)} custom-call(bf16[512,256]{1,0:T(8,128)(2,1)} %bitcast.54, bf16[8,512,512]{2,1,0:T(8,128)(2,1)} %get-tuple-element.13.w_ref, bf16[8,512,256]{2,1,0:T(8,128)(2,1)} %shard_map.55.rest_0_), custom_call_target="tpu_custom_call" | custom-call | flops 1073741824 | bytes 10747904 | tf_op jit(solution)/shard_map/pallas_call | solution.py:72
  210.0 0.0 reduce-scatter.5.cloned.1.call-update
  210.1 40.6 %reduce-scatter.5.cloned.1.call-done = bf16[1,256,512]{2,1,0:T(8,128)(2,1)} async-done(((bf16[8,256,512]{2,1,0:T(8,128)(2,1)}), bf16[1,256,512]{2,1,0:T(8,128)(2,1)}) %reduce-scatter.5.cloned.1.call-update) | async-done | bytes 262160 | tf_op jit(solution)/shard_map/reduce_scatter | solution.py:130
  250.7 0.0 copy-done.1
  (3 shorter events, 0.1 us)
Async XLA Ops:
  6.5 80.6 %copy-start = (bf16[3,512,512]{2,1,0:T(8,128)(2,1)S(1)}, bf16[3,512,512]{2,1,0:T(8,128)(2,1)}, u32[]{:S(2)}) copy-start(bf16[3,512,512]{2,1,0:T(8,128)(2,1)} %param.6) | copy-start | bytes 4718596
  6.5 80.6 %all-gather.2.cloned.1.call-start = ((), (), s32[]{:S(2)}) async-start(), calls=%async_computation.3 | async-start | bytes 4718592 | tf_op jit(solution)/shard_map/all_gather | solution.py:93
  6.5 8.9 %collective-permute-start = (bf16[256,512]{1,0:T(8,128)(2,1)}, bf16[256,512]{1,0:T(8,128)(2,1)S(1)}, u32[]{:S(2)}, u32[]{:S(2)}) collective-permute-start(bf16[256,512]{1,0:T(8,128)(2,1)} %param.5), channel_id=1, source_target_pairs={{0,1},{1,0},{2,3},{3,2},{4,5},{5,4},{6,7},{7,6},{8,9},{9,8},{10,11... | collective-permute-start | bytes 786440 | tf_op jit(solution)/shard_map/ppermute | solution.py:88
  17.9 165.5 %reduce-scatter.3.cloned.1.call-start = ((), (), s32[]{:S(2)}) async-start(), calls=%async_computation.4 | async-start | bytes 13369344 | tf_op jit(solution)/shard_map/reduce_scatter | solution.py:105
  18.0 11.9 %collective-permute-start.1 = (bf16[512,512]{1,0:T(8,128)(2,1)}, bf16[512,512]{1,0:T(8,128)(2,1)S(1)}, u32[]{:S(2)}, u32[]{:S(2)}) collective-permute-start(bf16[512,512]{1,0:T(8,128)(2,1)} %param.9), channel_id=1, source_target_pairs={{1,0},{16,17},{3,2},{18,19},{5,4},{20,21},{7,6},{22,23},{9,8},{24,... | collective-permute-start | bytes 1572872 | tf_op jit(solution)/shard_map/ppermute | solution.py:89
  29.9 4.9 %collective-permute-start.2 = (bf16[512,512]{1,0:T(8,128)(2,1)S(1)}, bf16[512,512]{1,0:T(8,128)(2,1)S(1)}, u32[]{:S(2)}, u32[]{:S(2)}) collective-permute-start(bf16[512,512]{1,0:T(8,128)(2,1)S(1)} %collective-permute-done.1), channel_id=1, source_target_pairs={{0,16},{16,0},{1,17},{17,1},{2,18},{18,2},{3,19},{19,3},{4,20},{20... | collective-permute-start | bytes 1572872 | tf_op jit(solution)/shard_map/ppermute | solution.py:95
  99.0 3.7 %copy-start.6 = (f32[32,128]{1,0:T(8,128)S(1)}, f32[32,128]{1,0:T(8,128)}, u32[]{:S(2)}) copy-start(f32[32,128]{1,0:T(8,128)} %param.7) | copy-start | bytes 49156
  99.0 151.7 %reduce-scatter.5.cloned.1.call-start = ((), (), s32[]{:S(2)}) async-start(), calls=%async_computation.5 | async-start | bytes 2359296 | tf_op jit(solution)/shard_map/reduce_scatter | solution.py:130
  99.0 20.4 %collective-permute-start.3 = (bf16[8,512,512]{1,2,0:T(8,128)(2,1)}, bf16[8,512,512]{1,2,0:T(8,128)(2,1)}, u32[]{:S(2)}, u32[]{:S(2)}) collective-permute-start(bf16[8,512,512]{1,2,0:T(8,128)(2,1)} %all_to_all.5), channel_id=1, source_target_pairs={{0,16},{16,0},{1,17},{17,1},{2,18},{18,2},{3,19},{19,3},{4,20},{20... | collective-permute-start | bytes 12582920 | tf_op jit(solution)/shard_map/ppermute | solution.py:113
  112.6 2.5 slice-start
  116.3 3.1 %copy-start.2 = (bf16[8,512,512]{1,2,0:T(8,128)(2,1)S(1)}, bf16[8,512,512]{1,2,0:T(8,128)(2,1)}, u32[]{:S(2)}) copy-start(bf16[8,512,512]{1,2,0:T(8,128)(2,1)} %all_to_all.5) | copy-start | bytes 12582916
  184.6 6.0 %collective-permute-start.4 = (bf16[127,512]{0,1:T(8,128)(2,1)S(1)}, bf16[127,512]{0,1:T(8,128)(2,1)S(1)}, u32[]{:S(2)}, u32[]{:S(2)}) collective-permute-start(bf16[127,512]{0,1:T(8,128)(2,1)S(1)} %slice_bitcast_fusion.1), channel_id=1, source_target_pairs={{0,16},{16,32},{32,48},{48,64},{64,80},{80,96},{96,112},{112,128},... | collective-permute-start | bytes 390152 | tf_op jit(solution)/shard_map/ppermute | solution.py:23
  191.1 3.5 %copy-start.3 = (bf16[256,3,512]{0,2,1:T(8,128)(2,1)S(1)}, bf16[256,3,512]{0,2,1:T(8,128)(2,1)}, u32[]{:S(2)}) copy-start(bf16[256,3,512]{0,2,1:T(8,128)(2,1)} %reduce-scatter.3.cloned.1.call-done) | copy-start | bytes 2359300
  191.1 3.5 %copy-start.7 = (f32[512]{0:T(512)S(1)}, f32[512]{0:T(512)}, u32[]{:S(2)}) copy-start(f32[512]{0:T(512)} %param.8) | copy-start | bytes 6148
  194.8 2.6 %copy-start.4 = (bf16[256,512]{0,1:T(8,128)(2,1)}, bf16[256,512]{0,1:T(8,128)(2,1)S(1)}, u32[]{:S(2)}) copy-start(bf16[256,512]{0,1:T(8,128)(2,1)S(1)} %fusion.16) | copy-start | bytes 786436
  194.8 9.0 %collective-permute-start.5 = (bf16[256,512]{0,1:T(8,128)(2,1)S(1)}, bf16[256,512]{0,1:T(8,128)(2,1)S(1)}, u32[]{:S(2)}, u32[]{:S(2)}) collective-permute-start(bf16[256,512]{0,1:T(8,128)(2,1)S(1)} %fusion.16), channel_id=1, source_target_pairs={{0,1},{1,0},{2,3},{3,2},{4,5},{5,4},{6,7},{7,6},{8,9},{9,8},{10,11... | collective-permute-start | bytes 786440 | tf_op jit(solution)/shard_map/ppermute | solution.py:127
  203.8 0.7 copy-start.5
  203.8 46.9 %copy-start.1 = (bf16[3,512,512]{2,1,0:T(8,128)(2,1)S(1)}, bf16[3,512,512]{2,1,0:T(8,128)(2,1)}, u32[]{:S(2)}) copy-start(bf16[3,512,512]{2,1,0:T(8,128)(2,1)} %param.6) | copy-start | bytes 4718596
Sparse Core Ops, SparseCore 0:
  18.1 59.5 all-gather.1
  99.1 84.2 reduce-scatter.2
  210.2 40.4 reduce-scatter.4
